TPU v7x, 512 devices: a whole 4x4x16 slice. The times are simulated.
512 devices in a mesh: ctx: 64 (over z, x_hi, core), head: 8 (over y, x_lo).
Axes of the slice: x: 4 (x_hi: 2, x_lo: 2; x = x_hi * 2 + x_lo), y: 4, z: 16, core: 2. Of those that a mesh axis runs over, the one named last changes fastest.
Arguments:
- tokens: bfloat16 [8192, 4096], P('ctx'), may hold values from -6 to 6
- norm_gain: float32 [4096], replicated, may hold values from 0.25 to 1.75
- w_query: bfloat16 [4096, 4096], P('ctx', 'head'), may hold values from -0.09375 to 0.09375
- w_key: bfloat16 [4096, 1024], P('ctx', 'head'), may hold values from -0.09375 to 0.09375
- w_value: bfloat16 [4096, 1024], P('ctx', 'head'), may hold values from -0.09375 to 0.09375
- w_out: bfloat16 [4096, 4096], P('head', 'ctx'), may hold values from -0.09375 to 0.09375
- row_map: int32 [8192], P('ctx'), may hold values from 0 to 8191, as said below
- doc_lengths: int32 [32], replicated, may hold values from 1 to 2048, 8192 in all
- doc_labels: int32 [32], replicated, may hold values from 0 to 1, as said below
Outputs:
- residual_out: bfloat16 [8192, 4096], P('ctx', 'head')
- refusal_direction: float32 [4096], P('head')
Inputs may be any that keep to these rules, and one draw needn't show every extreme that they name: `row_map`: the rows of ctx index c are two runs of 64 consecutive positions, run b(c) and run 2 * 64 - 1 - b(c) of the pack, b a permutation drawn from the seed; every position appears once. `doc_labels`: at least one prompt of each class.
All inputs are finite; a program needn't handle non-finite values.
Results may differ from a plain program's by a relative error of at most 0.008.
Values may be sent and summed in bfloat16 or wider, within the bound.
No kernel may reach another device: no remote copies, remote signals or barrier semaphores. Data moves between devices by JAX's collectives and lax.ppermute only.
A program may use at most 64 MiB of HBM per device.

v0:
```python
import math

import jax
import jax.numpy as jnp
from jax import lax
from jax.sharding import PartitionSpec as P

HEADS = 32
KV_HEADS = 8
HEAD_DIM = 128


ROPE_BASE = 500000.0
NEG_FILL = -1e30
BLOCK_KEYS = 512


def doc_layout(row_map, doc_lengths):
    doc_ends = jnp.cumsum(doc_lengths)
    doc_starts = doc_ends - doc_lengths
    doc_index = jnp.sum((row_map[:, None] >= doc_ends[None, :]).astype(jnp.int32), 1)
    member = doc_index[:, None] == jnp.arange(doc_ends.shape[0], dtype=jnp.int32)[None, :]
    in_doc = row_map - jnp.sum(jnp.where(member, doc_starts[None, :], 0), 1)
    return (doc_index, in_doc, doc_ends)


def rotate(values, in_doc):
    head_dim = values.shape[-1]
    half_dim = head_dim // 2
    inv_freq = jnp.exp(
        jnp.arange(half_dim).astype(jnp.float32) * (-2.0 * math.log(ROPE_BASE) / head_dim)
    )
    angles = in_doc.astype(jnp.float32)[:, None] * inv_freq[None, :]
    shape_out = (angles.shape[0],) + (1,) * (values.ndim - 2) + (half_dim,)
    cosine = jnp.cos(angles).reshape(shape_out)
    sine_val = jnp.sin(angles).reshape(shape_out)
    front_half = values[..., :half_dim]
    back_half = values[..., half_dim:]
    return jnp.concatenate(
        [front_half * cosine - back_half * sine_val, back_half * cosine + front_half * sine_val], -1
    )


def rms_norm(tokens, norm_gain):
    wide_tokens = tokens.astype(jnp.float32)
    row_scale = lax.rsqrt(jnp.mean(wide_tokens * wide_tokens, -1, keepdims=True) + 1e-05)
    return (wide_tokens * row_scale * norm_gain).astype(jnp.bfloat16)


def attend_keys(carried, key_block_set, queries, query_pos, query_doc, doc_ends):
    key_block, value_block, key_pos = key_block_set
    key_doc = jnp.sum((key_pos[:, None] >= doc_ends[None, :]).astype(jnp.int32), 1)
    allowed = (key_doc[None, :] == query_doc[:, None]) & (key_pos[None, :] <= query_pos[:, None])
    scale_factor = queries.shape[-1] ** (-0.5)
    running_max, running_sum, weighted = carried
    scores = (
        jnp.einsum("qgjd,kgd->gjqk", queries, key_block, preferred_element_type=jnp.float32)
        * scale_factor
    )
    scores = jnp.where(allowed[None, None], scores, NEG_FILL)
    new_max = jnp.maximum(running_max, jnp.max(scores, -1))
    weights = jnp.where(allowed[None, None], jnp.exp(scores - new_max[..., None]), 0.0)
    rescale = jnp.exp(running_max - new_max)
    new_sum = running_sum * rescale + jnp.sum(weights, -1)
    new_weighted = weighted * rescale[..., None] + jnp.einsum(
        "gjqk,kgd->gjqd",
        weights.astype(jnp.bfloat16),
        value_block,
        preferred_element_type=jnp.float32,
    )
    return (new_max, new_sum, new_weighted)


def make_fold(queries, query_pos, query_doc, doc_ends):

    def fold_keys(carried, pieces, offset):
        key_rows = pieces[0].shape[0]
        step_count = key_rows // BLOCK_KEYS
        stacked = tuple(
            (member.reshape((step_count, BLOCK_KEYS) + member.shape[1:]) for member in pieces)
        )

        def scan_step(softmax_state, key_block_set):
            return (
                attend_keys(softmax_state, key_block_set, queries, query_pos, query_doc, doc_ends),
                None,
            )

        final_state, unused = lax.scan(scan_step, carried, stacked)
        return final_state

    return fold_keys


def local(tokens, norm_gain, w_query, w_key, w_value, w_out, row_map, doc_lengths, doc_labels):
    tok_rows = tokens.shape[0]
    kv_local = w_key.shape[1] // HEAD_DIM
    group_size = HEADS // KV_HEADS
    normed = rms_norm(tokens, norm_gain)
    weight_pieces = (
        lax.all_gather(w_query, "ctx", axis=0, tiled=True),
        lax.all_gather(w_key, "ctx", axis=0, tiled=True),
        lax.all_gather(w_value, "ctx", axis=0, tiled=True),
    )
    queries, key_proj, value_proj = tuple(
        (
            jnp.dot(normed, weight_piece, preferred_element_type=jnp.float32)
            for weight_piece in weight_pieces
        )
    )
    doc_index, in_doc, doc_ends = doc_layout(row_map, doc_lengths)
    queries = rotate(queries.reshape(tok_rows, kv_local, group_size, HEAD_DIM), in_doc).astype(
        jnp.bfloat16
    )
    key_proj = rotate(key_proj.reshape(tok_rows, kv_local, HEAD_DIM), in_doc).astype(jnp.bfloat16)
    value_proj = value_proj.reshape(tok_rows, kv_local, HEAD_DIM).astype(jnp.bfloat16)
    initial = (
        jnp.full((kv_local, group_size, tok_rows), NEG_FILL, jnp.float32),
        jnp.zeros((kv_local, group_size, tok_rows), jnp.float32),
        jnp.zeros((kv_local, group_size, tok_rows, HEAD_DIM), jnp.float32),
    )
    fold_keys = make_fold(queries, row_map, doc_index, doc_ends)
    softmax_state = fold_keys(
        initial,
        (
            lax.all_gather(key_proj, "ctx", axis=0, tiled=True),
            lax.all_gather(value_proj, "ctx", axis=0, tiled=True),
            lax.all_gather(row_map, "ctx", axis=0, tiled=True),
        ),
        jnp.int32(0),
    )
    running_max, running_sum, weighted = softmax_state
    attended = weighted / running_sum[..., None]
    attended = (
        jnp.transpose(attended, (2, 0, 1, 3))
        .reshape(tok_rows, kv_local * group_size * HEAD_DIM)
        .astype(jnp.bfloat16)
    )
    partial_out = jnp.dot(
        attended,
        lax.all_gather(w_out, "ctx", axis=1, tiled=True),
        preferred_element_type=jnp.float32,
    )
    head_share = lax.psum_scatter(
        partial_out.astype(jnp.bfloat16), "head", scatter_dimension=1, tiled=True
    ).astype(jnp.float32)
    col_width = head_share.shape[1]
    own_cols = lax.dynamic_slice_in_dim(tokens, lax.axis_index("head") * col_width, col_width, 1)
    residual_out = (own_cols.astype(jnp.float32) + head_share).astype(jnp.bfloat16)
    is_last = row_map[:, None] == (doc_ends - 1)[None, :]
    label_f = doc_labels.astype(jnp.float32)
    harmful = jnp.sum(label_f)
    harmless = doc_labels.shape[0] - jnp.sum(label_f)
    stream = residual_out.astype(jnp.float32)
    harm_rows = jnp.sum(jnp.where(is_last, label_f[None, :], 0.0), 1)
    safe_rows = jnp.sum(jnp.where(is_last, (1.0 - label_f)[None, :], 0.0), 1)
    harm_sum, safe_sum = lax.psum(
        (jnp.sum(harm_rows[:, None] * stream, 0), jnp.sum(safe_rows[:, None] * stream, 0)), "ctx"
    )
    refusal_direction = harm_sum / harmful - safe_sum / harmless
    return (residual_out, refusal_direction)


def solution(mesh):
    placed = (
        P("ctx", None),
        P(),
        P("ctx", "head"),
        P("ctx", "head"),
        P("ctx", "head"),
        P("head", "ctx"),
        P("ctx"),
        P(),
        P(),
    )
    return jax.shard_map(
        local, mesh=mesh, in_specs=placed, out_specs=(P("ctx", "head"), P("head")), check_vma=False
    )
```

profile of v0, /device:TPU:6, one launch (start us, length us, event | category | flops | bytes accessed | tf_op | source)
XLA Modules:
  0.0 1049.3 jit_solution(1660407853010582978)
XLA Ops:
  11.1 1.5 fusion.19
  13.3 140.6 %all-gather.9.cloned.1.call-done = bf16[4096,128]{1,0:T(8,128)(2,1)} async-done(((bf16[64,128]{1,0:T(8,128)(2,1)}), bf16[4096,128]{1,0:T(8,128)(2,1)}) %all-gather.9.cloned.1.call-update) | async-done | bytes 1048592 | tf_op jit(solution)/shard_map/all_gather | solution.py:102
  153.9 2.2 convolution_bitcast_fusion.1
  157.6 135.0 %all-gather.15.cloned.1.call-done = bf16[4096,128]{1,0:T(8,128)(2,1)} async-done(((bf16[64,128]{1,0:T(8,128)(2,1)}), bf16[4096,128]{1,0:T(8,128)(2,1)}) %all-gather.15.cloned.1.call-update) | async-done | bytes 1048592 | tf_op jit(solution)/shard_map/all_gather | solution.py:103
  292.5 2.3 convolution_convert_fusion.1
  295.8 73.0 %all-gather.1 = s32[64,1,128]{2,1,0:T(1,128)S(1)} all-gather(s32[1,1,128]{2,1,0:T(1,128)S(1)} %bitcast.82), channel_id=1, replica_groups=mesh['ctx'=64,'head'=8] {'ctx'}, dimensions={0}, use_global_device_ids=true | all-gather | bytes 33280 | tf_op jit(solution)/shard_map/all_gather | solution.py:128
  370.1 58.9 %all-gather.11.cloned.1.call-done = bf16[8192,1,128]{0,2,1:T(8,128)(2,1)} async-done(((bf16[128,1,128]{0,2,1:T(8,128)(2,1)}), bf16[8192,1,128]{0,2,1:T(8,128)(2,1)}) %all-gather.11.cloned.1.call-update) | async-done | bytes 2097168 | tf_op jit(solution)/shard_map/all_gather | solution.py:126
  429.0 4.1 copy.39
  433.1 144.2 %all-gather.13.cloned.1.call-done = bf16[4096,512]{1,0:T(8,128)(2,1)} async-done(((bf16[64,512]{1,0:T(8,128)(2,1)}), bf16[4096,512]{1,0:T(8,128)(2,1)}) %all-gather.13.cloned.1.call-update) | async-done | bytes 4194320 | tf_op jit(solution)/shard_map/all_gather | solution.py:101
  577.3 2.9 fusion.35
  580.7 138.0 %all-gather.19.cloned.1.call-done = bf16[8192,128]{1,0:T(8,128)(2,1)} async-done(((bf16[128,128]{1,0:T(8,128)(2,1)}), bf16[8192,128]{1,0:T(8,128)(2,1)}) %all-gather.19.cloned.1.call-update) | async-done | bytes 2097168 | tf_op jit(solution)/shard_map/all_gather | solution.py:127
  718.7 50.8 %while.15 = (s32[]{:T(128)}, f32[1,4,128]{2,1,0:T(4,128)S(1)}, f32[1,4,128]{2,1,0:T(4,128)S(1)}, f32[1,4,128,128]{3,2,1,0:T(8,128)S(1)}, s32[16,512]{1,0:T(8,128...) while((s32[]{:T(128)}, f32[1,4,128]{2,1,0:T(4,128)S(1)}, ...), condition=%wide.region_8.9_spmd.clone, body=%wide.region_4.8_spmd.clone.sunk | while | flops 137021952 | bytes 4372749 | solution.py:89
  723.5 1.4 fusion.57
  726.6 1.4 fusion.57
  729.8 1.4 fusion.57
  733.0 1.4 fusion.57
  736.2 1.4 fusion.57
  739.3 1.4 fusion.57
  758.4 1.4 fusion.57
  769.7 97.7 %all-gather.17.cloned.1.call-done = bf16[512,4096]{0,1:T(8,128)(2,1)} async-done(((bf16[512,64]{0,1:T(8,128)(2,1)}), bf16[512,4096]{0,1:T(8,128)(2,1)}) %all-gather.17.cloned.1.call-update) | async-done | bytes 4194320 | tf_op jit(solution)/shard_map/all_gather | solution.py:141
  867.4 4.7 convolution_convert_fusion
  873.3 40.9 %reduce-scatter.2.cloned.1.call-done = bf16[128,512]{1,0:T(8,128)(2,1)} async-done(((bf16[128,4096]{1,0:T(8,128)(2,1)}), bf16[128,512]{1,0:T(8,128)(2,1)}) %reduce-scatter.2.cloned.1.call-update) | async-done | bytes 131088 | tf_op jit(solution)/shard_map/reduce_scatter | solution.py:144
  914.2 1.6 fusion.22
  915.8 125.5 %all-reduce = (f32[512]{0:T(512)S(1)}, f32[512]{0:T(512)S(1)}) all-reduce(f32[512]{0:T(512)S(1)} %get-tuple-element.143, f32[512]{0:T(512)S(1)} %get-tuple-element.142), channel_id=1, replica_groups=mesh['ctx'=64,'head'=8] {'ctx'}, use_global_device_ids=true, to_apply=%region_16.17 | all-reduce | flops 1024 | bytes 8192 | tf_op jit(solution)/shard_map/psum | solution.py:157
  (187 shorter events, 51.0 us)
Async XLA Ops:
  7.2 285.3 %copy-start = (bf16[128,4096]{1,0:T(8,128)(2,1)S(1)}, bf16[128,4096]{1,0:T(8,128)(2,1)}, u32[]{:S(2)}) copy-start(bf16[128,4096]{1,0:T(8,128)(2,1)} %param.11) | copy-start | bytes 3145732
  7.2 285.3 %copy-start.2 = (f32[4096]{0:T(1024)S(1)}, f32[4096]{0:T(1024)}, u32[]{:S(2)}) copy-start(f32[4096]{0:T(1024)} %param.12) | copy-start | bytes 49156
  7.2 146.7 %all-gather.9.cloned.1.call-start = ((), (), s32[]{:S(2)}) async-start(), calls=%async_computation.1 | async-start | bytes 1064960 | tf_op jit(solution)/shard_map/all_gather | solution.py:102
  7.9 284.6 %all-gather.15.cloned.1.call-start = ((), (), s32[]{:S(2)}) async-start(), calls=%async_computation.4 | async-start | bytes 1064960 | tf_op jit(solution)/shard_map/all_gather | solution.py:103
  8.7 420.4 %all-gather.11.cloned.1.call-start = ((), (), s32[]{:S(2)}) async-start(), calls=%async_computation.2 | async-start | bytes 2129920 | tf_op jit(solution)/shard_map/all_gather | solution.py:126
  156.1 139.8 %copy-start.1 = (s32[128]{0:T(128)S(1)}, s32[128]{0:T(128)}, u32[]{:S(2)}) copy-start(s32[128]{0:T(128)} %param.17) | copy-start | bytes 1540
  156.9 420.4 %all-gather.13.cloned.1.call-start = ((), (), s32[]{:S(2)}) async-start(), calls=%async_computation.3 | async-start | bytes 4259840 | tf_op jit(solution)/shard_map/all_gather | solution.py:101
  157.5 561.2 %all-gather.19.cloned.1.call-start = ((), (), s32[]{:S(2)}) async-start(), calls=%async_computation.7 | async-start | bytes 2129920 | tf_op jit(solution)/shard_map/all_gather | solution.py:127
  294.9 572.5 %all-gather.17.cloned.1.call-start = ((), (), s32[]{:S(2)}) async-start(), calls=%async_computation.5 | async-start | bytes 4259840 | tf_op jit(solution)/shard_map/all_gather | solution.py:141
  295.4 618.8 %reduce-scatter.2.cloned.1.call-start = ((), (), s32[]{:S(2)}) async-start(), calls=%async_computation.6 | async-start | bytes 1179648 | tf_op jit(solution)/shard_map/reduce_scatter | solution.py:144
  867.4 4.7 copy-start.3
Sparse Core Ops, SparseCore 0:
  11.3 142.5 all-gather.8
  157.2 135.2 all-gather.14
  296.1 132.9 all-gather.10
  432.2 145.0 all-gather.12
  580.4 138.2 all-gather.18
  721.9 145.4 all-gather.16
  872.2 42.0 reduce-scatter.1
where the time goes:
time: 1060 us; the launch traced here: 1050 us
  waiting for transfers between devices  758 us (72%)
  blocking collectives  198 us (19%)
  matrix products  53.2 us (5%)
  other arithmetic  17.8 us (2%)
  between operations  14.9 us (1%)
    all_gather x1, waiting for transfers between devices, local(): lax.all_gather(w_query, 'ctx', axis=0, tiled=True)  144 us
    all_gather x1, waiting for transfers between devices, local(): lax.all_gather(w_key, 'ctx', axis=0, tiled=True)  141 us
    all_gather x1, waiting for transfers between devices, local(): lax.all_gather(value_proj, 'ctx', axis=0, tiled=True)  138 us
    all_gather x1, waiting for transfers between devices, local(): lax.all_gather(w_value, 'ctx', axis=0, tiled=True)  135 us
    psum x1, blocking collectives, local(): lax.psum((jnp.sum(harm_rows[:, None] * stream, 0), jnp.sum(safe_rows[:, N...  125 us
    all_gather x1, waiting for transfers between devices, local(): lax.all_gather(w_out, 'ctx', axis=1, tiled=True)  97.7 us
    all_gather x1, blocking collectives, local(): lax.all_gather(row_map, 'ctx', axis=0, tiled=True)  73 us
    all_gather x1, waiting for transfers between devices, local(): lax.all_gather(key_proj, 'ctx', axis=0, tiled=True)  58.9 us
  transfers between devices with their start and end apart: 7, of which 7 were waited for; matrix products, arithmetic and copies ran while one was open for 7% of the time, Pallas kernels for 0%

commit v1 on v0

v1 whole, which is shorter than its diff:
```python
import math

import jax
import jax.numpy as jnp
from jax import lax
from jax.sharding import Mesh
from jax.sharding import PartitionSpec as P

HEADS = 32
KV_HEADS = 8
HEAD_DIM = 128
MOST = 2048
RUN = 64

ROPE_BASE = 500000.0
NEG_FILL = -1e30

CTX = ("z", "xh", "c")
HEAD = ("y", "xl")
GATHER_ORDER = ("z", "xh", "c")


def doc_layout(row_map, doc_lengths):
    doc_ends = jnp.cumsum(doc_lengths)
    doc_starts = doc_ends - doc_lengths
    doc_index = jnp.sum((row_map[:, None] >= doc_ends[None, :]).astype(jnp.int32), 1)
    member = doc_index[:, None] == jnp.arange(doc_ends.shape[0], dtype=jnp.int32)[None, :]
    in_doc = row_map - jnp.sum(jnp.where(member, doc_starts[None, :], 0), 1)
    return (doc_index, in_doc, doc_ends)


def rotate(values, in_doc):
    head_dim = values.shape[-1]
    half_dim = head_dim // 2
    inv_freq = jnp.exp(
        jnp.arange(half_dim).astype(jnp.float32) * (-2.0 * math.log(ROPE_BASE) / head_dim)
    )
    angles = in_doc.astype(jnp.float32)[:, None] * inv_freq[None, :]
    shape_out = (angles.shape[0],) + (1,) * (values.ndim - 2) + (half_dim,)
    cosine = jnp.cos(angles).reshape(shape_out)
    sine_val = jnp.sin(angles).reshape(shape_out)
    front_half = values[..., :half_dim]
    back_half = values[..., half_dim:]
    return jnp.concatenate(
        [front_half * cosine - back_half * sine_val, back_half * cosine + front_half * sine_val], -1
    )


def rms_norm(tokens, norm_gain):
    wide_tokens = tokens.astype(jnp.float32)
    row_scale = lax.rsqrt(jnp.mean(wide_tokens * wide_tokens, -1, keepdims=True) + 1e-05)
    return (wide_tokens * row_scale * norm_gain).astype(jnp.bfloat16)


def gather_ctx(x):
    for axis in GATHER_ORDER:
        x = lax.all_gather(x, axis, axis=0, tiled=True)
    return x


def to_gathered_order(x, sizes):
    nz, nxh, nc = sizes
    lead = x.shape[:-2]
    y = x.reshape(lead + (nz, nxh, nc, x.shape[-1]))
    n = len(lead)
    y = jnp.transpose(y, tuple(range(n)) + (n + 2, n + 1, n, n + 3))
    return y.reshape(x.shape)


def from_gathered_order(x, sizes):
    nz, nxh, nc = sizes
    lead = x.shape[:-2]
    y = x.reshape(lead + (nc, nxh, nz, x.shape[-1]))
    n = len(lead)
    y = jnp.transpose(y, tuple(range(n)) + (n + 2, n + 1, n, n + 3))
    return y.reshape(x.shape)


def make_local(sizes):
    nz, nxh, nc = sizes
    nctx = nz * nxh * nc

    def local(tokens, norm_gain, w_query, w_key, w_value, w_out, row_map, doc_lengths, doc_labels):
        tok_rows, width = tokens.shape
        d_rows = w_query.shape[0]
        q_cols = w_query.shape[1]
        kv_cols = w_key.shape[1]
        group_size = q_cols // kv_cols
        runs_here = tok_rows // RUN
        total_runs = runs_here * nctx
        win_runs = MOST // RUN + 1

        normed = rms_norm(tokens, norm_gain)
        doc_index, in_doc, doc_ends = doc_layout(row_map, doc_lengths)

        w_cols = q_cols + 2 * kv_cols + w_out.shape[0]
        pos_row = jnp.concatenate(
            [
                (row_map // RUN).astype(jnp.bfloat16),
                (row_map % RUN).astype(jnp.bfloat16),
                jnp.zeros((w_cols - 2 * tok_rows,), jnp.bfloat16),
            ]
        )[None, :]
        pad_rows = 8 - (d_rows + 1) % 8 if (d_rows + 1) % 8 else 0
        buf = jnp.concatenate(
            [
                jnp.concatenate([w_query, w_key, w_value, w_out.T], axis=1),
                pos_row,
                jnp.zeros((pad_rows, w_cols), jnp.bfloat16),
            ],
            axis=0,
        )
        blk_rows = buf.shape[0]
        gathered = gather_ctx(buf).reshape(nctx, blk_rows, w_cols)
        w_blocks = gathered[:, :d_rows, :]
        pos_code = gathered[:, d_rows, : 2 * tok_rows].astype(jnp.int32)
        key_pos_all = pos_code[:, :tok_rows] * RUN + pos_code[:, tok_rows:]

        normed_g = to_gathered_order(normed.reshape(tok_rows, nctx, d_rows), sizes)
        proj = jnp.einsum(
            "tjd,jdn->tn", normed_g, w_blocks[:, :, : q_cols + 2 * kv_cols],
            preferred_element_type=jnp.float32,
        )
        queries = proj[:, :q_cols].reshape(tok_rows, group_size, HEAD_DIM)
        key_proj = proj[:, q_cols : q_cols + kv_cols]
        value_proj = proj[:, q_cols + kv_cols :].astype(jnp.bfloat16)
        queries = rotate(queries, in_doc).astype(jnp.bfloat16)
        key_proj = rotate(key_proj, in_doc).astype(jnp.bfloat16)

        kv = gather_ctx(jnp.concatenate([key_proj, value_proj], axis=1))
        kv_halves = kv.reshape(total_runs, RUN, 2 * kv_cols)
        pos_halves = key_pos_all.reshape(total_runs, RUN)
        run_of_half = pos_halves[:, 0] // RUN
        half_of_run = jnp.zeros((total_runs,), jnp.int32).at[run_of_half].set(
            jnp.arange(total_runs, dtype=jnp.int32)
        )

        q_pos = row_map.reshape(runs_here, RUN)
        q_start = (row_map - in_doc).reshape(runs_here, RUN)
        q_run = q_pos[:, 0] // RUN
        first_run = jnp.maximum(q_run - (win_runs - 1), 0)
        win = first_run[:, None] + jnp.arange(win_runs, dtype=jnp.int32)[None, :]
        win_halves = half_of_run[win]
        kv_win = kv_halves[win_halves].reshape(runs_here, win_runs * RUN, 2 * kv_cols)
        k_pos = pos_halves[win_halves].reshape(runs_here, win_runs * RUN)
        k_win = kv_win[..., :kv_cols]
        v_win = kv_win[..., kv_cols:]

        q_runs = queries.reshape(runs_here, RUN, group_size, HEAD_DIM)
        scale_factor = HEAD_DIM ** (-0.5)
        scores = (
            jnp.einsum("rqgd,rkd->rgqk", q_runs, k_win, preferred_element_type=jnp.float32)
            * scale_factor
        )
        allowed = (k_pos[:, None, :] >= q_start[:, :, None]) & (k_pos[:, None, :] <= q_pos[:, :, None])
        allowed = allowed[:, None]
        scores = jnp.where(allowed, scores, NEG_FILL)
        row_top = jnp.max(scores, -1, keepdims=True)
        weights = jnp.where(allowed, jnp.exp(scores - row_top), 0.0)
        row_sum = jnp.sum(weights, -1, keepdims=True)
        mixed = (
            jnp.einsum(
                "rgqk,rkd->rgqd", weights.astype(jnp.bfloat16), v_win,
                preferred_element_type=jnp.float32,
            )
            / row_sum
        ).astype(jnp.bfloat16)
        attended = jnp.transpose(mixed, (0, 2, 1, 3)).reshape(tok_rows, q_cols)

        partial_g = jnp.einsum(
            "tk,jdk->tjd", attended, w_blocks[:, :, q_cols + 2 * kv_cols :],
            preferred_element_type=jnp.float32,
        )
        partial_out = from_gathered_order(partial_g, sizes).reshape(tok_rows, width)
        head_share = lax.psum_scatter(
            partial_out.astype(jnp.bfloat16), HEAD, scatter_dimension=1, tiled=True
        ).astype(jnp.float32)
        col_width = head_share.shape[1]
        head_idx = lax.axis_index("y") * lax.axis_size("xl") + lax.axis_index("xl")
        own_cols = lax.dynamic_slice_in_dim(tokens, head_idx * col_width, col_width, 1)
        residual_out = (own_cols.astype(jnp.float32) + head_share).astype(jnp.bfloat16)

        is_last = row_map[:, None] == (doc_ends - 1)[None, :]
        label_f = doc_labels.astype(jnp.float32)
        harmful = jnp.sum(label_f)
        harmless = doc_labels.shape[0] - jnp.sum(label_f)
        stream = residual_out.astype(jnp.float32)
        harm_rows = jnp.sum(jnp.where(is_last, label_f[None, :], 0.0), 1)
        safe_rows = jnp.sum(jnp.where(is_last, (1.0 - label_f)[None, :], 0.0), 1)
        sums = jnp.stack(
            [jnp.sum(harm_rows[:, None] * stream, 0), jnp.sum(safe_rows[:, None] * stream, 0)]
        )
        for axis in ("c", "xh", "z"):
            sums = lax.psum(sums, axis)
        refusal_direction = sums[0] / harmful - sums[1] / harmless
        return (residual_out, refusal_direction)

    return local


def solution(mesh):
    n_ctx = mesh.shape["ctx"]
    n_head = mesh.shape["head"]
    nc, nxh = 2, 2
    nz = n_ctx // (nc * nxh)
    ny, nxl = n_head // 2, 2
    fine = Mesh(mesh.devices.reshape(nz, nxh, nc, ny, nxl), ("z", "xh", "c", "y", "xl"))
    placed = (
        P(CTX, None),
        P(),
        P(CTX, HEAD),
        P(CTX, HEAD),
        P(CTX, HEAD),
        P(HEAD, CTX),
        P(CTX),
        P(),
        P(),
    )
    return jax.shard_map(
        make_local((nz, nxh, nc)),
        mesh=fine,
        in_specs=placed,
        out_specs=(P(CTX, HEAD), P(HEAD)),
        check_vma=False,
    )
```

time: 1060 us -> 478 us (0.45)
  waiting for transfers between devices: 758 us -> 376 us
  blocking collectives: 198 us -> 40.2 us
  matrix products: 53.2 us -> 14.2 us
  local copies, waits for them, and re-layouts: 5.99 us -> 18.1 us
    all_gather x6, waiting for transfers between devices: 714 us -> 330 us  [gather_ctx(): x = lax.all_gather(x, axis, axis=0, tiled=True)]
    psum x1 -> x3, blocking collectives: 125 us -> 40.2 us  [local(): sums = lax.psum(sums, axis)]
    all_gather x1 -> x0, blocking collectives: 73 us -> none  [local(): lax.all_gather(row_map, 'ctx', axis=0, tiled=True)]
    dot_general x36 -> x3, matrix products: 53.2 us -> 9.65 us  [the longest x1 3.86 us: local(): jnp.einsum('tjd,jdn->tn', normed_g, w_blocks[:, :, :q_cols + 2 * kv_cols]...]
  transfers between devices with their start and end apart: 7 -> 7, of which waited for: 7 -> 7; matrix products, arithmetic and copies ran while one was open for 7% -> 3% of each run, Pallas kernels for 0% -> 0%
where the time goes in v1:
time: 478 us; the launch traced here: 475 us
  waiting for transfers between devices  376 us (79%)
  blocking collectives  40.2 us (8%)
  local copies, waits for them, and re-layouts  18.1 us (4%)
  between operations  15 us (3%)
  matrix products  14.2 us (3%)
  other arithmetic  11 us (2%)
    all_gather x6, waiting for transfers between devices, gather_ctx(): x = lax.all_gather(x, axis, axis=0, tiled=True)  330 us
    reduce_scatter x1, waiting for transfers between devices, local(): lax.psum_scatter(partial_out.astype(jnp.bfloat16), HEAD, scatter_dimensio...  46.1 us
    psum x3, blocking collectives, local(): sums = lax.psum(sums, axis)  40.2 us
  transfers between devices with their start and end apart: 7, of which 7 were waited for; matrix products, arithmetic and copies ran while one was open for 3% of the time, Pallas kernels for 0%

profile of v1, /device:TPU:6, one launch (start us, length us, event | category | flops | bytes accessed | tf_op | source)
XLA Modules:
  0.0 474.7 jit_solution(11571126874237185977)
XLA Ops:
  10.4 1.7 maximum_maximum_fusion
  12.2 80.4 %all-gather.7.cloned.1.call-done = bf16[1152,1280]{1,0:T(8,128)(2,1)} async-done(((bf16[72,1280]{1,0:T(8,128)(2,1)}), bf16[1152,1280]{1,0:T(8,128)(2,1)}) %all-gather.7.cloned.1.call-update) | async-done | bytes 2949136 | tf_op jit(solution)/shard_map/all_gather | solution.py:57
  92.6 85.0 %all-gather.9.cloned.1.call-done = bf16[2304,1280]{1,0:T(8,128)(2,1)} async-done(((bf16[1152,1280]{1,0:T(8,128)(2,1)}), bf16[2304,1280]{1,0:T(8,128)(2,1)}) %all-gather.9.cloned.1.call-update) | async-done | bytes 5898256 | tf_op jit(solution)/shard_map/all_gather | solution.py:57
  177.7 1.1 copy-done
  180.9 34.5 %all-gather.11.cloned.1.call-done = bf16[4608,1280]{1,0:T(8,128)(2,1)} async-done(((bf16[2304,1280]{1,0:T(8,128)(2,1)}), bf16[4608,1280]{1,0:T(8,128)(2,1)}) %all-gather.11.cloned.1.call-update) | async-done | bytes 11796496 | tf_op jit(solution)/shard_map/all_gather | solution.py:57
  215.4 3.9 fusion.14
  220.8 72.5 %all-gather.13.cloned.1.call-done = bf16[2048,256]{1,0:T(8,128)(2,1)} async-done(((bf16[128,256]{1,0:T(8,128)(2,1)}), bf16[2048,256]{1,0:T(8,128)(2,1)}) %all-gather.13.cloned.1.call-update) | async-done | bytes 1048592 | tf_op jit(solution)/shard_map/all_gather | solution.py:57
  293.4 42.1 %all-gather.15.cloned.1.call-done = bf16[4096,256]{1,0:T(8,128)(2,1)} async-done(((bf16[2048,256]{1,0:T(8,128)(2,1)}), bf16[4096,256]{1,0:T(8,128)(2,1)}) %all-gather.15.cloned.1.call-update) | async-done | bytes 2097168 | tf_op jit(solution)/shard_map/all_gather | solution.py:57
  336.0 4.8 %slice.94 = bf16[64,64,512]{2,1,0:T(8,128)(2,1)} slice(bf16[64,72,1280]{2,1,0:T(8,128)(2,1)} %bitcast.76), slice={[0:64], [0:64], [768:1280]} | slice | bytes 8388608 | tf_op jit(solution)/shard_map/slice | solution.py:171
  340.8 1.0 slice_convert_fusion.1
  342.0 1.0 scatter_custom_fusion
  343.0 1.2 gather_fusion
  347.3 15.3 %all-gather.17.cloned.1.call-done = bf16[8192,256]{1,0:T(8,128)(2,1)} async-done(((bf16[4096,256]{1,0:T(8,128)(2,1)}), bf16[8192,256]{1,0:T(8,128)(2,1)}) %all-gather.17.cloned.1.call-update) | async-done | bytes 4194320 | tf_op jit(solution)/shard_map/all_gather | solution.py:57
  362.6 2.9 gather_fusion.2
  365.5 4.5 fusion.46
  370.0 2.4 fusion.23
  372.6 3.4 fusion.13
  376.0 1.1 copy.68
  378.5 46.1 %reduce-scatter.2.cloned.1.call-done = bf16[128,512]{0,1:T(8,128)(2,1)} async-done(((bf16[128,4096]{0,1:T(8,128)(2,1)}), bf16[128,512]{0,1:T(8,128)(2,1)}) %reduce-scatter.2.cloned.1.call-update) | async-done | bytes 131088 | tf_op jit(solution)/shard_map/reduce_scatter | solution.py:175
  424.6 1.1 fusion.26
  425.8 2.5 psum.21
  428.2 6.4 %psum.22 = f32[2,512]{1,0:T(2,128)S(1)} all-reduce(f32[2,512]{1,0:T(2,128)S(1)} %psum.21), channel_id=1, replica_groups=mesh['z'=16,'xh'=2,'c'=2,'y'=4,'xl'=2] {'xh'}, use_global_device_ids=true, to_apply=%region_13.14 | all-reduce | flops 1024 | bytes 8192 | tf_op jit(solution)/shard_map/psum | solution.py:194
  434.7 31.3 %psum.23 = f32[2,512]{1,0:T(2,128)S(1)} all-reduce(f32[2,512]{1,0:T(2,128)S(1)} %psum.22), channel_id=1, replica_groups=mesh['z'=16,'xh'=2,'c'=2,'y'=4,'xl'=2] {'z'}, use_global_device_ids=true, to_apply=%region_14.15 | all-reduce | flops 1024 | bytes 8192 | tf_op jit(solution)/shard_map/psum | solution.py:194
  466.7 1.2 divide_subtract_fusion
  (79 shorter events, 12.5 us)
Async XLA Ops:
  7.2 85.4 %all-gather.7.cloned.1.call-start = ((), (), s32[]{:S(2)}) async-start(), calls=%async_computation.1 | async-start | bytes 3133440 | tf_op jit(solution)/shard_map/all_gather | solution.py:57
  12.1 165.5 %all-gather.9.cloned.1.call-start = ((), (), s32[]{:S(2)}) async-start(), calls=%async_computation.2 | async-start | bytes 8847360 | tf_op jit(solution)/shard_map/all_gather | solution.py:57
  92.6 122.8 %all-gather.11.cloned.1.call-start = ((), (), s32[]{:S(2)}) async-start(), calls=%async_computation.3 | async-start | bytes 17694720 | tf_op jit(solution)/shard_map/all_gather | solution.py:57
  177.6 1.2 copy-start
  177.6 2.4 copy-start.1
  177.7 115.6 %all-gather.13.cloned.1.call-start = ((), (), s32[]{:S(2)}) async-start(), calls=%async_computation.4 | async-start | bytes 1114112 | tf_op jit(solution)/shard_map/all_gather | solution.py:57
  219.3 116.2 %copy-start.2 = (s32[128]{0:T(128)S(1)}, s32[128]{0:T(128)}, u32[]{:S(2)}) copy-start(s32[128]{0:T(128)} %param.15) | copy-start | bytes 1540
  220.8 114.7 %all-gather.15.cloned.1.call-start = ((), (), s32[]{:S(2)}) async-start(), calls=%async_computation.5 | async-start | bytes 3145728 | tf_op jit(solution)/shard_map/all_gather | solution.py:57
  293.3 69.3 %all-gather.17.cloned.1.call-start = ((), (), s32[]{:S(2)}) async-start(), calls=%async_computation.6 | async-start | bytes 6291456 | tf_op jit(solution)/shard_map/all_gather | solution.py:57
  335.5 89.2 %reduce-scatter.2.cloned.1.call-start = ((), (), s32[]{:S(2)}) async-start(), calls=%async_computation.7 | async-start | bytes 1179648 | tf_op jit(solution)/shard_map/reduce_scatter | solution.py:175
  376.0 1.1 copy-start.3
Sparse Core Ops, SparseCore 0:
  12.2 80.3 all-gather.6
  94.7 82.9 all-gather.8
  179.7 35.6 all-gather.10
  220.9 72.3 all-gather.12
  295.2 40.1 all-gather.14
  337.4 25.1 all-gather.16
  377.2 47.3 reduce-scatter.1

commit v2 on v1

--- a/solution.py
+++ b/solution.py
@@ -17,7 +17,6 @@
 
 CTX = ("z", "xh", "c")
 HEAD = ("y", "xl")
-GATHER_ORDER = ("z", "xh", "c")
 
 
 def doc_layout(row_map, doc_lengths):
@@ -52,28 +51,37 @@
     return (wide_tokens * row_scale * norm_gain).astype(jnp.bfloat16)
 
 
+def swap_cat(x, axis_name):
+    return jnp.concatenate([x, lax.ppermute(x, axis_name, [(0, 1), (1, 0)])], 0)
+
+
 def gather_ctx(x):
-    for axis in GATHER_ORDER:
-        x = lax.all_gather(x, axis, axis=0, tiled=True)
-    return x
+    x = lax.all_gather(x, "z", axis=0, tiled=True)
+    x = swap_cat(x, "xh")
+    return swap_cat(x, "c")
+
+
+def relative_index():
+    return (
+        lax.axis_index("c") ^ jnp.arange(2, dtype=jnp.int32),
+        lax.axis_index("xh") ^ jnp.arange(2, dtype=jnp.int32),
+    )
 
 
 def to_gathered_order(x, sizes):
     nz, nxh, nc = sizes
-    lead = x.shape[:-2]
-    y = x.reshape(lead + (nz, nxh, nc, x.shape[-1]))
-    n = len(lead)
-    y = jnp.transpose(y, tuple(range(n)) + (n + 2, n + 1, n, n + 3))
+    c_idx, xh_idx = relative_index()
+    y = jnp.transpose(x.reshape(x.shape[0], nz, nxh, nc, x.shape[-1]), (0, 3, 2, 1, 4))
+    y = jnp.take(jnp.take(y, c_idx, axis=1), xh_idx, axis=2)
     return y.reshape(x.shape)
 
 
 def from_gathered_order(x, sizes):
     nz, nxh, nc = sizes
-    lead = x.shape[:-2]
-    y = x.reshape(lead + (nc, nxh, nz, x.shape[-1]))
-    n = len(lead)
-    y = jnp.transpose(y, tuple(range(n)) + (n + 2, n + 1, n, n + 3))
-    return y.reshape(x.shape)
+    c_idx, xh_idx = relative_index()
+    y = x.reshape(x.shape[0], nc, nxh, nz, x.shape[-1])
+    y = jnp.take(jnp.take(y, c_idx, axis=1), xh_idx, axis=2)
+    return jnp.transpose(y, (0, 3, 2, 1, 4)).reshape(x.shape)
 
 
 def make_local(sizes):
@@ -93,33 +101,33 @@
         normed = rms_norm(tokens, norm_gain)
         doc_index, in_doc, doc_ends = doc_layout(row_map, doc_lengths)
 
-        w_cols = q_cols + 2 * kv_cols + w_out.shape[0]
+        qkv_cols = q_cols + 2 * kv_cols
         pos_row = jnp.concatenate(
             [
                 (row_map // RUN).astype(jnp.bfloat16),
                 (row_map % RUN).astype(jnp.bfloat16),
-                jnp.zeros((w_cols - 2 * tok_rows,), jnp.bfloat16),
+                jnp.zeros((qkv_cols - 2 * tok_rows,), jnp.bfloat16),
             ]
         )[None, :]
-        pad_rows = 8 - (d_rows + 1) % 8 if (d_rows + 1) % 8 else 0
+        pad_rows = -(d_rows + 1) % 8
         buf = jnp.concatenate(
             [
-                jnp.concatenate([w_query, w_key, w_value, w_out.T], axis=1),
+                jnp.concatenate([w_query, w_key, w_value], axis=1),
                 pos_row,
-                jnp.zeros((pad_rows, w_cols), jnp.bfloat16),
+                jnp.zeros((pad_rows, qkv_cols), jnp.bfloat16),
             ],
             axis=0,
         )
         blk_rows = buf.shape[0]
-        gathered = gather_ctx(buf).reshape(nctx, blk_rows, w_cols)
-        w_blocks = gathered[:, :d_rows, :]
-        pos_code = gathered[:, d_rows, : 2 * tok_rows].astype(jnp.int32)
+        w_qkv = gather_ctx(buf).reshape(nctx, blk_rows, qkv_cols)
+        w_o = gather_ctx(w_out.T).reshape(nctx, d_rows, w_out.shape[0])
+        pos_code = w_qkv[:, d_rows, : 2 * tok_rows].astype(jnp.int32)
         key_pos_all = pos_code[:, :tok_rows] * RUN + pos_code[:, tok_rows:]
 
         normed_g = to_gathered_order(normed.reshape(tok_rows, nctx, d_rows), sizes)
+        normed_g = jnp.pad(normed_g, ((0, 0), (0, 0), (0, blk_rows - d_rows)))
         proj = jnp.einsum(
-            "tjd,jdn->tn", normed_g, w_blocks[:, :, : q_cols + 2 * kv_cols],
-            preferred_element_type=jnp.float32,
+            "tjd,jdn->tn", normed_g, w_qkv, preferred_element_type=jnp.float32,
         )
         queries = proj[:, :q_cols].reshape(tok_rows, group_size, HEAD_DIM)
         key_proj = proj[:, q_cols : q_cols + kv_cols]
@@ -168,7 +176,7 @@
         attended = jnp.transpose(mixed, (0, 2, 1, 3)).reshape(tok_rows, q_cols)
 
         partial_g = jnp.einsum(
-            "tk,jdk->tjd", attended, w_blocks[:, :, q_cols + 2 * kv_cols :],
+            "tk,jdk->tjd", attended, w_o,
             preferred_element_type=jnp.float32,
         )
         partial_out = from_gathered_order(partial_g, sizes).reshape(tok_rows, width)

time: 478 us -> 422 us (0.88)
  waiting for transfers between devices: 376 us -> 278 us
  other arithmetic: 11 us -> 35.6 us
  starting transfers between devices: 0.27 us -> 16.1 us
    all_gather x6 -> x3, waiting for transfers between devices: 330 us -> 175 us  [gather_ctx(): x = lax.all_gather(x, 'z', axis=0, tiled=True)]
    ppermute x0 -> x6, waiting for transfers between devices: none -> 61.9 us  [swap_cat(): return jnp.concatenate([x, lax.ppermute(x, axis_name, [(0, 1), (1, 0)])], 0)]
    concatenate x1 -> x7, other arithmetic: 1.67 us -> 21.7 us  [the longest x6 20.1 us: swap_cat(): return jnp.concatenate([x, lax.ppermute(x, axis_name, [(0, 1), (1, 0)])], 0)]
    ppermute x0 -> x6, starting transfers between devices: none -> 15.9 us  [swap_cat(): return jnp.concatenate([x, lax.ppermute(x, axis_name, [(0, 1), (1, 0)])], 0)]
    reduce_scatter x1, waiting for transfers between devices: 46.1 us -> 41.1 us  [local(): lax.psum_scatter(partial_out.astype(jnp.bfloat16), HEAD, scatter_dimensio...]
  transfers between devices with their start and end apart: 7 -> 10, of which waited for: 7 -> 8; matrix products, arithmetic and copies ran while one was open for 3% -> 8% of each run, Pallas kernels for 0% -> 0%
where the time goes in v2:
time: 422 us; the launch traced here: 419 us
  waiting for transfers between devices  278 us (66%)
  blocking collectives  40.2 us (10%)
  other arithmetic  35.6 us (8%)
  local copies, waits for them, and re-layouts  22 us (5%)
  starting transfers between devices  16.1 us (4%)
  between operations  15 us (4%)
  matrix products  11.5 us (3%)
    all_gather x3, waiting for transfers between devices, gather_ctx(): x = lax.all_gather(x, 'z', axis=0, tiled=True)  175 us
    ppermute x6, waiting for transfers between devices, swap_cat(): return jnp.concatenate([x, lax.ppermute(x, axis_name, [(0, 1), (1, 0)])], 0)  61.9 us
    reduce_scatter x1, waiting for transfers between devices, local(): lax.psum_scatter(partial_out.astype(jnp.bfloat16), HEAD, scatter_dimensio...  41.1 us
    psum x3, blocking collectives, local(): sums = lax.psum(sums, axis)  40.2 us
    concatenate x6, other arithmetic, swap_cat(): return jnp.concatenate([x, lax.ppermute(x, axis_name, [(0, 1), (1, 0)])], 0)  20.1 us
    ppermute x6, starting transfers between devices, swap_cat(): return jnp.concatenate([x, lax.ppermute(x, axis_name, [(0, 1), (1, 0)])], 0)  15.9 us
  transfers between devices with their start and end apart: 10, of which 8 were waited for; matrix products, arithmetic and copies ran while one was open for 8% of the time, Pallas kernels for 0%

profile of v2, /device:TPU:6, one launch (start us, length us, event | category | flops | bytes accessed | tf_op | source)
XLA Modules:
  0.0 418.6 jit_solution(4112349526468133426)
XLA Ops:
  12.6 77.1 %all-gather.4.cloned.1.call-done = bf16[1152,768]{1,0:T(8,128)(2,1)} async-done(((bf16[72,768]{1,0:T(8,128)(2,1)}), bf16[1152,768]{1,0:T(8,128)(2,1)}) %all-gather.4.cloned.1.call-update) | async-done | bytes 1769488 | tf_op jit(solution)/shard_map/all_gather | solution.py:59
  89.7 3.3 collective-permute-start
  93.0 31.5 %collective-permute-done = bf16[1152,768]{1,0:T(8,128)(2,1)S(1)} collective-permute-done((bf16[1152,768]{1,0:T(8,128)(2,1)}, bf16[1152,768]{1,0:T(8,128)(2,1)S(1)}, u32[]{:S(2)}, u32[]{:S(2)}) %collective-permute-start) | collective-permute-done | bytes 1769504 | tf_op jit(solution)/shard_map/ppermute | solution.py:55
  124.6 4.2 pad_maximum_fusion.3
  135.2 1.9 collective-permute-done.1
  137.2 3.7 pad_maximum_fusion
  146.0 52.4 %all-gather.8.cloned.1.call-done = bf16[1024,512]{1,0:T(8,128)(2,1)} async-done(((bf16[64,512]{1,0:T(8,128)(2,1)}), bf16[1024,512]{1,0:T(8,128)(2,1)}) %all-gather.8.cloned.1.call-update) | async-done | bytes 1048592 | tf_op jit(solution)/shard_map/all_gather | solution.py:59
  198.4 3.5 collective-permute-start.4
  201.9 15.7 %collective-permute-done.4 = bf16[1024,512]{1,0:T(8,128)(2,1)S(1)} collective-permute-done((bf16[1024,512]{1,0:T(8,128)(2,1)}, bf16[1024,512]{1,0:T(8,128)(2,1)S(1)}, u32[]{:S(2)}, u32[]{:S(2)}) %collective-permute-start.4) | collective-permute-done | bytes 1048608 | tf_op jit(solution)/shard_map/ppermute | solution.py:55
  218.5 2.8 pad_maximum_fusion.5
  223.2 45.8 %all-gather.6.cloned.1.call-done = bf16[2048,256]{1,0:T(8,128)(2,1)} async-done(((bf16[128,256]{1,0:T(8,128)(2,1)}), bf16[2048,256]{1,0:T(8,128)(2,1)}) %all-gather.6.cloned.1.call-update) | async-done | bytes 1048592 | tf_op jit(solution)/shard_map/all_gather | solution.py:59
  269.0 3.3 collective-permute-start.2
  275.3 12.8 %collective-permute-done.2 = bf16[2048,256]{1,0:T(8,128)(2,1)S(1)} collective-permute-done((bf16[2048,256]{1,0:T(8,128)(2,1)}, bf16[2048,256]{1,0:T(8,128)(2,1)S(1)}, u32[]{:S(2)}, u32[]{:S(2)}) %collective-permute-start.2) | collective-permute-done | bytes 1048608 | tf_op jit(solution)/shard_map/ppermute | solution.py:55
  288.0 2.7 pad_maximum_fusion.4
  292.6 3.5 pad_maximum_fusion.2
  306.0 3.3 pad_maximum_fusion.1
  309.3 2.9 gather_fusion.4
  312.2 4.5 %fusion.47 = (f32[2,4,64]{2,1,0:T(4,128)S(1)}, bf16[2,4,64,2112]{3,2,1,0:T(8,128)(2,1)}) fusion(pred[2,64,2112]{2,1,0:T(8,128)(4,1)S(1)} %compare_and_fusion, bf16[2,2112,256]{2,1,0:T(8,128)(2,1)S(1)} %bitcast.84, bf16[2,64,4,64]{3,1,2,0:T(8,128)(2,1)} %copy.56, bf16[2,64,4,64]{3,1,2,0:T(8,128)(2,1)} %copy.55), kind=kOutput, calls=%fused_computation.125 | convolution fusion | flops 283576384 | bytes 3934208 | tf_op jit(solution)/shard_map/sub | solution.py:167
  316.8 2.4 fusion.18
  319.3 3.4 fusion.25
  327.7 41.1 %reduce-scatter.2.cloned.1.call-done = bf16[128,512]{0,1:T(8,128)(2,1)} async-done(((bf16[128,4096]{0,1:T(8,128)(2,1)}), bf16[128,512]{0,1:T(8,128)(2,1)}) %reduce-scatter.2.cloned.1.call-update) | async-done | bytes 131088 | tf_op jit(solution)/shard_map/reduce_scatter | solution.py:183
  369.9 2.5 psum.21
  372.4 6.4 %psum.22 = f32[2,512]{1,0:T(2,128)S(1)} all-reduce(f32[2,512]{1,0:T(2,128)S(1)} %psum.21), channel_id=1, replica_groups=mesh['z'=16,'xh'=2,'c'=2,'y'=4,'xl'=2] {'xh'}, use_global_device_ids=true, to_apply=%region_13.14 | all-reduce | flops 1024 | bytes 8192 | tf_op jit(solution)/shard_map/psum | solution.py:202
  378.8 31.3 %psum.23 = f32[2,512]{1,0:T(2,128)S(1)} all-reduce(f32[2,512]{1,0:T(2,128)S(1)} %psum.22), channel_id=1, replica_groups=mesh['z'=16,'xh'=2,'c'=2,'y'=4,'xl'=2] {'z'}, use_global_device_ids=true, to_apply=%region_14.15 | all-reduce | flops 1024 | bytes 8192 | tf_op jit(solution)/shard_map/psum | solution.py:202
  (132 shorter events, 41.7 us)
Async XLA Ops:
  7.2 82.5 %all-gather.4.cloned.1.call-start = ((), (), s32[]{:S(2)}) async-start(), calls=%async_computation.1 | async-start | bytes 1880064 | tf_op jit(solution)/shard_map/all_gather | solution.py:59
  12.6 118.2 %copy-start.6 = (bf16[128,4096]{1,0:T(8,128)(2,1)S(1)}, bf16[128,4096]{1,0:T(8,128)(2,1)}, u32[]{:S(2)}) copy-start(bf16[128,4096]{1,0:T(8,128)(2,1)} %param.9) | copy-start | bytes 3145732
  12.6 119.4 %copy-start.7 = (f32[4096]{0:T(1024)S(1)}, f32[4096]{0:T(1024)}, u32[]{:S(2)}) copy-start(f32[4096]{0:T(1024)} %param.10) | copy-start | bytes 49156
  12.6 185.8 %all-gather.8.cloned.1.call-start = ((), (), s32[]{:S(2)}) async-start(), calls=%async_computation.3 | async-start | bytes 1114112 | tf_op jit(solution)/shard_map/all_gather | solution.py:59
  89.7 34.9 %collective-permute-start = (bf16[1152,768]{1,0:T(8,128)(2,1)}, bf16[1152,768]{1,0:T(8,128)(2,1)S(1)}, u32[]{:S(2)}, u32[]{:S(2)}) collective-permute-start(bf16[1152,768]{1,0:T(8,128)(2,1)} %all-gather.4.cloned.1.call-done), channel_id=1, source_target_pairs={{0,16},{16,0},{1,17},{17,1},{2,18},{18,2},{3,19},{19,3},{4,20},{20... | collective-permute-start | bytes 5308424 | tf_op jit(solution)/shard_map/ppermute | solution.py:55
  124.6 4.2 copy-start.1
  128.7 8.4 %collective-permute-start.1 = (bf16[2304,768]{1,0:T(8,128)(2,1)}, bf16[2304,768]{1,0:T(8,128)(2,1)}, u32[]{:S(2)}, u32[]{:S(2)}) collective-permute-start(bf16[2304,768]{1,0:T(8,128)(2,1)} %pad_maximum_fusion.3), channel_id=1, source_target_pairs={{0,8},{8,0},{1,9},{9,1},{2,10},{10,2},{3,11},{11,3},{4,12},{12,4},... | collective-permute-start | bytes 10616840 | tf_op jit(solution)/shard_map/ppermute | solution.py:55
  130.7 138.3 %all-gather.6.cloned.1.call-start = ((), (), s32[]{:S(2)}) async-start(), calls=%async_computation.2 | async-start | bytes 1114112 | tf_op jit(solution)/shard_map/all_gather | solution.py:59
  134.8 6.1 %copy-start.14 = (pred[2]{0:T(512)(128)(4,1)}, pred[2]{0:T(512)(128)(4,1)S(1)}, u32[]{:S(2)}) copy-start(pred[2]{0:T(512)(128)(4,1)S(1)} %compare_and_fusion.2) | copy-start | bytes 10
  140.9 2.9 copy-start
  143.8 128.5 %copy-start.10 = (s32[128]{0:T(128)S(1)}, s32[128]{0:T(128)}, u32[]{:S(2)}) copy-start(s32[128]{0:T(128)} %param.15) | copy-start | bytes 1540
  145.9 222.9 %reduce-scatter.2.cloned.1.call-start = ((), (), s32[]{:S(2)}) async-start(), calls=%async_computation.4 | async-start | bytes 1179648 | tf_op jit(solution)/shard_map/reduce_scatter | solution.py:183
  198.4 94.2 %copy-start.2 = (bf16[1024,512]{1,0:T(8,128)(2,1)S(1)}, bf16[1024,512]{1,0:T(8,128)(2,1)}, u32[]{:S(2)}) copy-start(bf16[1024,512]{1,0:T(8,128)(2,1)} %all-gather.8.cloned.1.call-done) | copy-start | bytes 3145732
  198.4 19.2 %collective-permute-start.4 = (bf16[1024,512]{1,0:T(8,128)(2,1)}, bf16[1024,512]{1,0:T(8,128)(2,1)S(1)}, u32[]{:S(2)}, u32[]{:S(2)}) collective-permute-start(bf16[1024,512]{1,0:T(8,128)(2,1)} %all-gather.8.cloned.1.call-done), channel_id=1, source_target_pairs={{0,16},{16,0},{1,17},{17,1},{2,18},{18,2},{3,19},{19,3},{4,20},{20... | collective-permute-start | bytes 3145736 | tf_op jit(solution)/shard_map/ppermute | solution.py:55
  221.3 71.3 %collective-permute-start.5 = (bf16[2048,512]{1,0:T(8,128)(2,1)}, bf16[2048,512]{1,0:T(8,128)(2,1)}, u32[]{:S(2)}, u32[]{:S(2)}) collective-permute-start(bf16[2048,512]{1,0:T(8,128)(2,1)} %pad_maximum_fusion.5), channel_id=1, source_target_pairs={{0,8},{8,0},{1,9},{9,1},{2,10},{10,2},{3,11},{11,3},{4,12},{12,4},... | collective-permute-start | bytes 6291464 | tf_op jit(solution)/shard_map/ppermute | solution.py:55
  269.0 19.0 %collective-permute-start.2 = (bf16[2048,256]{1,0:T(8,128)(2,1)}, bf16[2048,256]{1,0:T(8,128)(2,1)S(1)}, u32[]{:S(2)}, u32[]{:S(2)}) collective-permute-start(bf16[2048,256]{1,0:T(8,128)(2,1)} %all-gather.6.cloned.1.call-done), channel_id=1, source_target_pairs={{0,16},{16,0},{1,17},{17,1},{2,18},{18,2},{3,19},{19,3},{4,20},{20... | collective-permute-start | bytes 3145736 | tf_op jit(solution)/shard_map/ppermute | solution.py:55
  272.4 2.1 copy-start.13
  275.3 17.4 %copy-start.5 = (bf16[1024,512]{1,0:T(8,128)(2,1)S(1)}, bf16[1024,512]{1,0:T(8,128)(2,1)}, u32[]{:S(2)}) copy-start(bf16[1024,512]{1,0:T(8,128)(2,1)} %copy-done.4) | copy-start | bytes 3145732
  290.7 15.3 %collective-permute-start.3 = (bf16[4096,256]{1,0:T(8,128)(2,1)}, bf16[4096,256]{1,0:T(8,128)(2,1)}, u32[]{:S(2)}, u32[]{:S(2)}) collective-permute-start(bf16[4096,256]{1,0:T(8,128)(2,1)} %pad_maximum_fusion.4), channel_id=1, source_target_pairs={{0,8},{8,0},{1,9},{9,1},{2,10},{10,2},{3,11},{11,3},{4,12},{12,4},... | collective-permute-start | bytes 6291464 | tf_op jit(solution)/shard_map/ppermute | solution.py:55
  296.1 9.9 %copy-start.3 = (bf16[2048,256]{1,0:T(8,128)(2,1)S(1)}, bf16[2048,256]{1,0:T(8,128)(2,1)}, u32[]{:S(2)}) copy-start(bf16[2048,256]{1,0:T(8,128)(2,1)} %all-gather.6.cloned.1.call-done) | copy-start | bytes 3145732
  319.3 4.2 %copy-start.9 = (pred[2]{0:T(512)(128)(4,1)S(1)}, pred[2]{0:T(512)(128)(4,1)}, u32[]{:S(2)}) copy-start(pred[2]{0:T(512)(128)(4,1)} %copy-done.8) | copy-start | bytes 10
  324.7 1.5 copy-start.17
  324.7 2.8 copy-start.11
  324.7 2.8 copy-start.12
  (4 other events, 3.8 us)
Sparse Core Ops, SparseCore 0:
  12.7 76.9 all-gather.3
  130.8 67.5 all-gather.7
  201.0 67.9 all-gather.5
  326.4 42.3 reduce-scatter.1

commit v3 on v2

--- a/solution.py
+++ b/solution.py
@@ -55,10 +55,12 @@
     return jnp.concatenate([x, lax.ppermute(x, axis_name, [(0, 1), (1, 0)])], 0)
 
 
-def gather_ctx(x):
-    x = lax.all_gather(x, "z", axis=0, tiled=True)
-    x = swap_cat(x, "xh")
-    return swap_cat(x, "c")
+def gather_z(x):
+    return lax.all_gather(x, "z", axis=0, tiled=True)
+
+
+def gather_pair(x):
+    return swap_cat(swap_cat(x, "xh"), "c")
 
 
 def relative_index():
@@ -110,17 +112,18 @@
             ]
         )[None, :]
         pad_rows = -(d_rows + 1) % 8
+        out_cols = w_out.shape[0]
         buf = jnp.concatenate(
             [
-                jnp.concatenate([w_query, w_key, w_value], axis=1),
-                pos_row,
-                jnp.zeros((pad_rows, qkv_cols), jnp.bfloat16),
+                jnp.concatenate([w_query, w_key, w_value, w_out.T], axis=1),
+                jnp.pad(pos_row, ((0, pad_rows), (0, out_cols))),
             ],
             axis=0,
         )
         blk_rows = buf.shape[0]
-        w_qkv = gather_ctx(buf).reshape(nctx, blk_rows, qkv_cols)
-        w_o = gather_ctx(w_out.T).reshape(nctx, d_rows, w_out.shape[0])
+        w_z = gather_z(buf)
+        w_qkv = gather_pair(w_z[:, :qkv_cols]).reshape(nctx, blk_rows, qkv_cols)
+        w_o = gather_pair(w_z[:, qkv_cols:]).reshape(nctx, blk_rows, out_cols)[:, :d_rows]
         pos_code = w_qkv[:, d_rows, : 2 * tok_rows].astype(jnp.int32)
         key_pos_all = pos_code[:, :tok_rows] * RUN + pos_code[:, tok_rows:]
 
@@ -135,7 +138,7 @@
         queries = rotate(queries, in_doc).astype(jnp.bfloat16)
         key_proj = rotate(key_proj, in_doc).astype(jnp.bfloat16)
 
-        kv = gather_ctx(jnp.concatenate([key_proj, value_proj], axis=1))
+        kv = gather_pair(gather_z(jnp.concatenate([key_proj, value_proj], axis=1)))
         kv_halves = kv.reshape(total_runs, RUN, 2 * kv_cols)
         pos_halves = key_pos_all.reshape(total_runs, RUN)
         run_of_half = pos_halves[:, 0] // RUN

time: 422 us -> 374 us (0.89)
  waiting for transfers between devices: 278 us -> 230 us
  local copies, waits for them, and re-layouts: 22 us -> 28.1 us
  other arithmetic: 35.6 us -> 30.3 us
    all_gather x3 -> x2, waiting for transfers between devices: 175 us -> 122 us  [gather_z(): return lax.all_gather(x, 'z', axis=0, tiled=True)]
    slice x0 -> x3, local copies, waits for them, and re-layouts: none -> 5.61 us  [the longest x1 2.67 us: local(): gather_pair(w_z[:, qkv_cols:]).reshape(nctx, blk_rows, out_cols)[:, :d_rows]]
    ppermute x6, waiting for transfers between devices: 61.9 us -> 67.2 us  [swap_cat(): return jnp.concatenate([x, lax.ppermute(x, axis_name, [(0, 1), (1, 0)])], 0)]
    gather x3, local copies, waits for them, and re-layouts: 1.57 us -> 5.92 us  [to_gathered_order(): y = jnp.take(jnp.take(y, c_idx, axis=1), xh_idx, axis=2)]
  transfers between devices with their start and end apart: 10 -> 9, of which waited for: 8 -> 6; matrix products, arithmetic and copies ran while one was open for 8% -> 10% of each run, Pallas kernels for 0% -> 0%
where the time goes in v3:
time: 374 us; the launch traced here: 370 us
  waiting for transfers between devices  230 us (61%)
  blocking collectives  40.2 us (11%)
  other arithmetic  30.3 us (8%)
  local copies, waits for them, and re-layouts  28.1 us (8%)
  starting transfers between devices  16.1 us (4%)
  between operations  14.8 us (4%)
  matrix products  10.5 us (3%)
    all_gather x2, waiting for transfers between devices, gather_z(): return lax.all_gather(x, 'z', axis=0, tiled=True)  122 us
    ppermute x6, waiting for transfers between devices, swap_cat(): return jnp.concatenate([x, lax.ppermute(x, axis_name, [(0, 1), (1, 0)])], 0)  67.2 us
    reduce_scatter x1, waiting for transfers between devices, local(): lax.psum_scatter(partial_out.astype(jnp.bfloat16), HEAD, scatter_dimensio...  41.3 us
    psum x3, blocking collectives, local(): sums = lax.psum(sums, axis)  40.2 us
    concatenate x6, other arithmetic, swap_cat(): return jnp.concatenate([x, lax.ppermute(x, axis_name, [(0, 1), (1, 0)])], 0)  16.5 us
    ppermute x6, starting transfers between devices, swap_cat(): return jnp.concatenate([x, lax.ppermute(x, axis_name, [(0, 1), (1, 0)])], 0)  16 us
  transfers between devices with their start and end apart: 9, of which 6 were waited for; matrix products, arithmetic and copies ran while one was open for 10% of the time, Pallas kernels for 0%

profile of v3, /device:TPU:6, one launch (start us, length us, event | category | flops | bytes accessed | tf_op | source)
XLA Modules:
  0.0 370.5 jit_solution(10222787951417290050)
XLA Ops:
  12.0 80.4 %all-gather.3.cloned.1.call-done = bf16[1152,1280]{1,0:T(8,128)(2,1)} async-done(((bf16[72,1280]{1,0:T(8,128)(2,1)}), bf16[1152,1280]{1,0:T(8,128)(2,1)}) %all-gather.3.cloned.1.call-update) | async-done | bytes 2949136 | tf_op jit(solution)/shard_map/all_gather | solution.py:59
  94.0 3.4 collective-permute-start
  97.4 31.5 %collective-permute-done = bf16[1152,768]{1,0:T(8,128)(2,1)S(1)} collective-permute-done((bf16[1152,768]{1,0:T(8,128)(2,1)S(1)}, bf16[1152,768]{1,0:T(8,128)(2,1)S(1)}, u32[]{:S(2)}, u32[]{:S(2)}) %collective-permute-start) | collective-permute-done | bytes 1769504 | tf_op jit(solution)/shard_map/ppermute | solution.py:55
  128.9 2.2 pad_maximum_fusion.3
  137.5 3.0 gather_fusion.2
  146.7 3.4 collective-permute-start.4
  150.0 3.3 pad_maximum_fusion
  157.8 20.7 %collective-permute-done.4 = bf16[1152,512]{1,0:T(8,128)(2,1)} collective-permute-done((bf16[1152,512]{1,0:T(8,128)(2,1)S(1)}, bf16[1152,512]{1,0:T(8,128)(2,1)}, u32[]{:S(2)}, u32[]{:S(2)}) %collective-permute-start.4) | collective-permute-done | bytes 1179680 | tf_op jit(solution)/shard_map/ppermute | solution.py:55
  178.5 2.8 pad_maximum_fusion.4
  183.3 41.5 %all-gather.5.cloned.1.call-done = bf16[2048,256]{1,0:T(8,128)(2,1)} async-done(((bf16[128,256]{1,0:T(8,128)(2,1)}), bf16[2048,256]{1,0:T(8,128)(2,1)}) %all-gather.5.cloned.1.call-update) | async-done | bytes 1048592 | tf_op jit(solution)/shard_map/all_gather | solution.py:59
  224.8 3.4 collective-permute-start.2
  228.6 15.0 %collective-permute-done.2 = bf16[2048,256]{1,0:T(8,128)(2,1)S(1)} collective-permute-done((bf16[2048,256]{1,0:T(8,128)(2,1)}, bf16[2048,256]{1,0:T(8,128)(2,1)S(1)}, u32[]{:S(2)}, u32[]{:S(2)}) %collective-permute-start.2) | collective-permute-done | bytes 1048608 | tf_op jit(solution)/shard_map/ppermute | solution.py:55
  243.6 2.7 pad_maximum_fusion.5
  248.2 2.2 pad_maximum_fusion.1
  250.4 2.7 slice.104
  258.7 3.3 pad_maximum_fusion.2
  262.0 2.9 gather_fusion.4
  264.9 3.6 fusion.49
  268.5 2.4 fusion.18
  271.0 3.4 fusion.27
  279.3 41.3 %reduce-scatter.2.cloned.1.call-done = bf16[128,512]{0,1:T(8,128)(2,1)} async-done(((bf16[128,4096]{0,1:T(8,128)(2,1)}), bf16[128,512]{0,1:T(8,128)(2,1)}) %reduce-scatter.2.cloned.1.call-update) | async-done | bytes 131088 | tf_op jit(solution)/shard_map/reduce_scatter | solution.py:186
  322.6 2.5 psum.21
  325.0 6.4 %psum.22 = f32[2,512]{1,0:T(2,128)S(1)} all-reduce(f32[2,512]{1,0:T(2,128)S(1)} %psum.21), channel_id=1, replica_groups=mesh['z'=16,'xh'=2,'c'=2,'y'=4,'xl'=2] {'xh'}, use_global_device_ids=true, to_apply=%region_13.14 | all-reduce | flops 1024 | bytes 8192 | tf_op jit(solution)/shard_map/psum | solution.py:205
  331.5 31.3 %psum.23 = f32[2,512]{1,0:T(2,128)S(1)} all-reduce(f32[2,512]{1,0:T(2,128)S(1)} %psum.22), channel_id=1, replica_groups=mesh['z'=16,'xh'=2,'c'=2,'y'=4,'xl'=2] {'z'}, use_global_device_ids=true, to_apply=%region_14.15 | all-reduce | flops 1024 | bytes 8192 | tf_op jit(solution)/shard_map/psum | solution.py:205
  (108 shorter events, 40.6 us)
Async XLA Ops:
  7.2 85.2 %all-gather.3.cloned.1.call-start = ((), (), s32[]{:S(2)}) async-start(), calls=%async_computation.1 | async-start | bytes 3133440 | tf_op jit(solution)/shard_map/all_gather | solution.py:59
  11.9 212.8 %all-gather.5.cloned.1.call-start = ((), (), s32[]{:S(2)}) async-start(), calls=%async_computation.2 | async-start | bytes 1114112 | tf_op jit(solution)/shard_map/all_gather | solution.py:59
  94.0 34.9 %collective-permute-start = (bf16[1152,768]{1,0:T(8,128)(2,1)S(1)}, bf16[1152,768]{1,0:T(8,128)(2,1)S(1)}, u32[]{:S(2)}, u32[]{:S(2)}) collective-permute-start(bf16[1152,768]{1,0:T(8,128)(2,1)S(1)} %slice.90), channel_id=1, source_target_pairs={{0,16},{16,0},{1,17},{17,1},{2,18},{18,2},{3,19},{19,3},{4,20},{20... | collective-permute-start | bytes 5308424 | tf_op jit(solution)/shard_map/ppermute | solution.py:55
  128.9 2.4 copy-start.2
  131.3 4.3 %copy-start.4 = (f32[4096]{0:T(1024)S(1)}, f32[4096]{0:T(1024)}, u32[]{:S(2)}) copy-start(f32[4096]{0:T(1024)} %param.10) | copy-start | bytes 49156
  131.3 18.8 %collective-permute-start.1 = (bf16[2304,768]{1,0:T(8,128)(2,1)}, bf16[2304,768]{1,0:T(8,128)(2,1)}, u32[]{:S(2)}, u32[]{:S(2)}) collective-permute-start(bf16[2304,768]{1,0:T(8,128)(2,1)} %pad_maximum_fusion.3), channel_id=1, source_target_pairs={{0,8},{8,0},{1,9},{9,1},{2,10},{10,2},{3,11},{11,3},{4,12},{12,4},... | collective-permute-start | bytes 10616840 | tf_op jit(solution)/shard_map/ppermute | solution.py:55
  134.9 5.5 %copy-start.1 = (bf16[128,4096]{0,1:T(8,128)(2,1)}, bf16[128,4096]{0,1:T(8,128)(2,1)S(1)}, u32[]{:S(2)}) copy-start(bf16[128,4096]{0,1:T(8,128)(2,1)S(1)} %copy.43) | copy-start | bytes 3145732
  146.7 31.9 %collective-permute-start.4 = (bf16[1152,512]{1,0:T(8,128)(2,1)S(1)}, bf16[1152,512]{1,0:T(8,128)(2,1)}, u32[]{:S(2)}, u32[]{:S(2)}) collective-permute-start(bf16[1152,512]{1,0:T(8,128)(2,1)S(1)} %slice.103), channel_id=1, source_target_pairs={{0,16},{16,0},{1,17},{17,1},{2,18},{18,2},{3,19},{19,3},{4,20},{20... | collective-permute-start | bytes 3538952 | tf_op jit(solution)/shard_map/ppermute | solution.py:55
  153.4 2.9 copy-start
  156.3 71.9 %copy-start.5 = (s32[128]{0:T(128)S(1)}, s32[128]{0:T(128)}, u32[]{:S(2)}) copy-start(s32[128]{0:T(128)} %param.15) | copy-start | bytes 1540
  157.8 162.8 %reduce-scatter.2.cloned.1.call-start = ((), (), s32[]{:S(2)}) async-start(), calls=%async_computation.3 | async-start | bytes 1179648 | tf_op jit(solution)/shard_map/reduce_scatter | solution.py:186
  181.4 66.8 %collective-permute-start.5 = (bf16[2304,512]{1,0:T(8,128)(2,1)}, bf16[2304,512]{1,0:T(8,128)(2,1)}, u32[]{:S(2)}, u32[]{:S(2)}) collective-permute-start(bf16[2304,512]{1,0:T(8,128)(2,1)} %pad_maximum_fusion.4), channel_id=1, source_target_pairs={{0,8},{8,0},{1,9},{9,1},{2,10},{10,2},{3,11},{11,3},{4,12},{12,4},... | collective-permute-start | bytes 7077896 | tf_op jit(solution)/shard_map/ppermute | solution.py:55
  224.8 18.9 %collective-permute-start.2 = (bf16[2048,256]{1,0:T(8,128)(2,1)}, bf16[2048,256]{1,0:T(8,128)(2,1)S(1)}, u32[]{:S(2)}, u32[]{:S(2)}) collective-permute-start(bf16[2048,256]{1,0:T(8,128)(2,1)} %all-gather.5.cloned.1.call-done), channel_id=1, source_target_pairs={{0,16},{16,0},{1,17},{17,1},{2,18},{18,2},{3,19},{19,3},{4,20},{20... | collective-permute-start | bytes 3145736 | tf_op jit(solution)/shard_map/ppermute | solution.py:55
  246.3 12.4 %collective-permute-start.3 = (bf16[4096,256]{1,0:T(8,128)(2,1)}, bf16[4096,256]{1,0:T(8,128)(2,1)}, u32[]{:S(2)}, u32[]{:S(2)}) collective-permute-start(bf16[4096,256]{1,0:T(8,128)(2,1)} %pad_maximum_fusion.5), channel_id=1, source_target_pairs={{0,8},{8,0},{1,9},{9,1},{2,10},{10,2},{3,11},{11,3},{4,12},{12,4},... | collective-permute-start | bytes 6291464 | tf_op jit(solution)/shard_map/ppermute | solution.py:55
  253.0 5.6 %copy-start.3 = (bf16[2048,256]{1,0:T(8,128)(2,1)S(1)}, bf16[2048,256]{1,0:T(8,128)(2,1)}, u32[]{:S(2)}) copy-start(bf16[2048,256]{1,0:T(8,128)(2,1)} %all-gather.5.cloned.1.call-done) | copy-start | bytes 3145732
  276.4 1.5 copy-start.6
Sparse Core Ops, SparseCore 0:
  12.1 80.3 all-gather.2
  157.9 66.8 all-gather.4
  278.0 42.5 reduce-scatter.1

commit v4 on v3

--- a/solution.py
+++ b/solution.py
@@ -86,7 +86,25 @@
     return jnp.transpose(y, (0, 3, 2, 1, 4)).reshape(x.shape)
 
 
-def make_local(sizes):
+def reduce_scatter_head(x, head_sizes):
+    ny, nxl = head_sizes
+    rows, width = x.shape
+    xl = lax.axis_index("xl")
+    y = lax.axis_index("y")
+    grouped = x.reshape(rows, ny, nxl, width // (ny * nxl))
+    kept = jnp.take(grouped, xl, axis=2)
+    sent = jnp.take(grouped, (xl + 1) % nxl, axis=2).astype(jnp.bfloat16)
+    summed = kept + lax.ppermute(sent, "xl", [(0, 1), (1, 0)]).astype(jnp.float32)
+    acc = jnp.take(summed, y, axis=1)
+    for shift in range(1, ny):
+        piece = jnp.take(summed, (y + shift) % ny, axis=1).astype(jnp.bfloat16)
+        acc = acc + lax.ppermute(
+            piece, "y", [(i, (i + shift) % ny) for i in range(ny)]
+        ).astype(jnp.float32)
+    return acc
+
+
+def make_local(sizes, head_sizes):
     nz, nxh, nc = sizes
     nctx = nz * nxh * nc
 
@@ -183,11 +201,9 @@
             preferred_element_type=jnp.float32,
         )
         partial_out = from_gathered_order(partial_g, sizes).reshape(tok_rows, width)
-        head_share = lax.psum_scatter(
-            partial_out.astype(jnp.bfloat16), HEAD, scatter_dimension=1, tiled=True
-        ).astype(jnp.float32)
+        head_share = reduce_scatter_head(partial_out, head_sizes)
         col_width = head_share.shape[1]
-        head_idx = lax.axis_index("y") * lax.axis_size("xl") + lax.axis_index("xl")
+        head_idx = lax.axis_index("y") * head_sizes[1] + lax.axis_index("xl")
         own_cols = lax.dynamic_slice_in_dim(tokens, head_idx * col_width, col_width, 1)
         residual_out = (own_cols.astype(jnp.float32) + head_share).astype(jnp.bfloat16)
 
@@ -228,7 +244,7 @@
         P(),
     )
     return jax.shard_map(
-        make_local((nz, nxh, nc)),
+        make_local((nz, nxh, nc), (ny, nxl)),
         mesh=fine,
         in_specs=placed,
         out_specs=(P(CTX, HEAD), P(HEAD)),

time: 374 us -> 366 us (0.979)
  waiting for transfers between devices: 230 us -> 207 us
  starting transfers between devices: 16.1 us -> 29 us
  other arithmetic: 30.3 us -> 35.4 us
    reduce_scatter x1 -> x0, waiting for transfers between devices: 41.3 us -> none  [local(): lax.psum_scatter(partial_out.astype(jnp.bfloat16), HEAD, scatter_dimensio...]
    ppermute x0 -> x4, waiting for transfers between devices: none -> 17.7 us  [the longest x1 13.4 us: reduce_scatter_head(): lax.ppermute(sent, 'xl', [(0, 1), (1, 0)]).astype(jnp.float32)]
    ppermute x0 -> x4, starting transfers between devices: none -> 13 us  [the longest x3 10.2 us: reduce_scatter_head(): lax.ppermute(piece, 'y', [(i, (i + shift) % ny) for i in range(ny)])]
  transfers between devices with their start and end apart: 9 -> 12, of which waited for: 6 -> 8; matrix products, arithmetic and copies ran while one was open for 10% -> 10% of each run, Pallas kernels for 0% -> 0%
where the time goes in v4:
time: 366 us; the launch traced here: 365 us
  waiting for transfers between devices  207 us (57%)
  blocking collectives  38.4 us (10%)
  other arithmetic  35.4 us (10%)
  starting transfers between devices  29 us (8%)
  local copies, waits for them, and re-layouts  29 us (8%)
  between operations  15.3 us (4%)
  matrix products  10.5 us (3%)
    all_gather x2, waiting for transfers between devices, gather_z(): return lax.all_gather(x, 'z', axis=0, tiled=True)  122 us
    ppermute x6, waiting for transfers between devices, swap_cat(): return jnp.concatenate([x, lax.ppermute(x, axis_name, [(0, 1), (1, 0)])], 0)  67.3 us
    psum x3, blocking collectives, local(): sums = lax.psum(sums, axis)  38.4 us
    concatenate x6, other arithmetic, swap_cat(): return jnp.concatenate([x, lax.ppermute(x, axis_name, [(0, 1), (1, 0)])], 0)  16.5 us
    ppermute x6, starting transfers between devices, swap_cat(): return jnp.concatenate([x, lax.ppermute(x, axis_name, [(0, 1), (1, 0)])], 0)  16 us
    ppermute x1, waiting for transfers between devices, reduce_scatter_head(): lax.ppermute(sent, 'xl', [(0, 1), (1, 0)]).astype(jnp.float32)  13.4 us
    ppermute x3, starting transfers between devices, reduce_scatter_head(): lax.ppermute(piece, 'y', [(i, (i + shift) % ny) for i in range(ny)])  10.2 us
  transfers between devices with their start and end apart: 12, of which 8 were waited for; matrix products, arithmetic and copies ran while one was open for 10% of the time, Pallas kernels for 0%

profile of v4, /device:TPU:6, one launch (start us, length us, event | category | flops | bytes accessed | tf_op | source)
XLA Modules:
  0.0 364.5 jit_solution(4073207348337288373)
XLA Ops:
  12.0 80.4 %all-gather.3.cloned.1.call-done = bf16[1152,1280]{1,0:T(8,128)(2,1)} async-done(((bf16[72,1280]{1,0:T(8,128)(2,1)}), bf16[1152,1280]{1,0:T(8,128)(2,1)}) %all-gather.3.cloned.1.call-update) | async-done | bytes 2949136 | tf_op jit(solution)/shard_map/all_gather | solution.py:59
  94.0 3.4 collective-permute-start
  97.4 31.5 %collective-permute-done = bf16[1152,768]{1,0:T(8,128)(2,1)S(1)} collective-permute-done((bf16[1152,768]{1,0:T(8,128)(2,1)S(1)}, bf16[1152,768]{1,0:T(8,128)(2,1)S(1)}, u32[]{:S(2)}, u32[]{:S(2)}) %collective-permute-start) | collective-permute-done | bytes 1769504 | tf_op jit(solution)/shard_map/ppermute | solution.py:55
  146.6 3.4 collective-permute-start.4
  150.0 3.3 pad_maximum_fusion
  157.7 20.8 %collective-permute-done.4 = bf16[1152,512]{1,0:T(8,128)(2,1)} collective-permute-done((bf16[1152,512]{1,0:T(8,128)(2,1)S(1)}, bf16[1152,512]{1,0:T(8,128)(2,1)}, u32[]{:S(2)}, u32[]{:S(2)}) %collective-permute-start.4) | collective-permute-done | bytes 1179680 | tf_op jit(solution)/shard_map/ppermute | solution.py:55
  178.5 2.8 pad_maximum_fusion.4
  183.2 41.5 %all-gather.5.cloned.1.call-done = bf16[2048,256]{1,0:T(8,128)(2,1)} async-done(((bf16[128,256]{1,0:T(8,128)(2,1)}), bf16[2048,256]{1,0:T(8,128)(2,1)}) %all-gather.5.cloned.1.call-update) | async-done | bytes 1048592 | tf_op jit(solution)/shard_map/all_gather | solution.py:59
  224.7 3.4 collective-permute-start.2
  228.6 15.0 %collective-permute-done.2 = bf16[2048,256]{1,0:T(8,128)(2,1)S(1)} collective-permute-done((bf16[2048,256]{1,0:T(8,128)(2,1)}, bf16[2048,256]{1,0:T(8,128)(2,1)S(1)}, u32[]{:S(2)}, u32[]{:S(2)}) %collective-permute-start.2) | collective-permute-done | bytes 1048608 | tf_op jit(solution)/shard_map/ppermute | solution.py:55
  243.6 2.7 pad_maximum_fusion.5
  250.3 2.7 slice.124
  258.6 3.3 pad_maximum_fusion.2
  262.0 2.9 gather_fusion.4
  264.8 3.6 fusion.55
  271.0 3.4 fusion.32
  282.6 2.8 collective-permute-start.6
  285.5 13.4 %collective-permute-done.6 = bf16[128,4,512]{0,2,1:T(8,128)(2,1)} collective-permute-done((bf16[128,4,512]{0,2,1:T(8,128)(2,1)S(1)}, bf16[128,4,512]{0,2,1:T(8,128)(2,1)}, u32[]{:S(2)}, u32[]{:S(2)}) %collective-permute-start.6) | collective-permute-done | bytes 524320 | tf_op jit(solution)/shard_map/ppermute | solution.py:97
  300.1 4.6 %collective-permute-start.9 = (bf16[128,512]{0,1:T(8,128)(2,1)S(1)}, bf16[128,512]{0,1:T(8,128)(2,1)S(1)}, u32[]{:S(2)}, u32[]{:S(2)}) collective-permute-start(bf16[128,512]{0,1:T(8,128)(2,1)S(1)} %get-tuple-element.38), channel_id=1, source_target_pairs={{0,6},{2,0},{4,2},{6,4},{1,7},{3,1},{5,3},{7,5},{8,14},{10,8},{12,... | collective-permute-start | bytes 393224 | tf_op jit(solution)/shard_map/ppermute | solution.py:101
  304.8 2.7 collective-permute-start.8
  307.5 2.8 collective-permute-start.7
  318.1 2.5 psum.21
  320.5 6.4 %psum.22 = f32[2,512]{1,0:T(2,128)S(1)} all-reduce(f32[2,512]{1,0:T(2,128)S(1)} %psum.21), channel_id=1, replica_groups=mesh['z'=16,'xh'=2,'c'=2,'y'=4,'xl'=2] {'xh'}, use_global_device_ids=true, to_apply=%region_12.15 | all-reduce | flops 1024 | bytes 8192 | tf_op jit(solution)/shard_map/psum | solution.py:221
  326.9 29.5 %psum.23 = f32[2,512]{1,0:T(2,128)S(1)} all-reduce(f32[2,512]{1,0:T(2,128)S(1)} %psum.22), channel_id=1, replica_groups=mesh['z'=16,'xh'=2,'c'=2,'y'=4,'xl'=2] {'z'}, use_global_device_ids=true, to_apply=%region_13.16 | all-reduce | flops 1024 | bytes 8192 | tf_op jit(solution)/shard_map/psum | solution.py:221
  (114 shorter events, 60.5 us)
Async XLA Ops:
  7.2 85.2 %all-gather.3.cloned.1.call-start = ((), (), s32[]{:S(2)}) async-start(), calls=%async_computation | async-start | bytes 3133440 | tf_op jit(solution)/shard_map/all_gather | solution.py:59
  11.9 212.8 %all-gather.5.cloned.1.call-start = ((), (), s32[]{:S(2)}) async-start(), calls=%async_computation.1 | async-start | bytes 1114112 | tf_op jit(solution)/shard_map/all_gather | solution.py:59
  94.0 34.9 %collective-permute-start = (bf16[1152,768]{1,0:T(8,128)(2,1)S(1)}, bf16[1152,768]{1,0:T(8,128)(2,1)S(1)}, u32[]{:S(2)}, u32[]{:S(2)}) collective-permute-start(bf16[1152,768]{1,0:T(8,128)(2,1)S(1)} %slice.110), channel_id=1, source_target_pairs={{0,16},{16,0},{1,17},{17,1},{2,18},{18,2},{3,19},{19,3},{4,20},{20... | collective-permute-start | bytes 5308424 | tf_op jit(solution)/shard_map/ppermute | solution.py:55
  128.9 2.4 copy-start.2
  131.3 4.3 %copy-start.4 = (f32[4096]{0:T(1024)S(1)}, f32[4096]{0:T(1024)}, u32[]{:S(2)}) copy-start(f32[4096]{0:T(1024)} %param.14) | copy-start | bytes 49156
  131.3 18.7 %collective-permute-start.1 = (bf16[2304,768]{1,0:T(8,128)(2,1)}, bf16[2304,768]{1,0:T(8,128)(2,1)}, u32[]{:S(2)}, u32[]{:S(2)}) collective-permute-start(bf16[2304,768]{1,0:T(8,128)(2,1)} %pad_maximum_fusion.3), channel_id=1, source_target_pairs={{0,8},{8,0},{1,9},{9,1},{2,10},{10,2},{3,11},{11,3},{4,12},{12,4},... | collective-permute-start | bytes 10616840 | tf_op jit(solution)/shard_map/ppermute | solution.py:55
  134.9 2.4 copy-start.1
  146.6 31.9 %collective-permute-start.4 = (bf16[1152,512]{1,0:T(8,128)(2,1)S(1)}, bf16[1152,512]{1,0:T(8,128)(2,1)}, u32[]{:S(2)}, u32[]{:S(2)}) collective-permute-start(bf16[1152,512]{1,0:T(8,128)(2,1)S(1)} %slice.123), channel_id=1, source_target_pairs={{0,16},{16,0},{1,17},{17,1},{2,18},{18,2},{3,19},{19,3},{4,20},{20... | collective-permute-start | bytes 3538952 | tf_op jit(solution)/shard_map/ppermute | solution.py:55
  153.3 2.9 copy-start
  157.7 70.4 %copy-start.5 = (s32[128]{0:T(128)S(1)}, s32[128]{0:T(128)}, u32[]{:S(2)}) copy-start(s32[128]{0:T(128)} %param.19) | copy-start | bytes 1540
  181.3 66.8 %collective-permute-start.5 = (bf16[2304,512]{1,0:T(8,128)(2,1)}, bf16[2304,512]{1,0:T(8,128)(2,1)}, u32[]{:S(2)}, u32[]{:S(2)}) collective-permute-start(bf16[2304,512]{1,0:T(8,128)(2,1)} %pad_maximum_fusion.4), channel_id=1, source_target_pairs={{0,8},{8,0},{1,9},{9,1},{2,10},{10,2},{3,11},{11,3},{4,12},{12,4},... | collective-permute-start | bytes 7077896 | tf_op jit(solution)/shard_map/ppermute | solution.py:55
  224.7 18.9 %collective-permute-start.2 = (bf16[2048,256]{1,0:T(8,128)(2,1)}, bf16[2048,256]{1,0:T(8,128)(2,1)S(1)}, u32[]{:S(2)}, u32[]{:S(2)}) collective-permute-start(bf16[2048,256]{1,0:T(8,128)(2,1)} %all-gather.5.cloned.1.call-done), channel_id=1, source_target_pairs={{0,16},{16,0},{1,17},{17,1},{2,18},{18,2},{3,19},{19,3},{4,20},{20... | collective-permute-start | bytes 3145736 | tf_op jit(solution)/shard_map/ppermute | solution.py:55
  246.2 12.4 %collective-permute-start.3 = (bf16[4096,256]{1,0:T(8,128)(2,1)}, bf16[4096,256]{1,0:T(8,128)(2,1)}, u32[]{:S(2)}, u32[]{:S(2)}) collective-permute-start(bf16[4096,256]{1,0:T(8,128)(2,1)} %pad_maximum_fusion.5), channel_id=1, source_target_pairs={{0,8},{8,0},{1,9},{9,1},{2,10},{10,2},{3,11},{11,3},{4,12},{12,4},... | collective-permute-start | bytes 6291464 | tf_op jit(solution)/shard_map/ppermute | solution.py:55
  253.0 5.6 %copy-start.3 = (bf16[2048,256]{1,0:T(8,128)(2,1)S(1)}, bf16[2048,256]{1,0:T(8,128)(2,1)}, u32[]{:S(2)}) copy-start(bf16[2048,256]{1,0:T(8,128)(2,1)} %all-gather.5.cloned.1.call-done) | copy-start | bytes 3145732
  282.4 27.9 %copy-start.6 = (s32[32]{0:T(128)S(1)}, s32[32]{0:T(128)}, u32[]{:S(2)}) copy-start(s32[32]{0:T(128)} %param.21) | copy-start | bytes 388
  282.6 16.3 %collective-permute-start.6 = (bf16[128,4,512]{0,2,1:T(8,128)(2,1)S(1)}, bf16[128,4,512]{0,2,1:T(8,128)(2,1)}, u32[]{:S(2)}, u32[]{:S(2)}) collective-permute-start(bf16[128,4,512]{0,2,1:T(8,128)(2,1)S(1)} %bitcast_convert_fusion), channel_id=1, source_target_pairs={{0,1},{1,0},{2,3},{3,2},{4,5},{5,4},{6,7},{7,6},{8,9},{9,8},{10,11... | collective-permute-start | bytes 1572872 | tf_op jit(solution)/shard_map/ppermute | solution.py:97
  300.1 11.7 %collective-permute-start.9 = (bf16[128,512]{0,1:T(8,128)(2,1)S(1)}, bf16[128,512]{0,1:T(8,128)(2,1)S(1)}, u32[]{:S(2)}, u32[]{:S(2)}) collective-permute-start(bf16[128,512]{0,1:T(8,128)(2,1)S(1)} %get-tuple-element.38), channel_id=1, source_target_pairs={{0,6},{2,0},{4,2},{6,4},{1,7},{3,1},{5,3},{7,5},{8,14},{10,8},{12,... | collective-permute-start | bytes 393224 | tf_op jit(solution)/shard_map/ppermute | solution.py:101
  304.8 9.5 %collective-permute-start.8 = (bf16[128,512]{0,1:T(8,128)(2,1)S(1)}, bf16[128,512]{0,1:T(8,128)(2,1)S(1)}, u32[]{:S(2)}, u32[]{:S(2)}) collective-permute-start(bf16[128,512]{0,1:T(8,128)(2,1)S(1)} %get-tuple-element.39), channel_id=1, source_target_pairs={{0,4},{2,6},{4,0},{6,2},{1,5},{3,7},{5,1},{7,3},{8,12},{10,14},{12... | collective-permute-start | bytes 393224 | tf_op jit(solution)/shard_map/ppermute | solution.py:101
  307.5 8.6 %collective-permute-start.7 = (bf16[128,512]{0,1:T(8,128)(2,1)S(1)}, bf16[128,512]{0,1:T(8,128)(2,1)S(1)}, u32[]{:S(2)}, u32[]{:S(2)}) collective-permute-start(bf16[128,512]{0,1:T(8,128)(2,1)S(1)} %get-tuple-element.37), channel_id=1, source_target_pairs={{0,2},{2,4},{4,6},{6,0},{1,3},{3,5},{5,7},{7,1},{8,10},{10,12},{12... | collective-permute-start | bytes 393224 | tf_op jit(solution)/shard_map/ppermute | solution.py:101
Sparse Core Ops, SparseCore 0:
  12.1 80.3 all-gather.2
  157.8 66.8 all-gather.4

commit v5 on v4

--- a/solution.py
+++ b/solution.py
@@ -122,42 +122,41 @@
         doc_index, in_doc, doc_ends = doc_layout(row_map, doc_lengths)
 
         qkv_cols = q_cols + 2 * kv_cols
-        pos_row = jnp.concatenate(
-            [
-                (row_map // RUN).astype(jnp.bfloat16),
-                (row_map % RUN).astype(jnp.bfloat16),
-                jnp.zeros((qkv_cols - 2 * tok_rows,), jnp.bfloat16),
-            ]
-        )[None, :]
-        pad_rows = -(d_rows + 1) % 8
         out_cols = w_out.shape[0]
-        buf = jnp.concatenate(
-            [
-                jnp.concatenate([w_query, w_key, w_value, w_out.T], axis=1),
-                jnp.pad(pos_row, ((0, pad_rows), (0, out_cols))),
-            ],
-            axis=0,
-        )
-        blk_rows = buf.shape[0]
-        w_z = gather_z(buf)
-        w_qkv = gather_pair(w_z[:, :qkv_cols]).reshape(nctx, blk_rows, qkv_cols)
-        w_o = gather_pair(w_z[:, qkv_cols:]).reshape(nctx, blk_rows, out_cols)[:, :d_rows]
-        pos_code = w_qkv[:, d_rows, : 2 * tok_rows].astype(jnp.int32)
-        key_pos_all = pos_code[:, :tok_rows] * RUN + pos_code[:, tok_rows:]
-
-        normed_g = to_gathered_order(normed.reshape(tok_rows, nctx, d_rows), sizes)
-        normed_g = jnp.pad(normed_g, ((0, 0), (0, 0), (0, blk_rows - d_rows)))
-        proj = jnp.einsum(
-            "tjd,jdn->tn", normed_g, w_qkv, preferred_element_type=jnp.float32,
-        )
+        w_z = gather_z(jnp.concatenate([w_query, w_key, w_value, w_out.T], axis=1))
+        w_o = gather_pair(w_z[:, qkv_cols:]).reshape(nctx, d_rows, out_cols)
+        w_proj = w_z[:, :qkv_cols]
+
+        pair = ("xh", "c")
+        npair = nxh * nc
+        me = lax.axis_index("xh") * nc + lax.axis_index("c")
+        quarters = jnp.transpose(
+            normed.reshape(tok_rows, nz, nxh, nc, d_rows), (0, 2, 3, 1, 4)
+        ).reshape(tok_rows, npair, nz * d_rows)
+        proj = jnp.dot(
+            jnp.take(quarters, me, axis=1), w_proj, preferred_element_type=jnp.float32
+        )
+        for flip in range(1, npair):
+            perm = [(i, i ^ flip) for i in range(npair)]
+            theirs = lax.ppermute(jnp.take(quarters, me ^ flip, axis=1), pair, perm)
+            part = jnp.dot(theirs, w_proj, preferred_element_type=jnp.float32)
+            proj = proj + lax.ppermute(part, pair, perm)
         queries = proj[:, :q_cols].reshape(tok_rows, group_size, HEAD_DIM)
         key_proj = proj[:, q_cols : q_cols + kv_cols]
         value_proj = proj[:, q_cols + kv_cols :].astype(jnp.bfloat16)
         queries = rotate(queries, in_doc).astype(jnp.bfloat16)
         key_proj = rotate(key_proj, in_doc).astype(jnp.bfloat16)
 
-        kv = gather_pair(gather_z(jnp.concatenate([key_proj, value_proj], axis=1)))
-        kv_halves = kv.reshape(total_runs, RUN, 2 * kv_cols)
+        assert 2 * tok_rows == 2 * kv_cols
+        pos_row = jnp.concatenate([row_map // RUN, row_map % RUN]).astype(jnp.bfloat16)[None, :]
+        kv_buf = jnp.concatenate(
+            [jnp.concatenate([key_proj, value_proj], axis=1), jnp.pad(pos_row, ((0, 7), (0, 0)))],
+            axis=0,
+        )
+        kv = gather_pair(gather_z(kv_buf)).reshape(nctx, tok_rows + 8, 2 * kv_cols)
+        pos_code = kv[:, tok_rows, :].astype(jnp.int32)
+        key_pos_all = pos_code[:, :tok_rows] * RUN + pos_code[:, tok_rows:]
+        kv_halves = kv[:, :tok_rows].reshape(total_runs, RUN, 2 * kv_cols)
         pos_halves = key_pos_all.reshape(total_runs, RUN)
         run_of_half = pos_halves[:, 0] // RUN
         half_of_run = jnp.zeros((total_runs,), jnp.int32).at[run_of_half].set(

time: 366 us -> 349 us (0.954)
  waiting for transfers between devices: 207 us -> 171 us
  starting transfers between devices: 29 us -> 42.8 us
  matrix products: 10.5 us -> 21 us
  local copies, waits for them, and re-layouts: 29 us -> 23.9 us
    ppermute x6 -> x4, waiting for transfers between devices: 67.3 us -> 12.7 us  [swap_cat(): return jnp.concatenate([x, lax.ppermute(x, axis_name, [(0, 1), (1, 0)])], 0)]
    ppermute x0 -> x6, starting transfers between devices: none -> 18.1 us  [the longest x3 9.09 us: local(): theirs = lax.ppermute(jnp.take(quarters, me ^ flip, axis=1), pair, perm)]
    ppermute x0 -> x6, waiting for transfers between devices: none -> 11.2 us  [the longest x3 11.2 us: local(): proj = proj + lax.ppermute(part, pair, perm)]
    dot_general x1 -> x4, matrix products: 1.15 us -> 10.7 us  [the longest x3 8.54 us: local(): part = jnp.dot(theirs, w_proj, preferred_element_type=jnp.float32)]
    all_gather x2, waiting for transfers between devices: 122 us -> 130 us  [gather_z(): return lax.all_gather(x, 'z', axis=0, tiled=True)]
    gather x3 -> x0, local copies, waits for them, and re-layouts: 5.01 us -> none  [to_gathered_order(): y = jnp.take(jnp.take(y, c_idx, axis=1), xh_idx, axis=2)]
    ppermute x6 -> x4, starting transfers between devices: 16 us -> 11 us  [swap_cat(): return jnp.concatenate([x, lax.ppermute(x, axis_name, [(0, 1), (1, 0)])], 0)]
    concatenate x6 -> x4, other arithmetic: 16.5 us -> 19.3 us  [swap_cat(): return jnp.concatenate([x, lax.ppermute(x, axis_name, [(0, 1), (1, 0)])], 0)]
  transfers between devices with their start and end apart: 12 -> 16, of which waited for: 8 -> 7; matrix products, arithmetic and copies ran while one was open for 10% -> 9% of each run, Pallas kernels for 0% -> 0%
where the time goes in v5:
time: 349 us; the launch traced here: 348 us
  waiting for transfers between devices  171 us (49%)
  starting transfers between devices  42.8 us (12%)
  blocking collectives  38.2 us (11%)
  other arithmetic  35.9 us (10%)
  local copies, waits for them, and re-layouts  23.9 us (7%)
  matrix products  21 us (6%)
  between operations  15.5 us (4%)
    all_gather x2, waiting for transfers between devices, gather_z(): return lax.all_gather(x, 'z', axis=0, tiled=True)  130 us
    psum x3, blocking collectives, local(): sums = lax.psum(sums, axis)  38.2 us
    concatenate x4, other arithmetic, swap_cat(): return jnp.concatenate([x, lax.ppermute(x, axis_name, [(0, 1), (1, 0)])], 0)  19.3 us
    ppermute x1, waiting for transfers between devices, reduce_scatter_head(): lax.ppermute(sent, 'xl', [(0, 1), (1, 0)]).astype(jnp.float32)  14.2 us
    ppermute x4, waiting for transfers between devices, swap_cat(): return jnp.concatenate([x, lax.ppermute(x, axis_name, [(0, 1), (1, 0)])], 0)  12.7 us
    ppermute x3, starting transfers between devices, reduce_scatter_head(): lax.ppermute(piece, 'y', [(i, (i + shift) % ny) for i in range(ny)])  11.4 us
    ppermute x3, waiting for transfers between devices, local(): proj = proj + lax.ppermute(part, pair, perm)  11.2 us
    ppermute x4, starting transfers between devices, swap_cat(): return jnp.concatenate([x, lax.ppermute(x, axis_name, [(0, 1), (1, 0)])], 0)  11 us
  transfers between devices with their start and end apart: 16, of which 7 were waited for; matrix products, arithmetic and copies ran while one was open for 9% of the time, Pallas kernels for 0%

profile of v5, /device:TPU:6, one launch (start us, length us, event | category | flops | bytes accessed | tf_op | source)
XLA Modules:
  0.0 347.9 jit_solution(17918508273790234646)
XLA Ops:
  14.3 3.3 collective-permute-start.2
  17.7 3.9 %collective-permute-start.4 = (bf16[128,1024]{1,0:T(8,128)(2,1)S(1)}, bf16[128,1024]{1,0:T(8,128)(2,1)}, u32[]{:S(2)}, u32[]{:S(2)}) collective-permute-start(bf16[128,1024]{1,0:T(8,128)(2,1)S(1)} %bitcast.123), channel_id=1, source_target_pairs={{0,24},{8,16},{16,8},{24,0},{1,25},{9,17},{17,9},{25,1},{2,26},{10... | collective-permute-start | bytes 786440 | tf_op jit(solution)/shard_map/ppermute | solution.py:141
  22.6 66.9 %all-gather.3.cloned.1.call-done = bf16[1024,1280]{1,0:T(8,128)(2,1)} async-done(((bf16[64,1280]{1,0:T(8,128)(2,1)}), bf16[1024,1280]{1,0:T(8,128)(2,1)}) %all-gather.3.cloned.1.call-update) | async-done | bytes 2621456 | tf_op jit(solution)/shard_map/all_gather | solution.py:59
  89.5 3.1 fusion.26
  94.5 3.0 fusion.24
  97.5 3.4 collective-permute-start.3
  103.3 3.8 %collective-permute-start.5 = (f32[128,768]{0,1:T(8,128)}, f32[128,768]{0,1:T(8,128)S(1)}, u32[]{:S(2)}, u32[]{:S(2)}) collective-permute-start(f32[128,768]{0,1:T(8,128)} %fusion.22), channel_id=1, source_target_pairs={{0,24},{8,16},{16,8},{24,0},{1,25},{9,17},{17,9},{25,1},{2,26},{10... | collective-permute-start | bytes 1179656 | tf_op jit(solution)/shard_map/ppermute | solution.py:143
  109.4 3.6 %collective-permute-done.3 = f32[128,768]{0,1:T(8,128)S(1)} collective-permute-done((f32[128,768]{0,1:T(8,128)}, f32[128,768]{0,1:T(8,128)S(1)}, u32[]{:S(2)}, u32[]{:S(2)}) %collective-permute-start.3) | collective-permute-done | bytes 393248 | tf_op jit(solution)/shard_map/ppermute | solution.py:143
  113.0 7.6 %collective-permute-done.5 = f32[128,768]{0,1:T(8,128)S(1)} collective-permute-done((f32[128,768]{0,1:T(8,128)}, f32[128,768]{0,1:T(8,128)S(1)}, u32[]{:S(2)}, u32[]{:S(2)}) %collective-permute-start.5) | collective-permute-done | bytes 393248 | tf_op jit(solution)/shard_map/ppermute | solution.py:143
  124.4 3.4 collective-permute-start.8
  127.8 63.6 %all-gather.5.cloned.1.call-done = bf16[2176,256]{1,0:T(8,128)(2,1)} async-done(((bf16[136,256]{1,0:T(8,128)(2,1)}), bf16[2176,256]{1,0:T(8,128)(2,1)}) %all-gather.5.cloned.1.call-update) | async-done | bytes 1114128 | tf_op jit(solution)/shard_map/all_gather | solution.py:59
  191.4 3.5 collective-permute-start.6
  199.6 12.7 %collective-permute-done.6 = bf16[2176,256]{1,0:T(8,128)(2,1)S(1)} collective-permute-done((bf16[2176,256]{1,0:T(8,128)(2,1)}, bf16[2176,256]{1,0:T(8,128)(2,1)S(1)}, u32[]{:S(2)}, u32[]{:S(2)}) %collective-permute-start.6) | collective-permute-done | bytes 1114144 | tf_op jit(solution)/shard_map/ppermute | solution.py:55
  222.1 3.6 %pad_maximum_fusion.1 = bf16[4096,512]{1,0:T(8,128)(2,1)} fusion(bf16[2048,512]{1,0:T(8,128)(2,1)} %collective-permute-done.9, bf16[1024,512]{1,0:T(8,128)(2,1)} %collective-permute-done.8, bf16[1024,512]{1,0:T(8,128)(2,1)S(1)} %slice.129), kind=kLoop, calls=%fused_computation.14 | loop fusion | flops 12582912 | bytes 8388608 | tf_op jit(solution)/shard_map/concatenate | solution.py:55
  225.7 11.3 %pad_maximum_fusion = bf16[8704,256]{1,0:T(8,128)(2,1)S(1)} fusion(bf16[4352,256]{1,0:T(8,128)(2,1)} %collective-permute-done.7, bf16[2176,256]{1,0:T(8,128)(2,1)S(1)} %copy-done.2, bf16[2176,256]{1,0:T(8,128)(2,1)S(1)} %copy-done), kind=kLoop, calls=%fused_computation.13 | loop fusion | flops 13369344 | bytes 8912896 | tf_op jit(solution)/shard_map/concatenate | solution.py:55
  246.3 4.5 %fusion.66 = (f32[2,4,64]{2,1,0:T(4,128)S(1)}, bf16[2,4,64,2112]{3,2,1,0:T(8,128)(2,1)}) fusion(pred[2,64,2112]{2,1,0:T(8,128)(4,1)S(1)} %compare_and_fusion, bf16[2,2112,256]{2,1,0:T(8,128)(2,1)S(1)} %bitcast.120, bf16[2,64,4,64]{3,1,2,0:T(8,128)(2,1)} %copy.107, bf16[2,64,4,64]{3,1,2,0:T(8,128)(2,1)} %copy.106), kind=kOutput, calls=%fused_computation.145 | convolution fusion | flops 283576384 | bytes 3934208 | tf_op jit(solution)/shard_map/sub | solution.py:187
  253.4 3.4 fusion.42
  258.9 3.3 select_bitcast_fusion.1
  268.3 14.2 %collective-permute-done.10 = bf16[128,4,512]{0,2,1:T(8,128)(2,1)} collective-permute-done((bf16[128,4,512]{0,2,1:T(8,128)(2,1)}, bf16[128,4,512]{0,2,1:T(8,128)(2,1)}, u32[]{:S(2)}, u32[]{:S(2)}) %collective-permute-start.10) | collective-permute-done | bytes 524320 | tf_op jit(solution)/shard_map/ppermute | solution.py:97
  284.7 3.4 collective-permute-start.11
  288.1 4.6 %collective-permute-start.12 = (bf16[128,512]{0,1:T(8,128)(2,1)S(1)}, bf16[128,512]{0,1:T(8,128)(2,1)S(1)}, u32[]{:S(2)}, u32[]{:S(2)}) collective-permute-start(bf16[128,512]{0,1:T(8,128)(2,1)S(1)} %get-tuple-element.55), channel_id=1, source_target_pairs={{0,4},{2,6},{4,0},{6,2},{1,5},{3,7},{5,1},{7,3},{8,12},{10,14},{12... | collective-permute-start | bytes 393224 | tf_op jit(solution)/shard_map/ppermute | solution.py:101
  292.8 3.3 collective-permute-start.13
  303.3 6.4 %psum.22 = f32[2,512]{1,0:T(2,128)S(1)} all-reduce(f32[2,512]{1,0:T(2,128)S(1)} %psum.21), channel_id=1, replica_groups=mesh['z'=16,'xh'=2,'c'=2,'y'=4,'xl'=2] {'xh'}, use_global_device_ids=true, to_apply=%region_12.16 | all-reduce | flops 1024 | bytes 8192 | tf_op jit(solution)/shard_map/psum | solution.py:220
  309.7 29.3 %psum.23 = f32[2,512]{1,0:T(2,128)S(1)} all-reduce(f32[2,512]{1,0:T(2,128)S(1)} %psum.22), channel_id=1, replica_groups=mesh['z'=16,'xh'=2,'c'=2,'y'=4,'xl'=2] {'z'}, use_global_device_ids=true, to_apply=%region_13.17 | all-reduce | flops 1024 | bytes 8192 | tf_op jit(solution)/shard_map/psum | solution.py:220
  (131 shorter events, 63.4 us)
Async XLA Ops:
  7.2 82.3 %all-gather.3.cloned.1.call-start = ((), (), s32[]{:S(2)}) async-start(), calls=%async_computation | async-start | bytes 2785280 | tf_op jit(solution)/shard_map/all_gather | solution.py:59
  8.8 182.6 %all-gather.5.cloned.1.call-start = ((), (), s32[]{:S(2)}) async-start(), calls=%async_computation.1 | async-start | bytes 1183744 | tf_op jit(solution)/shard_map/all_gather | solution.py:59
  11.8 9.8 %copy-start.9 = (s32[32]{0:T(128)S(1)}, s32[32]{0:T(128)}, u32[]{:S(2)}) copy-start(s32[32]{0:T(128)} %param.22) | copy-start | bytes 388
  11.8 10.0 %copy-start.10 = (s32[128]{0:T(128)S(1)}, s32[128]{0:T(128)}, u32[]{:S(2)}) copy-start(s32[128]{0:T(128)} %param.21) | copy-start | bytes 1540
  12.2 10.4 %collective-permute-start = (bf16[128,1024]{1,0:T(8,128)(2,1)S(1)}, bf16[128,1024]{1,0:T(8,128)(2,1)}, u32[]{:S(2)}, u32[]{:S(2)}) collective-permute-start(bf16[128,1024]{1,0:T(8,128)(2,1)S(1)} %bitcast.125), channel_id=1, source_target_pairs={{0,8},{8,0},{16,24},{24,16},{1,9},{9,1},{17,25},{25,17},{2,10},{10... | collective-permute-start | bytes 786440 | tf_op jit(solution)/shard_map/ppermute | solution.py:141
  14.3 80.2 %collective-permute-start.2 = (bf16[128,1024]{1,0:T(8,128)(2,1)S(1)}, bf16[128,1024]{1,0:T(8,128)(2,1)}, u32[]{:S(2)}, u32[]{:S(2)}) collective-permute-start(bf16[128,1024]{1,0:T(8,128)(2,1)S(1)} %bitcast.124), channel_id=1, source_target_pairs={{0,16},{8,24},{16,0},{24,8},{1,17},{9,25},{17,1},{25,9},{2,18},{10... | collective-permute-start | bytes 786440 | tf_op jit(solution)/shard_map/ppermute | solution.py:141
  17.7 83.1 %collective-permute-start.4 = (bf16[128,1024]{1,0:T(8,128)(2,1)S(1)}, bf16[128,1024]{1,0:T(8,128)(2,1)}, u32[]{:S(2)}, u32[]{:S(2)}) collective-permute-start(bf16[128,1024]{1,0:T(8,128)(2,1)S(1)} %bitcast.123), channel_id=1, source_target_pairs={{0,24},{8,16},{16,8},{24,0},{1,25},{9,17},{17,9},{25,1},{2,26},{10... | collective-permute-start | bytes 786440 | tf_op jit(solution)/shard_map/ppermute | solution.py:141
  89.5 11.4 %copy-start.5 = (bf16[1024,1280]{1,0:T(8,128)(2,1)S(1)}, bf16[1024,1280]{1,0:T(8,128)(2,1)}, u32[]{:S(2)}) copy-start(bf16[1024,1280]{1,0:T(8,128)(2,1)} %all-gather.3.cloned.1.call-done) | copy-start | bytes 7864324
  92.6 16.9 %collective-permute-start.1 = (f32[128,768]{0,1:T(8,128)}, f32[128,768]{0,1:T(8,128)S(1)}, u32[]{:S(2)}, u32[]{:S(2)}) collective-permute-start(f32[128,768]{0,1:T(8,128)} %fusion.26), channel_id=1, source_target_pairs={{0,8},{8,0},{16,24},{24,16},{1,9},{9,1},{17,25},{25,17},{2,10},{10... | collective-permute-start | bytes 1179656 | tf_op jit(solution)/shard_map/ppermute | solution.py:143
  97.5 15.5 %collective-permute-start.3 = (f32[128,768]{0,1:T(8,128)}, f32[128,768]{0,1:T(8,128)S(1)}, u32[]{:S(2)}, u32[]{:S(2)}) collective-permute-start(f32[128,768]{0,1:T(8,128)} %fusion.24), channel_id=1, source_target_pairs={{0,16},{8,24},{16,0},{24,8},{1,17},{9,25},{17,1},{25,9},{2,18},{10... | collective-permute-start | bytes 1179656 | tf_op jit(solution)/shard_map/ppermute | solution.py:143
  103.3 17.3 %collective-permute-start.5 = (f32[128,768]{0,1:T(8,128)}, f32[128,768]{0,1:T(8,128)S(1)}, u32[]{:S(2)}, u32[]{:S(2)}) collective-permute-start(f32[128,768]{0,1:T(8,128)} %fusion.22), channel_id=1, source_target_pairs={{0,24},{8,16},{16,8},{24,0},{1,25},{9,17},{17,9},{25,1},{2,26},{10... | collective-permute-start | bytes 1179656 | tf_op jit(solution)/shard_map/ppermute | solution.py:143
  124.4 70.5 %collective-permute-start.8 = (bf16[1024,512]{1,0:T(8,128)(2,1)S(1)}, bf16[1024,512]{1,0:T(8,128)(2,1)}, u32[]{:S(2)}, u32[]{:S(2)}) collective-permute-start(bf16[1024,512]{1,0:T(8,128)(2,1)S(1)} %slice.129), channel_id=1, source_target_pairs={{0,16},{16,0},{1,17},{17,1},{2,18},{18,2},{3,19},{19,3},{4,20},{20... | collective-permute-start | bytes 3145736 | tf_op jit(solution)/shard_map/ppermute | solution.py:55
  191.4 20.9 %copy-start = (bf16[2176,256]{1,0:T(8,128)(2,1)S(1)}, bf16[2176,256]{1,0:T(8,128)(2,1)}, u32[]{:S(2)}) copy-start(bf16[2176,256]{1,0:T(8,128)(2,1)} %all-gather.5.cloned.1.call-done) | copy-start | bytes 3342340
  191.4 20.9 %collective-permute-start.6 = (bf16[2176,256]{1,0:T(8,128)(2,1)}, bf16[2176,256]{1,0:T(8,128)(2,1)S(1)}, u32[]{:S(2)}, u32[]{:S(2)}) collective-permute-start(bf16[2176,256]{1,0:T(8,128)(2,1)} %all-gather.5.cloned.1.call-done), channel_id=1, source_target_pairs={{0,16},{16,0},{1,17},{17,1},{2,18},{18,2},{3,19},{19,3},{4,20},{20... | collective-permute-start | bytes 3342344 | tf_op jit(solution)/shard_map/ppermute | solution.py:55
  197.6 20.4 %slice-start = ((f32[128,768]{0,1:T(8,128)}), f32[128,512]{0,1:T(8,128)S(1)}, s32[]{:S(2)}) async-start(f32[128,768]{0,1:T(8,128)} %copy-done.4), calls=%async_computation.2 | async-start | bytes 524288 | tf_op jit(solution)/shard_map/slice | solution.py:144
  197.6 24.5 %collective-permute-start.9 = (bf16[2048,512]{1,0:T(8,128)(2,1)}, bf16[2048,512]{1,0:T(8,128)(2,1)}, u32[]{:S(2)}, u32[]{:S(2)}) collective-permute-start(bf16[2048,512]{1,0:T(8,128)(2,1)} %pad_maximum_fusion.3), channel_id=1, source_target_pairs={{0,8},{8,0},{1,9},{9,1},{2,10},{10,2},{3,11},{11,3},{4,12},{12,4},... | collective-permute-start | bytes 6291464 | tf_op jit(solution)/shard_map/ppermute | solution.py:55
  214.1 11.6 %collective-permute-start.7 = (bf16[4352,256]{1,0:T(8,128)(2,1)}, bf16[4352,256]{1,0:T(8,128)(2,1)}, u32[]{:S(2)}, u32[]{:S(2)}) collective-permute-start(bf16[4352,256]{1,0:T(8,128)(2,1)} %pad_maximum_fusion.2), channel_id=1, source_target_pairs={{0,8},{8,0},{1,9},{9,1},{2,10},{10,2},{3,11},{11,3},{4,12},{12,4},... | collective-permute-start | bytes 6684680 | tf_op jit(solution)/shard_map/ppermute | solution.py:55
  265.0 31.1 %copy-start.14 = (s32[32]{0:T(128)S(1)}, s32[32]{0:T(128)}, u32[]{:S(2)}) copy-start(s32[32]{0:T(128)} %param.23) | copy-start | bytes 388
  265.0 32.4 %copy-start.11 = (s32[128]{0:T(128)S(1)}, s32[128]{0:T(128)}, u32[]{:S(2)}) copy-start(s32[128]{0:T(128)} %param.21) | copy-start | bytes 1540
  265.1 32.4 %copy-start.12 = (s32[32]{0:T(128)S(1)}, s32[32]{0:T(128)}, u32[]{:S(2)}) copy-start(s32[32]{0:T(128)} %get-tuple-element.73) | copy-start | bytes 388
  266.0 16.5 %collective-permute-start.10 = (bf16[128,4,512]{0,2,1:T(8,128)(2,1)}, bf16[128,4,512]{0,2,1:T(8,128)(2,1)}, u32[]{:S(2)}, u32[]{:S(2)}) collective-permute-start(bf16[128,4,512]{0,2,1:T(8,128)(2,1)} %bitcast_convert_fusion), channel_id=1, source_target_pairs={{0,1},{1,0},{2,3},{3,2},{4,5},{5,4},{6,7},{7,6},{8,9},{9,8},{10,11... | collective-permute-start | bytes 1572872 | tf_op jit(solution)/shard_map/ppermute | solution.py:97
  284.7 12.9 %collective-permute-start.11 = (bf16[128,512]{0,1:T(8,128)(2,1)S(1)}, bf16[128,512]{0,1:T(8,128)(2,1)S(1)}, u32[]{:S(2)}, u32[]{:S(2)}) collective-permute-start(bf16[128,512]{0,1:T(8,128)(2,1)S(1)} %get-tuple-element.53), channel_id=1, source_target_pairs={{0,2},{2,4},{4,6},{6,0},{1,3},{3,5},{5,7},{7,1},{8,10},{10,12},{12... | collective-permute-start | bytes 393224 | tf_op jit(solution)/shard_map/ppermute | solution.py:101
  288.1 9.5 %collective-permute-start.12 = (bf16[128,512]{0,1:T(8,128)(2,1)S(1)}, bf16[128,512]{0,1:T(8,128)(2,1)S(1)}, u32[]{:S(2)}, u32[]{:S(2)}) collective-permute-start(bf16[128,512]{0,1:T(8,128)(2,1)S(1)} %get-tuple-element.55), channel_id=1, source_target_pairs={{0,4},{2,6},{4,0},{6,2},{1,5},{3,7},{5,1},{7,3},{8,12},{10,14},{12... | collective-permute-start | bytes 393224 | tf_op jit(solution)/shard_map/ppermute | solution.py:101
  292.8 6.9 %collective-permute-start.13 = (bf16[128,512]{0,1:T(8,128)(2,1)S(1)}, bf16[128,512]{0,1:T(8,128)(2,1)S(1)}, u32[]{:S(2)}, u32[]{:S(2)}) collective-permute-start(bf16[128,512]{0,1:T(8,128)(2,1)S(1)} %get-tuple-element.54), channel_id=1, source_target_pairs={{0,6},{2,0},{4,2},{6,4},{1,7},{3,1},{5,3},{7,5},{8,14},{10,8},{12,... | collective-permute-start | bytes 393224 | tf_op jit(solution)/shard_map/ppermute | solution.py:101
  (8 other events, 18.4 us)
Sparse Core Ops, SparseCore 0:
  10.1 79.3 all-gather.2
  123.2 68.1 all-gather.4

commit v6 on v5

--- a/solution.py
+++ b/solution.py
@@ -153,10 +153,14 @@
             [jnp.concatenate([key_proj, value_proj], axis=1), jnp.pad(pos_row, ((0, 7), (0, 0)))],
             axis=0,
         )
-        kv = gather_pair(gather_z(kv_buf)).reshape(nctx, tok_rows + 8, 2 * kv_cols)
-        pos_code = kv[:, tok_rows, :].astype(jnp.int32)
+        kv_z = gather_z(kv_buf)
+        kv_zx = (kv_z, lax.ppermute(kv_z, "xh", [(0, 1), (1, 0)]))
+        kv_pieces = kv_zx + tuple(lax.ppermute(kv_zx, "c", [(0, 1), (1, 0)]))
+        blk_rows = tok_rows + 8
+        pos_code = jnp.concatenate(
+            [p.reshape(nz, blk_rows, 2 * kv_cols)[:, tok_rows, :] for p in kv_pieces]
+        ).astype(jnp.int32)
         key_pos_all = pos_code[:, :tok_rows] * RUN + pos_code[:, tok_rows:]
-        kv_halves = kv[:, :tok_rows].reshape(total_runs, RUN, 2 * kv_cols)
         pos_halves = key_pos_all.reshape(total_runs, RUN)
         run_of_half = pos_halves[:, 0] // RUN
         half_of_run = jnp.zeros((total_runs,), jnp.int32).at[run_of_half].set(
@@ -169,7 +173,16 @@
         first_run = jnp.maximum(q_run - (win_runs - 1), 0)
         win = first_run[:, None] + jnp.arange(win_runs, dtype=jnp.int32)[None, :]
         win_halves = half_of_run[win]
-        kv_win = kv_halves[win_halves].reshape(runs_here, win_runs * RUN, 2 * kv_cols)
+        units = blk_rows // 8
+        half_block = win_halves // 2
+        piece_of = half_block // nz
+        unit0 = (half_block % nz) * units + (win_halves % 2) * (RUN // 8)
+        unit_idx = unit0[..., None] + jnp.arange(RUN // 8, dtype=jnp.int32)
+        kv_win = None
+        for p, piece in enumerate(kv_pieces):
+            got = piece.reshape(nz * units, 8, 2 * kv_cols)[unit_idx]
+            kv_win = got if kv_win is None else jnp.where((piece_of == p)[..., None, None, None], got, kv_win)
+        kv_win = kv_win.reshape(runs_here, win_runs * RUN, 2 * kv_cols)
         k_pos = pos_halves[win_halves].reshape(runs_here, win_runs * RUN)
         k_win = kv_win[..., :kv_cols]
         v_win = kv_win[..., kv_cols:]

time: 349 us -> 358 us (1.026)
  local copies, waits for them, and re-layouts: 23.9 us -> 38.5 us
  other arithmetic: 35.9 us -> 29.9 us
    all_gather x2, waiting for transfers between devices: 130 us -> 101 us  [gather_z(): return lax.all_gather(x, 'z', axis=0, tiled=True)]
    concatenate x4 -> x2, other arithmetic: 19.3 us -> 4.99 us  [swap_cat(): return jnp.concatenate([x, lax.ppermute(x, axis_name, [(0, 1), (1, 0)])], 0)]
    ppermute x0 -> x3, waiting for transfers between devices: none -> 14.2 us  [the longest x1 14.2 us: local(): kv_zx = (kv_z, lax.ppermute(kv_z, 'xh', [(0, 1), (1, 0)]))]
    gather x1 -> x4, local copies, waits for them, and re-layouts: 2.89 us -> 15.5 us  [local(): got = piece.reshape(nz * units, 8, 2 * kv_cols)[unit_idx]]
    ppermute x4 -> x2, waiting for transfers between devices: 12.7 us -> 24.6 us  [swap_cat(): return jnp.concatenate([x, lax.ppermute(x, axis_name, [(0, 1), (1, 0)])], 0)]
    select_n x0 -> x2, other arithmetic: none -> 7.6 us  [the longest x1 7.53 us: local(): jnp.where((piece_of == p)[..., None, None, None], got, kv_win)]
    ppermute x0 -> x3, starting transfers between devices: none -> 7.07 us  [the longest x2 3.83 us: local(): kv_pieces = kv_zx + tuple(lax.ppermute(kv_zx, 'c', [(0, 1), (1, 0)]))]
    ppermute x4 -> x2, starting transfers between devices: 11 us -> 5.4 us  [swap_cat(): return jnp.concatenate([x, lax.ppermute(x, axis_name, [(0, 1), (1, 0)])], 0)]
  transfers between devices with their start and end apart: 16 -> 17, of which waited for: 7 -> 9; matrix products, arithmetic and copies ran while one was open for 9% -> 8% of each run, Pallas kernels for 0% -> 0%
where the time goes in v6:
time: 358 us; the launch traced here: 356 us
  waiting for transfers between devices  168 us (47%)
  starting transfers between devices  44.3 us (12%)
  local copies, waits for them, and re-layouts  38.5 us (11%)
  blocking collectives  38.1 us (11%)
  other arithmetic  29.9 us (8%)
  matrix products  21.4 us (6%)
  between operations  15.6 us (4%)
    all_gather x2, waiting for transfers between devices, gather_z(): return lax.all_gather(x, 'z', axis=0, tiled=True)  101 us
    psum x3, blocking collectives, local(): sums = lax.psum(sums, axis)  38.1 us
    ppermute x2, waiting for transfers between devices, swap_cat(): return jnp.concatenate([x, lax.ppermute(x, axis_name, [(0, 1), (1, 0)])], 0)  24.6 us
    gather x4, local copies, waits for them, and re-layouts, local(): got = piece.reshape(nz * units, 8, 2 * kv_cols)[unit_idx]  15.5 us
    ppermute x1, waiting for transfers between devices, local(): kv_zx = (kv_z, lax.ppermute(kv_z, 'xh', [(0, 1), (1, 0)]))  14.2 us
    ppermute x1, waiting for transfers between devices, reduce_scatter_head(): lax.ppermute(sent, 'xl', [(0, 1), (1, 0)]).astype(jnp.float32)  14.2 us
    ppermute x3, waiting for transfers between devices, local(): proj = proj + lax.ppermute(part, pair, perm)  11.2 us
    ppermute x3, starting transfers between devices, reduce_scatter_head(): lax.ppermute(piece, 'y', [(i, (i + shift) % ny) for i in range(ny)])  10.8 us
  transfers between devices with their start and end apart: 17, of which 9 were waited for; matrix products, arithmetic and copies ran while one was open for 8% of the time, Pallas kernels for 0%

profile of v6, /device:TPU:6, one launch (start us, length us, event | category | flops | bytes accessed | tf_op | source)
XLA Modules:
  0.0 356.1 jit_solution(3811357441294643253)
XLA Ops:
  12.2 3.3 collective-permute-start.2
  23.2 66.3 %all-gather.3.cloned.1.call-done = bf16[1024,1280]{1,0:T(8,128)(2,1)} async-done(((bf16[64,1280]{1,0:T(8,128)(2,1)}), bf16[1024,1280]{1,0:T(8,128)(2,1)}) %all-gather.3.cloned.1.call-update) | async-done | bytes 2621456 | tf_op jit(solution)/shard_map/all_gather | solution.py:59
  97.5 3.4 collective-permute-start.5
  103.4 4.0 %collective-permute-start.3 = (f32[128,768]{0,1:T(8,128)}, f32[128,768]{0,1:T(8,128)S(1)}, u32[]{:S(2)}, u32[]{:S(2)}) collective-permute-start(f32[128,768]{0,1:T(8,128)} %fusion.26), channel_id=1, source_target_pairs={{0,16},{8,24},{16,0},{24,8},{1,17},{9,25},{17,1},{25,9},{2,18},{10... | collective-permute-start | bytes 1179656 | tf_op jit(solution)/shard_map/ppermute | solution.py:143
  111.9 9.1 %collective-permute-done.3 = f32[128,768]{0,1:T(8,128)S(1)} collective-permute-done((f32[128,768]{0,1:T(8,128)}, f32[128,768]{0,1:T(8,128)S(1)}, u32[]{:S(2)}, u32[]{:S(2)}) %collective-permute-start.3) | collective-permute-done | bytes 393248 | tf_op jit(solution)/shard_map/ppermute | solution.py:143
  124.7 3.5 collective-permute-start.9
  128.2 24.6 %collective-permute-done.9 = bf16[1024,512]{1,0:T(8,128)(2,1)S(1)} collective-permute-done((bf16[1024,512]{1,0:T(8,128)(2,1)S(1)}, bf16[1024,512]{1,0:T(8,128)(2,1)S(1)}, u32[]{:S(2)}, u32[]{:S(2)}) %collective-permute-start.9) | collective-permute-done | bytes 1048608 | tf_op jit(solution)/shard_map/ppermute | solution.py:55
  157.2 34.3 %all-gather.5.cloned.1.call-done = bf16[2176,256]{1,0:T(8,128)(2,1)} async-done(((bf16[136,256]{1,0:T(8,128)(2,1)}), bf16[2176,256]{1,0:T(8,128)(2,1)}) %all-gather.5.cloned.1.call-update) | async-done | bytes 1114128 | tf_op jit(solution)/shard_map/all_gather | solution.py:59
  191.5 3.2 collective-permute-start.6
  197.9 14.2 %collective-permute-done.6 = bf16[2176,256]{1,0:T(8,128)(2,1)S(1)} collective-permute-done((bf16[2176,256]{1,0:T(8,128)(2,1)}, bf16[2176,256]{1,0:T(8,128)(2,1)S(1)}, u32[]{:S(2)}, u32[]{:S(2)}) %collective-permute-start.6) | collective-permute-done | bytes 1114144 | tf_op jit(solution)/shard_map/ppermute | solution.py:157
  219.5 3.5 pad_maximum_fusion
  232.4 4.2 %gather_fusion.4 = bf16[528,8,256]{2,1,0:T(8,128)(2,1)} fusion(bf16[272,8,256]{2,1,0:T(8,128)(2,1)} %bitcast.156, s32[1024]{0:T(1024)S(1)} %pad_clamp_fusion.2), kind=kCustom, calls=%fused_computation.4 | custom fusion | bytes 4327488 | tf_op jit(solution)/shard_map/gather | solution.py:183
  236.6 4.3 %gather_fusion.3 = bf16[528,8,256]{2,1,0:T(8,128)(2,1)} fusion(bf16[272,8,256]{2,1,0:T(8,128)(2,1)} %bitcast.19, s32[1024]{0:T(1024)S(1)} %pad_clamp_fusion.2), kind=kCustom, calls=%fused_computation.3 | custom fusion | bytes 4327488 | tf_op jit(solution)/shard_map/gather | solution.py:183
  240.9 4.3 %gather_fusion.2 = bf16[528,8,256]{2,1,0:T(8,128)(2,1)} fusion(bf16[272,8,256]{2,1,0:T(8,128)(2,1)} %bitcast.17, s32[1024]{0:T(1024)S(1)} %pad_clamp_fusion.2), kind=kCustom, calls=%fused_computation.2 | custom fusion | bytes 4327488 | tf_op jit(solution)/shard_map/gather | solution.py:183
  246.1 7.5 %fusion.9 = bf16[2,2112,256]{2,1,0:T(8,128)(2,1)} fusion(pred[2,2112]{1,0:T(4,128)(4,1)S(1)} %broadcast_in_dim.170, pred[2,2112]{1,0:T(4,128)(4,1)S(1)} %broadcast_in_dim.167, pred[2,2112]{1,0:T(4,128)(4,1)S(1)} %broadcast_in_dim.164, bf16[2,2112,256]{2,1,0:T(8,128)(2,1)S(1)} %bitcast.147, bf16[2,2112,256]{2,1,0:T(8,128)(2,1)} %bitcast.148, ...), kind=kLoop, calls=%fused_computation.23 | loop fusion | flops 3244032 | bytes 10826112 | tf_op jit(solution)/shard_map/jit(_where)/select_n | solution.py:184
  253.6 5.0 %fusion.71 = (f32[2,4,64]{2,1,0:T(4,128)S(1)}, bf16[2,4,64,2112]{3,2,1,0:T(8,128)(2,1)}) fusion(pred[2,64,2112]{2,1,0:T(8,128)(4,1)S(1)} %compare_and_fusion, bf16[2,2112,256]{2,1,0:T(8,128)(2,1)} %fusion.9, bf16[2,64,4,64]{3,1,2,0:T(8,128)(2,1)} %copy.164, bf16[2,64,4,64]{3,1,2,0:T(8,128)(2,1)} %copy.163), kind=kOutput, calls=%fused_computation.174 | convolution fusion | flops 283576384 | bytes 4065280 | tf_op jit(solution)/shard_map/sub | solution.py:200
  261.2 3.4 fusion.44
  266.6 3.3 select_bitcast_fusion.1
  276.1 14.2 %collective-permute-done.11 = bf16[128,4,512]{0,2,1:T(8,128)(2,1)} collective-permute-done((bf16[128,4,512]{0,2,1:T(8,128)(2,1)}, bf16[128,4,512]{0,2,1:T(8,128)(2,1)}, u32[]{:S(2)}, u32[]{:S(2)}) %collective-permute-start.11) | collective-permute-done | bytes 524320 | tf_op jit(solution)/shard_map/ppermute | solution.py:97
  292.5 3.4 collective-permute-start.12
  295.9 3.7 %collective-permute-start.14 = (bf16[128,512]{0,1:T(8,128)(2,1)S(1)}, bf16[128,512]{0,1:T(8,128)(2,1)S(1)}, u32[]{:S(2)}, u32[]{:S(2)}) collective-permute-start(bf16[128,512]{0,1:T(8,128)(2,1)S(1)} %get-tuple-element.59), channel_id=1, source_target_pairs={{0,6},{2,0},{4,2},{6,4},{1,7},{3,1},{5,3},{7,5},{8,14},{10,8},{12,... | collective-permute-start | bytes 393224 | tf_op jit(solution)/shard_map/ppermute | solution.py:101
  299.6 3.7 %collective-permute-start.13 = (bf16[128,512]{0,1:T(8,128)(2,1)S(1)}, bf16[128,512]{0,1:T(8,128)(2,1)S(1)}, u32[]{:S(2)}, u32[]{:S(2)}) collective-permute-start(bf16[128,512]{0,1:T(8,128)(2,1)S(1)} %get-tuple-element.60), channel_id=1, source_target_pairs={{0,4},{2,6},{4,0},{6,2},{1,5},{3,7},{5,1},{7,3},{8,12},{10,14},{12... | collective-permute-start | bytes 393224 | tf_op jit(solution)/shard_map/ppermute | solution.py:101
  311.6 6.4 %psum.22 = f32[2,512]{1,0:T(2,128)S(1)} all-reduce(f32[2,512]{1,0:T(2,128)S(1)} %psum.21), channel_id=1, replica_groups=mesh['z'=16,'xh'=2,'c'=2,'y'=4,'xl'=2] {'xh'}, use_global_device_ids=true, to_apply=%region_12.16 | all-reduce | flops 1024 | bytes 8192 | tf_op jit(solution)/shard_map/psum | solution.py:233
  318.0 29.2 %psum.23 = f32[2,512]{1,0:T(2,128)S(1)} all-reduce(f32[2,512]{1,0:T(2,128)S(1)} %psum.22), channel_id=1, replica_groups=mesh['z'=16,'xh'=2,'c'=2,'y'=4,'xl'=2] {'z'}, use_global_device_ids=true, to_apply=%region_13.17 | all-reduce | flops 1024 | bytes 8192 | tf_op jit(solution)/shard_map/psum | solution.py:233
  (152 shorter events, 78.5 us)
Async XLA Ops:
  7.2 82.3 %all-gather.3.cloned.1.call-start = ((), (), s32[]{:S(2)}) async-start(), calls=%async_computation | async-start | bytes 2785280 | tf_op jit(solution)/shard_map/all_gather | solution.py:59
  8.8 182.7 %all-gather.5.cloned.1.call-start = ((), (), s32[]{:S(2)}) async-start(), calls=%async_computation.1 | async-start | bytes 1183744 | tf_op jit(solution)/shard_map/all_gather | solution.py:59
  12.2 88.8 %collective-permute-start.2 = (bf16[128,1024]{1,0:T(8,128)(2,1)S(1)}, bf16[128,1024]{1,0:T(8,128)(2,1)}, u32[]{:S(2)}, u32[]{:S(2)}) collective-permute-start(bf16[128,1024]{1,0:T(8,128)(2,1)S(1)} %bitcast.161), channel_id=1, source_target_pairs={{0,16},{8,24},{16,0},{24,8},{1,17},{9,25},{17,1},{25,9},{2,18},{10... | collective-permute-start | bytes 786440 | tf_op jit(solution)/shard_map/ppermute | solution.py:141
  15.7 78.9 %collective-permute-start.4 = (bf16[128,1024]{1,0:T(8,128)(2,1)S(1)}, bf16[128,1024]{1,0:T(8,128)(2,1)}, u32[]{:S(2)}, u32[]{:S(2)}) collective-permute-start(bf16[128,1024]{1,0:T(8,128)(2,1)S(1)} %bitcast.162), channel_id=1, source_target_pairs={{0,24},{8,16},{16,8},{24,0},{1,25},{9,17},{17,9},{25,1},{2,26},{10... | collective-permute-start | bytes 786440 | tf_op jit(solution)/shard_map/ppermute | solution.py:141
  19.0 4.1 %collective-permute-start = (bf16[128,1024]{1,0:T(8,128)(2,1)S(1)}, bf16[128,1024]{1,0:T(8,128)(2,1)}, u32[]{:S(2)}, u32[]{:S(2)}) collective-permute-start(bf16[128,1024]{1,0:T(8,128)(2,1)S(1)} %bitcast.163), channel_id=1, source_target_pairs={{0,8},{8,0},{16,24},{24,16},{1,9},{9,1},{17,25},{25,17},{2,10},{10... | collective-permute-start | bytes 786440 | tf_op jit(solution)/shard_map/ppermute | solution.py:141
  89.5 11.5 %copy-start.5 = (bf16[1024,1280]{1,0:T(8,128)(2,1)S(1)}, bf16[1024,1280]{1,0:T(8,128)(2,1)}, u32[]{:S(2)}) copy-start(bf16[1024,1280]{1,0:T(8,128)(2,1)} %all-gather.3.cloned.1.call-done) | copy-start | bytes 7864324
  92.6 17.1 %collective-permute-start.1 = (f32[128,768]{0,1:T(8,128)}, f32[128,768]{0,1:T(8,128)S(1)}, u32[]{:S(2)}, u32[]{:S(2)}) collective-permute-start(f32[128,768]{0,1:T(8,128)} %fusion.28), channel_id=1, source_target_pairs={{0,8},{8,0},{16,24},{24,16},{1,9},{9,1},{17,25},{25,17},{2,10},{10... | collective-permute-start | bytes 1179656 | tf_op jit(solution)/shard_map/ppermute | solution.py:143
  97.5 14.4 %collective-permute-start.5 = (f32[128,768]{0,1:T(8,128)}, f32[128,768]{0,1:T(8,128)S(1)}, u32[]{:S(2)}, u32[]{:S(2)}) collective-permute-start(f32[128,768]{0,1:T(8,128)} %fusion.24), channel_id=1, source_target_pairs={{0,24},{8,16},{16,8},{24,0},{1,25},{9,17},{17,9},{25,1},{2,26},{10... | collective-permute-start | bytes 1179656 | tf_op jit(solution)/shard_map/ppermute | solution.py:143
  103.4 17.5 %collective-permute-start.3 = (f32[128,768]{0,1:T(8,128)}, f32[128,768]{0,1:T(8,128)S(1)}, u32[]{:S(2)}, u32[]{:S(2)}) collective-permute-start(f32[128,768]{0,1:T(8,128)} %fusion.26), channel_id=1, source_target_pairs={{0,16},{8,24},{16,0},{24,8},{1,17},{9,25},{17,1},{25,9},{2,18},{10... | collective-permute-start | bytes 1179656 | tf_op jit(solution)/shard_map/ppermute | solution.py:143
  124.7 89.9 %slice-start = ((f32[128,768]{0,1:T(8,128)}), f32[128,512]{0,1:T(8,128)S(1)}, s32[]{:S(2)}) async-start(f32[128,768]{0,1:T(8,128)} %copy-done.4), calls=%async_computation.2 | async-start | bytes 524288 | tf_op jit(solution)/shard_map/slice | solution.py:144
  124.7 28.1 %collective-permute-start.9 = (bf16[1024,512]{1,0:T(8,128)(2,1)S(1)}, bf16[1024,512]{1,0:T(8,128)(2,1)S(1)}, u32[]{:S(2)}, u32[]{:S(2)}) collective-permute-start(bf16[1024,512]{1,0:T(8,128)(2,1)S(1)} %slice.145), channel_id=1, source_target_pairs={{0,16},{16,0},{1,17},{17,1},{2,18},{18,2},{3,19},{19,3},{4,20},{20... | collective-permute-start | bytes 3145736 | tf_op jit(solution)/shard_map/ppermute | solution.py:55
  155.2 64.2 %collective-permute-start.10 = (bf16[2048,512]{1,0:T(8,128)(2,1)}, bf16[2048,512]{1,0:T(8,128)(2,1)}, u32[]{:S(2)}, u32[]{:S(2)}) collective-permute-start(bf16[2048,512]{1,0:T(8,128)(2,1)} %pad_maximum_fusion.1), channel_id=1, source_target_pairs={{0,8},{8,0},{1,9},{9,1},{2,10},{10,2},{3,11},{11,3},{4,12},{12,4},... | collective-permute-start | bytes 6291464 | tf_op jit(solution)/shard_map/ppermute | solution.py:55
  191.5 20.6 %collective-permute-start.6 = (bf16[2176,256]{1,0:T(8,128)(2,1)}, bf16[2176,256]{1,0:T(8,128)(2,1)S(1)}, u32[]{:S(2)}, u32[]{:S(2)}) collective-permute-start(bf16[2176,256]{1,0:T(8,128)(2,1)} %all-gather.5.cloned.1.call-done), channel_id=1, source_target_pairs={{0,16},{16,0},{1,17},{17,1},{2,18},{18,2},{3,19},{19,3},{4,20},{20... | collective-permute-start | bytes 3342344 | tf_op jit(solution)/shard_map/ppermute | solution.py:157
  194.8 19.7 %copy-start.7 = (s32[2,64]{1,0:T(2,128)}, s32[2,64]{1,0:T(2,128)S(1)}, u32[]{:S(2)}) copy-start(s32[2,64]{1,0:T(2,128)S(1)} %reshape.402) | copy-start | bytes 1540
  195.9 27.1 %collective-permute-start.7 = (bf16[2176,256]{1,0:T(8,128)(2,1)}, bf16[2176,256]{1,0:T(8,128)(2,1)}, u32[]{:S(2)}, u32[]{:S(2)}) collective-permute-start(bf16[2176,256]{1,0:T(8,128)(2,1)} %all-gather.5.cloned.1.call-done), channel_id=1, source_target_pairs={{0,8},{8,0},{1,9},{9,1},{2,10},{10,2},{3,11},{11,3},{4,12},{12,4},... | collective-permute-start | bytes 3342344 | tf_op jit(solution)/shard_map/ppermute | solution.py:158
  212.1 11.8 %copy-start = (bf16[2176,256]{1,0:T(8,128)(2,1)}, bf16[2176,256]{1,0:T(8,128)(2,1)S(1)}, u32[]{:S(2)}) copy-start(bf16[2176,256]{1,0:T(8,128)(2,1)S(1)} %collective-permute-done.6) | copy-start | bytes 3342340
  212.1 11.8 %collective-permute-start.8 = (bf16[2176,256]{1,0:T(8,128)(2,1)S(1)}, bf16[2176,256]{1,0:T(8,128)(2,1)}, u32[]{:S(2)}, u32[]{:S(2)}) collective-permute-start(bf16[2176,256]{1,0:T(8,128)(2,1)S(1)} %collective-permute-done.6), channel_id=1, source_target_pairs={{0,8},{8,0},{1,9},{9,1},{2,10},{10,2},{3,11},{11,3},{4,12},{12,4},... | collective-permute-start | bytes 3342344 | tf_op jit(solution)/shard_map/ppermute | solution.py:158
  272.8 30.4 %copy-start.14 = (s32[32]{0:T(128)S(1)}, s32[32]{0:T(128)}, u32[]{:S(2)}) copy-start(s32[32]{0:T(128)} %param.23) | copy-start | bytes 388
  272.8 31.8 %copy-start.12 = (s32[128]{0:T(128)S(1)}, s32[128]{0:T(128)}, u32[]{:S(2)}) copy-start(s32[128]{0:T(128)} %param.21) | copy-start | bytes 1540
  272.9 31.8 %copy-start.13 = (s32[32]{0:T(128)S(1)}, s32[32]{0:T(128)}, u32[]{:S(2)}) copy-start(s32[32]{0:T(128)} %get-tuple-element.80) | copy-start | bytes 388
  273.8 16.5 %collective-permute-start.11 = (bf16[128,4,512]{0,2,1:T(8,128)(2,1)}, bf16[128,4,512]{0,2,1:T(8,128)(2,1)}, u32[]{:S(2)}, u32[]{:S(2)}) collective-permute-start(bf16[128,4,512]{0,2,1:T(8,128)(2,1)} %bitcast_convert_fusion), channel_id=1, source_target_pairs={{0,1},{1,0},{2,3},{3,2},{4,5},{5,4},{6,7},{7,6},{8,9},{9,8},{10,11... | collective-permute-start | bytes 1572872 | tf_op jit(solution)/shard_map/ppermute | solution.py:97
  292.5 12.3 %collective-permute-start.12 = (bf16[128,512]{0,1:T(8,128)(2,1)S(1)}, bf16[128,512]{0,1:T(8,128)(2,1)S(1)}, u32[]{:S(2)}, u32[]{:S(2)}) collective-permute-start(bf16[128,512]{0,1:T(8,128)(2,1)S(1)} %get-tuple-element.58), channel_id=1, source_target_pairs={{0,2},{2,4},{4,6},{6,0},{1,3},{3,5},{5,7},{7,1},{8,10},{10,12},{12... | collective-permute-start | bytes 393224 | tf_op jit(solution)/shard_map/ppermute | solution.py:101
  295.9 8.9 %collective-permute-start.14 = (bf16[128,512]{0,1:T(8,128)(2,1)S(1)}, bf16[128,512]{0,1:T(8,128)(2,1)S(1)}, u32[]{:S(2)}, u32[]{:S(2)}) collective-permute-start(bf16[128,512]{0,1:T(8,128)(2,1)S(1)} %get-tuple-element.59), channel_id=1, source_target_pairs={{0,6},{2,0},{4,2},{6,4},{1,7},{3,1},{5,3},{7,5},{8,14},{10,8},{12,... | collective-permute-start | bytes 393224 | tf_op jit(solution)/shard_map/ppermute | solution.py:101
  299.6 8.4 %collective-permute-start.13 = (bf16[128,512]{0,1:T(8,128)(2,1)S(1)}, bf16[128,512]{0,1:T(8,128)(2,1)S(1)}, u32[]{:S(2)}, u32[]{:S(2)}) collective-permute-start(bf16[128,512]{0,1:T(8,128)(2,1)S(1)} %get-tuple-element.60), channel_id=1, source_target_pairs={{0,4},{2,6},{4,0},{6,2},{1,5},{3,7},{5,1},{7,3},{8,12},{10,14},{12... | collective-permute-start | bytes 393224 | tf_op jit(solution)/shard_map/ppermute | solution.py:101
  (9 other events, 36.3 us)
Sparse Core Ops, SparseCore 0:
  10.1 79.3 all-gather.2
  123.5 67.9 all-gather.4

commit v7 on v5

--- a/solution.py
+++ b/solution.py
@@ -133,14 +133,16 @@
         quarters = jnp.transpose(
             normed.reshape(tok_rows, nz, nxh, nc, d_rows), (0, 2, 3, 1, 4)
         ).reshape(tok_rows, npair, nz * d_rows)
-        proj = jnp.dot(
-            jnp.take(quarters, me, axis=1), w_proj, preferred_element_type=jnp.float32
-        )
-        for flip in range(1, npair):
-            perm = [(i, i ^ flip) for i in range(npair)]
-            theirs = lax.ppermute(jnp.take(quarters, me ^ flip, axis=1), pair, perm)
-            part = jnp.dot(theirs, w_proj, preferred_element_type=jnp.float32)
-            proj = proj + lax.ppermute(part, pair, perm)
+        perms = [[(i, i ^ flip) for i in range(npair)] for flip in range(1, npair)]
+        theirs = [
+            lax.ppermute(jnp.take(quarters, me ^ flip, axis=1), pair, perm)
+            for flip, perm in zip(range(1, npair), perms)
+        ]
+        stacked = jnp.concatenate([jnp.take(quarters, me, axis=1)] + theirs, axis=0)
+        parts = jnp.dot(stacked, w_proj, preferred_element_type=jnp.float32)
+        proj = parts[:tok_rows]
+        for k, perm in enumerate(perms):
+            proj = proj + lax.ppermute(parts[(k + 1) * tok_rows : (k + 2) * tok_rows], pair, perm)
         queries = proj[:, :q_cols].reshape(tok_rows, group_size, HEAD_DIM)
         key_proj = proj[:, q_cols : q_cols + kv_cols]
         value_proj = proj[:, q_cols + kv_cols :].astype(jnp.bfloat16)

time: 349 us -> 347 us (level)
  matrix products: 21 us -> 12.9 us
  waiting for transfers between devices: 171 us -> 175 us
    ppermute x6, waiting for transfers between devices: 11.2 us -> 24.8 us  [the longest x3 15.7 us: local(): lax.ppermute(parts[(k + 1) * tok_rows:(k + 2) * tok_rows], pair, perm)]
    all_gather x2, waiting for transfers between devices: 130 us -> 121 us  [gather_z(): return lax.all_gather(x, 'z', axis=0, tiled=True)]
    dot_general x4 -> x1, matrix products: 10.7 us -> 2.61 us  [local(): parts = jnp.dot(stacked, w_proj, preferred_element_type=jnp.float32)]
  transfers between devices with their start and end apart: 16 -> 16, of which waited for: 7 -> 9; matrix products, arithmetic and copies ran while one was open for 9% -> 6% of each run, Pallas kernels for 0% -> 0%
where the time goes in v7:
time: 347 us; the launch traced here: 346 us
  waiting for transfers between devices  175 us (50%)
  starting transfers between devices  42.7 us (12%)
  blocking collectives  38.2 us (11%)
  other arithmetic  37.2 us (11%)
  local copies, waits for them, and re-layouts  24.3 us (7%)
  between operations  15.4 us (4%)
  matrix products  12.9 us (4%)
    all_gather x2, waiting for transfers between devices, gather_z(): return lax.all_gather(x, 'z', axis=0, tiled=True)  121 us
    psum x3, blocking collectives, local(): sums = lax.psum(sums, axis)  38.2 us
    concatenate x4, other arithmetic, swap_cat(): return jnp.concatenate([x, lax.ppermute(x, axis_name, [(0, 1), (1, 0)])], 0)  19.3 us
    ppermute x3, waiting for transfers between devices, local(): lax.ppermute(parts[(k + 1) * tok_rows:(k + 2) * tok_rows], pair, perm)  15.7 us
    ppermute x1, waiting for transfers between devices, reduce_scatter_head(): lax.ppermute(sent, 'xl', [(0, 1), (1, 0)]).astype(jnp.float32)  14.2 us
    ppermute x4, waiting for transfers between devices, swap_cat(): return jnp.concatenate([x, lax.ppermute(x, axis_name, [(0, 1), (1, 0)])], 0)  12.6 us
    ppermute x3, starting transfers between devices, reduce_scatter_head(): lax.ppermute(piece, 'y', [(i, (i + shift) % ny) for i in range(ny)])  11.4 us
    ppermute x4, starting transfers between devices, swap_cat(): return jnp.concatenate([x, lax.ppermute(x, axis_name, [(0, 1), (1, 0)])], 0)  10.8 us
  transfers between devices with their start and end apart: 16, of which 9 were waited for; matrix products, arithmetic and copies ran while one was open for 6% of the time, Pallas kernels for 0%

profile of v7, /device:TPU:6, one launch (start us, length us, event | category | flops | bytes accessed | tf_op | source)
XLA Modules:
  0.0 345.9 jit_solution(9631258097297682458)
XLA Ops:
  14.0 3.3 collective-permute-start.1
  17.3 3.9 %collective-permute-start.2 = (bf16[128,1024]{0,1:T(8,128)(2,1)S(1)}, bf16[128,1024]{0,1:T(8,128)(2,1)S(1)}, u32[]{:S(2)}, u32[]{:S(2)}) collective-permute-start(bf16[128,1024]{0,1:T(8,128)(2,1)S(1)} %get-tuple-element.60), channel_id=1, source_target_pairs={{0,24},{8,16},{16,8},{24,0},{1,25},{9,17},{17,9},{25,1},{2,26},{10... | collective-permute-start | bytes 786440 | tf_op jit(solution)/shard_map/ppermute | solution.py:138
  22.2 4.3 %collective-permute-done.1 = bf16[128,1024]{0,1:T(8,128)(2,1)S(1)} collective-permute-done((bf16[128,1024]{0,1:T(8,128)(2,1)S(1)}, bf16[128,1024]{0,1:T(8,128)(2,1)S(1)}, u32[]{:S(2)}, u32[]{:S(2)}) %collective-permute-start.1) | collective-permute-done | bytes 262176 | tf_op jit(solution)/shard_map/ppermute | solution.py:138
  26.5 4.8 %collective-permute-done.2 = bf16[128,1024]{0,1:T(8,128)(2,1)S(1)} collective-permute-done((bf16[128,1024]{0,1:T(8,128)(2,1)S(1)}, bf16[128,1024]{0,1:T(8,128)(2,1)S(1)}, u32[]{:S(2)}, u32[]{:S(2)}) %collective-permute-start.2) | collective-permute-done | bytes 262176 | tf_op jit(solution)/shard_map/ppermute | solution.py:138
  31.3 58.2 %all-gather.3.cloned.1.call-done = bf16[1024,1280]{1,0:T(8,128)(2,1)} async-done(((bf16[64,1280]{1,0:T(8,128)(2,1)}), bf16[1024,1280]{1,0:T(8,128)(2,1)}) %all-gather.3.cloned.1.call-update) | async-done | bytes 2621456 | tf_op jit(solution)/shard_map/all_gather | solution.py:59
  94.9 3.4 collective-permute-start.4
  98.2 3.8 %collective-permute-start.5 = (f32[128,768]{0,1:T(8,128)S(1)}, f32[128,768]{0,1:T(8,128)}, u32[]{:S(2)}, u32[]{:S(2)}) collective-permute-start(f32[128,768]{0,1:T(8,128)S(1)} %get-tuple-element.55), channel_id=1, source_target_pairs={{0,24},{8,16},{16,8},{24,0},{1,25},{9,17},{17,9},{25,1},{2,26},{10... | collective-permute-start | bytes 1179656 | tf_op jit(solution)/shard_map/ppermute | solution.py:145
  102.2 8.0 %collective-permute-done.4 = f32[128,768]{0,1:T(8,128)} collective-permute-done((f32[128,768]{0,1:T(8,128)S(1)}, f32[128,768]{0,1:T(8,128)}, u32[]{:S(2)}, u32[]{:S(2)}) %collective-permute-start.4) | collective-permute-done | bytes 393248 | tf_op jit(solution)/shard_map/ppermute | solution.py:145
  110.3 7.6 %collective-permute-done.5 = f32[128,768]{0,1:T(8,128)} collective-permute-done((f32[128,768]{0,1:T(8,128)S(1)}, f32[128,768]{0,1:T(8,128)}, u32[]{:S(2)}, u32[]{:S(2)}) %collective-permute-start.5) | collective-permute-done | bytes 393248 | tf_op jit(solution)/shard_map/ppermute | solution.py:145
  122.9 3.4 collective-permute-start.8
  126.3 63.3 %all-gather.5.cloned.1.call-done = bf16[2176,256]{1,0:T(8,128)(2,1)} async-done(((bf16[136,256]{1,0:T(8,128)(2,1)}), bf16[2176,256]{1,0:T(8,128)(2,1)}) %all-gather.5.cloned.1.call-update) | async-done | bytes 1114128 | tf_op jit(solution)/shard_map/all_gather | solution.py:59
  189.6 3.5 %collective-permute-start.6 = (bf16[2176,256]{1,0:T(8,128)(2,1)}, bf16[2176,256]{1,0:T(8,128)(2,1)S(1)}, u32[]{:S(2)}, u32[]{:S(2)}) collective-permute-start(bf16[2176,256]{1,0:T(8,128)(2,1)} %all-gather.5.cloned.1.call-done), channel_id=1, source_target_pairs={{0,16},{16,0},{1,17},{17,1},{2,18},{18,2},{3,19},{19,3},{4,20},{20... | collective-permute-start | bytes 3342344 | tf_op jit(solution)/shard_map/ppermute | solution.py:55
  197.9 12.6 %collective-permute-done.6 = bf16[2176,256]{1,0:T(8,128)(2,1)S(1)} collective-permute-done((bf16[2176,256]{1,0:T(8,128)(2,1)}, bf16[2176,256]{1,0:T(8,128)(2,1)S(1)}, u32[]{:S(2)}, u32[]{:S(2)}) %collective-permute-start.6) | collective-permute-done | bytes 1114144 | tf_op jit(solution)/shard_map/ppermute | solution.py:55
  220.0 3.6 %pad_maximum_fusion.1 = bf16[4096,512]{1,0:T(8,128)(2,1)} fusion(bf16[2048,512]{1,0:T(8,128)(2,1)} %collective-permute-done.9, bf16[1024,512]{1,0:T(8,128)(2,1)} %collective-permute-done.8, bf16[1024,512]{1,0:T(8,128)(2,1)S(1)} %slice.149), kind=kLoop, calls=%fused_computation.14 | loop fusion | flops 12582912 | bytes 8388608 | tf_op jit(solution)/shard_map/concatenate | solution.py:55
  223.7 11.3 %pad_maximum_fusion = bf16[8704,256]{1,0:T(8,128)(2,1)S(1)} fusion(bf16[4352,256]{1,0:T(8,128)(2,1)} %collective-permute-done.7, bf16[2176,256]{1,0:T(8,128)(2,1)S(1)} %copy-done.2, bf16[2176,256]{1,0:T(8,128)(2,1)S(1)} %copy-done), kind=kLoop, calls=%fused_computation.13 | loop fusion | flops 13369344 | bytes 8912896 | tf_op jit(solution)/shard_map/concatenate | solution.py:55
  244.3 4.5 %fusion.64 = (f32[2,4,64]{2,1,0:T(4,128)S(1)}, bf16[2,4,64,2112]{3,2,1,0:T(8,128)(2,1)}) fusion(pred[2,64,2112]{2,1,0:T(8,128)(4,1)S(1)} %compare_and_fusion, bf16[2,2112,256]{2,1,0:T(8,128)(2,1)S(1)} %bitcast.117, bf16[2,64,4,64]{3,1,2,0:T(8,128)(2,1)} %copy.98, bf16[2,64,4,64]{3,1,2,0:T(8,128)(2,1)} %copy.97), kind=kOutput, calls=%fused_computation.144 | convolution fusion | flops 283576384 | bytes 3934208 | tf_op jit(solution)/shard_map/sub | solution.py:189
  251.3 3.4 fusion.41
  256.8 3.3 select_bitcast_fusion.1
  266.2 14.2 %collective-permute-done.10 = bf16[128,4,512]{0,2,1:T(8,128)(2,1)} collective-permute-done((bf16[128,4,512]{0,2,1:T(8,128)(2,1)}, bf16[128,4,512]{0,2,1:T(8,128)(2,1)}, u32[]{:S(2)}, u32[]{:S(2)}) %collective-permute-start.10) | collective-permute-done | bytes 524320 | tf_op jit(solution)/shard_map/ppermute | solution.py:97
  282.7 3.4 collective-permute-start.11
  286.1 4.6 %collective-permute-start.12 = (bf16[128,512]{0,1:T(8,128)(2,1)S(1)}, bf16[128,512]{0,1:T(8,128)(2,1)S(1)}, u32[]{:S(2)}, u32[]{:S(2)}) collective-permute-start(bf16[128,512]{0,1:T(8,128)(2,1)S(1)} %get-tuple-element.58), channel_id=1, source_target_pairs={{0,4},{2,6},{4,0},{6,2},{1,5},{3,7},{5,1},{7,3},{8,12},{10,14},{12... | collective-permute-start | bytes 393224 | tf_op jit(solution)/shard_map/ppermute | solution.py:101
  290.7 3.3 collective-permute-start.13
  301.2 6.4 %psum.22 = f32[2,512]{1,0:T(2,128)S(1)} all-reduce(f32[2,512]{1,0:T(2,128)S(1)} %psum.21), channel_id=1, replica_groups=mesh['z'=16,'xh'=2,'c'=2,'y'=4,'xl'=2] {'xh'}, use_global_device_ids=true, to_apply=%region_12.16 | all-reduce | flops 1024 | bytes 8192 | tf_op jit(solution)/shard_map/psum | solution.py:222
  307.7 29.3 %psum.23 = f32[2,512]{1,0:T(2,128)S(1)} all-reduce(f32[2,512]{1,0:T(2,128)S(1)} %psum.22), channel_id=1, replica_groups=mesh['z'=16,'xh'=2,'c'=2,'y'=4,'xl'=2] {'z'}, use_global_device_ids=true, to_apply=%region_13.17 | all-reduce | flops 1024 | bytes 8192 | tf_op jit(solution)/shard_map/psum | solution.py:222
  (128 shorter events, 62.8 us)
Async XLA Ops:
  7.2 82.3 %all-gather.3.cloned.1.call-start = ((), (), s32[]{:S(2)}) async-start(), calls=%async_computation | async-start | bytes 2785280 | tf_op jit(solution)/shard_map/all_gather | solution.py:59
  8.8 180.7 %all-gather.5.cloned.1.call-start = ((), (), s32[]{:S(2)}) async-start(), calls=%async_computation.1 | async-start | bytes 1183744 | tf_op jit(solution)/shard_map/all_gather | solution.py:59
  11.8 10.1 %copy-start.9 = (s32[128]{0:T(128)S(1)}, s32[128]{0:T(128)}, u32[]{:S(2)}) copy-start(s32[128]{0:T(128)} %param.21) | copy-start | bytes 1540
  12.1 10.1 %collective-permute-start = (bf16[128,1024]{0,1:T(8,128)(2,1)S(1)}, bf16[128,1024]{0,1:T(8,128)(2,1)S(1)}, u32[]{:S(2)}, u32[]{:S(2)}) collective-permute-start(bf16[128,1024]{0,1:T(8,128)(2,1)S(1)} %get-tuple-element.62), channel_id=1, source_target_pairs={{0,8},{8,0},{16,24},{24,16},{1,9},{9,1},{17,25},{25,17},{2,10},{10... | collective-permute-start | bytes 786440 | tf_op jit(solution)/shard_map/ppermute | solution.py:138
  14.0 12.5 %collective-permute-start.1 = (bf16[128,1024]{0,1:T(8,128)(2,1)S(1)}, bf16[128,1024]{0,1:T(8,128)(2,1)S(1)}, u32[]{:S(2)}, u32[]{:S(2)}) collective-permute-start(bf16[128,1024]{0,1:T(8,128)(2,1)S(1)} %get-tuple-element.61), channel_id=1, source_target_pairs={{0,16},{8,24},{16,0},{24,8},{1,17},{9,25},{17,1},{25,9},{2,18},{10... | collective-permute-start | bytes 786440 | tf_op jit(solution)/shard_map/ppermute | solution.py:138
  17.3 14.0 %collective-permute-start.2 = (bf16[128,1024]{0,1:T(8,128)(2,1)S(1)}, bf16[128,1024]{0,1:T(8,128)(2,1)S(1)}, u32[]{:S(2)}, u32[]{:S(2)}) collective-permute-start(bf16[128,1024]{0,1:T(8,128)(2,1)S(1)} %get-tuple-element.60), channel_id=1, source_target_pairs={{0,24},{8,16},{16,8},{24,0},{1,25},{9,17},{17,9},{25,1},{2,26},{10... | collective-permute-start | bytes 786440 | tf_op jit(solution)/shard_map/ppermute | solution.py:138
  26.5 63.0 %copy-start.13 = (bf16[128,1024]{0,1:T(8,128)(2,1)}, bf16[128,1024]{0,1:T(8,128)(2,1)S(1)}, u32[]{:S(2)}) copy-start(bf16[128,1024]{0,1:T(8,128)(2,1)S(1)} %collective-permute-done.1) | copy-start | bytes 786436
  31.3 58.2 %copy-start.14 = (bf16[128,1024]{0,1:T(8,128)(2,1)}, bf16[128,1024]{0,1:T(8,128)(2,1)S(1)}, u32[]{:S(2)}) copy-start(bf16[128,1024]{0,1:T(8,128)(2,1)S(1)} %collective-permute-done.2) | copy-start | bytes 786436
  92.9 9.3 %collective-permute-start.3 = (f32[128,768]{0,1:T(8,128)}, f32[128,768]{0,1:T(8,128)}, u32[]{:S(2)}, u32[]{:S(2)}) collective-permute-start(f32[128,768]{0,1:T(8,128)} %get-tuple-element.53), channel_id=1, source_target_pairs={{0,8},{8,0},{16,24},{24,16},{1,9},{9,1},{17,25},{25,17},{2,10},{10... | collective-permute-start | bytes 1179656 | tf_op jit(solution)/shard_map/ppermute | solution.py:145
  94.9 15.4 %collective-permute-start.4 = (f32[128,768]{0,1:T(8,128)S(1)}, f32[128,768]{0,1:T(8,128)}, u32[]{:S(2)}, u32[]{:S(2)}) collective-permute-start(f32[128,768]{0,1:T(8,128)S(1)} %get-tuple-element.54), channel_id=1, source_target_pairs={{0,16},{8,24},{16,0},{24,8},{1,17},{9,25},{17,1},{25,9},{2,18},{10... | collective-permute-start | bytes 1179656 | tf_op jit(solution)/shard_map/ppermute | solution.py:145
  98.2 19.7 %collective-permute-start.5 = (f32[128,768]{0,1:T(8,128)S(1)}, f32[128,768]{0,1:T(8,128)}, u32[]{:S(2)}, u32[]{:S(2)}) collective-permute-start(f32[128,768]{0,1:T(8,128)S(1)} %get-tuple-element.55), channel_id=1, source_target_pairs={{0,24},{8,16},{16,8},{24,0},{1,25},{9,17},{17,9},{25,1},{2,26},{10... | collective-permute-start | bytes 1179656 | tf_op jit(solution)/shard_map/ppermute | solution.py:145
  122.9 70.2 %collective-permute-start.8 = (bf16[1024,512]{1,0:T(8,128)(2,1)S(1)}, bf16[1024,512]{1,0:T(8,128)(2,1)}, u32[]{:S(2)}, u32[]{:S(2)}) collective-permute-start(bf16[1024,512]{1,0:T(8,128)(2,1)S(1)} %slice.149), channel_id=1, source_target_pairs={{0,16},{16,0},{1,17},{17,1},{2,18},{18,2},{3,19},{19,3},{4,20},{20... | collective-permute-start | bytes 3145736 | tf_op jit(solution)/shard_map/ppermute | solution.py:55
  189.6 20.9 %copy-start = (bf16[2176,256]{1,0:T(8,128)(2,1)S(1)}, bf16[2176,256]{1,0:T(8,128)(2,1)}, u32[]{:S(2)}) copy-start(bf16[2176,256]{1,0:T(8,128)(2,1)} %all-gather.5.cloned.1.call-done) | copy-start | bytes 3342340
  189.6 20.9 %collective-permute-start.6 = (bf16[2176,256]{1,0:T(8,128)(2,1)}, bf16[2176,256]{1,0:T(8,128)(2,1)S(1)}, u32[]{:S(2)}, u32[]{:S(2)}) collective-permute-start(bf16[2176,256]{1,0:T(8,128)(2,1)} %all-gather.5.cloned.1.call-done), channel_id=1, source_target_pairs={{0,16},{16,0},{1,17},{17,1},{2,18},{18,2},{3,19},{19,3},{4,20},{20... | collective-permute-start | bytes 3342344 | tf_op jit(solution)/shard_map/ppermute | solution.py:55
  195.8 20.2 %slice-start = ((f32[128,768]{0,1:T(8,128)}), f32[128,512]{0,1:T(8,128)S(1)}, s32[]{:S(2)}) async-start(f32[128,768]{0,1:T(8,128)} %copy-done.4), calls=%async_computation.2 | async-start | bytes 524288 | tf_op jit(solution)/shard_map/slice | solution.py:146
  195.8 24.2 %collective-permute-start.9 = (bf16[2048,512]{1,0:T(8,128)(2,1)}, bf16[2048,512]{1,0:T(8,128)(2,1)}, u32[]{:S(2)}, u32[]{:S(2)}) collective-permute-start(bf16[2048,512]{1,0:T(8,128)(2,1)} %pad_maximum_fusion.3), channel_id=1, source_target_pairs={{0,8},{8,0},{1,9},{9,1},{2,10},{10,2},{3,11},{11,3},{4,12},{12,4},... | collective-permute-start | bytes 6291464 | tf_op jit(solution)/shard_map/ppermute | solution.py:55
  212.3 11.4 %collective-permute-start.7 = (bf16[4352,256]{1,0:T(8,128)(2,1)}, bf16[4352,256]{1,0:T(8,128)(2,1)}, u32[]{:S(2)}, u32[]{:S(2)}) collective-permute-start(bf16[4352,256]{1,0:T(8,128)(2,1)} %pad_maximum_fusion.2), channel_id=1, source_target_pairs={{0,8},{8,0},{1,9},{9,1},{2,10},{10,2},{3,11},{11,3},{4,12},{12,4},... | collective-permute-start | bytes 6684680 | tf_op jit(solution)/shard_map/ppermute | solution.py:55
  263.0 31.1 %copy-start.15 = (s32[32]{0:T(128)S(1)}, s32[32]{0:T(128)}, u32[]{:S(2)}) copy-start(s32[32]{0:T(128)} %param.23) | copy-start | bytes 388
  263.0 32.4 %copy-start.10 = (s32[128]{0:T(128)S(1)}, s32[128]{0:T(128)}, u32[]{:S(2)}) copy-start(s32[128]{0:T(128)} %param.21) | copy-start | bytes 1540
  263.0 32.4 %copy-start.11 = (s32[32]{0:T(128)S(1)}, s32[32]{0:T(128)}, u32[]{:S(2)}) copy-start(s32[32]{0:T(128)} %get-tuple-element.77) | copy-start | bytes 388
  263.9 16.5 %collective-permute-start.10 = (bf16[128,4,512]{0,2,1:T(8,128)(2,1)}, bf16[128,4,512]{0,2,1:T(8,128)(2,1)}, u32[]{:S(2)}, u32[]{:S(2)}) collective-permute-start(bf16[128,4,512]{0,2,1:T(8,128)(2,1)} %bitcast_convert_fusion), channel_id=1, source_target_pairs={{0,1},{1,0},{2,3},{3,2},{4,5},{5,4},{6,7},{7,6},{8,9},{9,8},{10,11... | collective-permute-start | bytes 1572872 | tf_op jit(solution)/shard_map/ppermute | solution.py:97
  282.7 12.9 %collective-permute-start.11 = (bf16[128,512]{0,1:T(8,128)(2,1)S(1)}, bf16[128,512]{0,1:T(8,128)(2,1)S(1)}, u32[]{:S(2)}, u32[]{:S(2)}) collective-permute-start(bf16[128,512]{0,1:T(8,128)(2,1)S(1)} %get-tuple-element.56), channel_id=1, source_target_pairs={{0,2},{2,4},{4,6},{6,0},{1,3},{3,5},{5,7},{7,1},{8,10},{10,12},{12... | collective-permute-start | bytes 393224 | tf_op jit(solution)/shard_map/ppermute | solution.py:101
  286.1 9.5 %collective-permute-start.12 = (bf16[128,512]{0,1:T(8,128)(2,1)S(1)}, bf16[128,512]{0,1:T(8,128)(2,1)S(1)}, u32[]{:S(2)}, u32[]{:S(2)}) collective-permute-start(bf16[128,512]{0,1:T(8,128)(2,1)S(1)} %get-tuple-element.58), channel_id=1, source_target_pairs={{0,4},{2,6},{4,0},{6,2},{1,5},{3,7},{5,1},{7,3},{8,12},{10,14},{12... | collective-permute-start | bytes 393224 | tf_op jit(solution)/shard_map/ppermute | solution.py:101
  290.7 6.9 %collective-permute-start.13 = (bf16[128,512]{0,1:T(8,128)(2,1)S(1)}, bf16[128,512]{0,1:T(8,128)(2,1)S(1)}, u32[]{:S(2)}, u32[]{:S(2)}) collective-permute-start(bf16[128,512]{0,1:T(8,128)(2,1)S(1)} %get-tuple-element.57), channel_id=1, source_target_pairs={{0,6},{2,0},{4,2},{6,4},{1,7},{3,1},{5,3},{7,5},{8,14},{10,8},{12,... | collective-permute-start | bytes 393224 | tf_op jit(solution)/shard_map/ppermute | solution.py:101
  (9 other events, 27.8 us)
Sparse Core Ops, SparseCore 0:
  10.1 79.3 all-gather.2
  121.7 67.7 all-gather.4

commit v8 on v7

--- a/solution.py
+++ b/solution.py
@@ -61,6 +61,21 @@
 
 def gather_pair(x):
     return swap_cat(swap_cat(x, "xh"), "c")
+
+
+def ring_gather(x, axis_name, n):
+    fwd, bwd = x, x
+    by_offset = {0: x}
+    for step in range(1, n // 2 + 1):
+        fwd = lax.ppermute(fwd, axis_name, [(i, (i + 1) % n) for i in range(n)])
+        by_offset[n - step] = fwd
+        if len(by_offset) < n:
+            bwd = lax.ppermute(bwd, axis_name, [(i, (i - 1) % n) for i in range(n)])
+            by_offset[step] = bwd
+    rel = jnp.stack([by_offset[k] for k in range(n)])
+    here = lax.axis_index(axis_name)
+    absolute = jnp.take(rel, (jnp.arange(n, dtype=jnp.int32) - here) % n, axis=0)
+    return absolute.reshape((n * x.shape[0],) + x.shape[1:])
 
 
 def relative_index():
@@ -121,11 +136,11 @@
         normed = rms_norm(tokens, norm_gain)
         doc_index, in_doc, doc_ends = doc_layout(row_map, doc_lengths)
 
-        qkv_cols = q_cols + 2 * kv_cols
         out_cols = w_out.shape[0]
-        w_z = gather_z(jnp.concatenate([w_query, w_key, w_value, w_out.T], axis=1))
-        w_o = gather_pair(w_z[:, qkv_cols:]).reshape(nctx, d_rows, out_cols)
-        w_proj = w_z[:, :qkv_cols]
+        w_z = gather_z(jnp.concatenate([w_key, w_value, w_out.T], axis=1))
+        w_kv = w_z[:, : 2 * kv_cols]
+        w_o = gather_pair(w_z[:, 2 * kv_cols :]).reshape(nctx, d_rows, out_cols)
+        w_q = ring_gather(w_query, "z", nz)
 
         pair = ("xh", "c")
         npair = nxh * nc
@@ -139,13 +154,21 @@
             for flip, perm in zip(range(1, npair), perms)
         ]
         stacked = jnp.concatenate([jnp.take(quarters, me, axis=1)] + theirs, axis=0)
-        parts = jnp.dot(stacked, w_proj, preferred_element_type=jnp.float32)
-        proj = parts[:tok_rows]
-        for k, perm in enumerate(perms):
-            proj = proj + lax.ppermute(parts[(k + 1) * tok_rows : (k + 2) * tok_rows], pair, perm)
-        queries = proj[:, :q_cols].reshape(tok_rows, group_size, HEAD_DIM)
-        key_proj = proj[:, q_cols : q_cols + kv_cols]
-        value_proj = proj[:, q_cols + kv_cols :].astype(jnp.bfloat16)
+
+        def exchange(weights):
+            parts = jnp.dot(stacked, weights, preferred_element_type=jnp.float32)
+            total = parts[:tok_rows]
+            for k, perm in enumerate(perms):
+                total = total + lax.ppermute(
+                    parts[(k + 1) * tok_rows : (k + 2) * tok_rows], pair, perm
+                )
+            return total
+
+        proj_kv = exchange(w_kv)
+        proj_q = exchange(w_q)
+        queries = proj_q.reshape(tok_rows, group_size, HEAD_DIM)
+        key_proj = proj_kv[:, :kv_cols]
+        value_proj = proj_kv[:, kv_cols:].astype(jnp.bfloat16)
         queries = rotate(queries, in_doc).astype(jnp.bfloat16)
         key_proj = rotate(key_proj, in_doc).astype(jnp.bfloat16)
 

time: 347 us -> 373 us (1.075)
  starting transfers between devices: 42.7 us -> 110 us
  waiting for transfers between devices: 175 us -> 120 us
  local copies, waits for them, and re-layouts: 24.3 us -> 37.7 us
    ppermute x3 -> x21, starting transfers between devices: 9.08 us -> 75.4 us  [the longest x7 41.7 us: ring_gather(): bwd = lax.ppermute(bwd, axis_name, [(i, (i - 1) % n) for i in range(n)])]
    all_gather x2, waiting for transfers between devices: 121 us -> 56.4 us  [gather_z(): return lax.all_gather(x, 'z', axis=0, tiled=True)]
    unnamed x35 -> x66, local copies, waits for them, and re-layouts: 4.28 us -> 14.8 us
    ppermute x4, waiting for transfers between devices: 12.6 us -> 22.9 us  [swap_cat(): return jnp.concatenate([x, lax.ppermute(x, axis_name, [(0, 1), (1, 0)])], 0)]
    ppermute x3 -> x21, waiting for transfers between devices: 15.7 us -> 17.8 us  [the longest x8 10 us: ring_gather(): fwd = lax.ppermute(fwd, axis_name, [(i, (i + 1) % n) for i in range(n)])]
  transfers between devices with their start and end apart: 16 -> 34, of which waited for: 9 -> 13; matrix products, arithmetic and copies ran while one was open for 6% -> 12% of each run, Pallas kernels for 0% -> 0%
where the time goes in v8:
time: 373 us; the launch traced here: 371 us
  waiting for transfers between devices  120 us (32%)
  starting transfers between devices  110 us (29%)
  other arithmetic  38.2 us (10%)
  local copies, waits for them, and re-layouts  37.7 us (10%)
  blocking collectives  35.9 us (10%)
  between operations  15.7 us (4%)
  matrix products  13.8 us (4%)
    all_gather x2, waiting for transfers between devices, gather_z(): return lax.all_gather(x, 'z', axis=0, tiled=True)  56.4 us
    ppermute x7, starting transfers between devices, ring_gather(): bwd = lax.ppermute(bwd, axis_name, [(i, (i - 1) % n) for i in range(n)])  41.7 us
    psum x3, blocking collectives, local(): sums = lax.psum(sums, axis)  35.9 us
    ppermute x4, waiting for transfers between devices, swap_cat(): return jnp.concatenate([x, lax.ppermute(x, axis_name, [(0, 1), (1, 0)])], 0)  22.9 us
    concatenate x4, other arithmetic, swap_cat(): return jnp.concatenate([x, lax.ppermute(x, axis_name, [(0, 1), (1, 0)])], 0)  19.3 us
    ppermute x6, starting transfers between devices, exchange(): lax.ppermute(parts[(k + 1) * tok_rows:(k + 2) * tok_rows], pair, perm)  18.4 us
    ppermute x8, starting transfers between devices, ring_gather(): fwd = lax.ppermute(fwd, axis_name, [(i, (i + 1) % n) for i in range(n)])  15.3 us
    unnamed x66, local copies, waits for them, and re-layouts  14.8 us
  transfers between devices with their start and end apart: 34, of which 13 were waited for; matrix products, arithmetic and copies ran while one was open for 12% of the time, Pallas kernels for 0%

profile of v8, /device:TPU:6, one launch (start us, length us, event | category | flops | bytes accessed | tf_op | source)
XLA Modules:
  0.0 371.0 jit_solution(3231479360174492483)
XLA Ops:
  7.2 11.4 %collective-permute-start.8 = (bf16[64,512]{1,0:T(8,128)(2,1)}, bf16[64,512]{1,0:T(8,128)(2,1)S(1)}, u32[]{:S(2)}, u32[]{:S(2)}) collective-permute-start(bf16[64,512]{1,0:T(8,128)(2,1)} %param.17), channel_id=1, source_target_pairs={{0,480},{32,0},{64,32},{96,64},{128,96},{160,128},{192,160},{224,1... | collective-permute-start | bytes 196616 | tf_op jit(solution)/shard_map/ppermute | solution.py:73
  30.6 3.9 %collective-permute-start.2 = (bf16[128,1024]{0,1:T(8,128)(2,1)S(1)}, bf16[128,1024]{0,1:T(8,128)(2,1)S(1)}, u32[]{:S(2)}, u32[]{:S(2)}) collective-permute-start(bf16[128,1024]{0,1:T(8,128)(2,1)S(1)} %get-tuple-element.56), channel_id=1, source_target_pairs={{0,24},{8,16},{16,8},{24,0},{1,25},{9,17},{17,9},{25,1},{2,26},{10... | collective-permute-start | bytes 786440 | tf_op jit(solution)/shard_map/ppermute | solution.py:153
  39.8 4.8 %collective-permute-done.2 = bf16[128,1024]{0,1:T(8,128)(2,1)S(1)} collective-permute-done((bf16[128,1024]{0,1:T(8,128)(2,1)S(1)}, bf16[128,1024]{0,1:T(8,128)(2,1)S(1)}, u32[]{:S(2)}, u32[]{:S(2)}) %collective-permute-start.2) | collective-permute-done | bytes 262176 | tf_op jit(solution)/shard_map/ppermute | solution.py:153
  44.6 46.8 %all-gather.3.cloned.1.call-done = bf16[1024,768]{1,0:T(8,128)(2,1)} async-done(((bf16[64,768]{1,0:T(8,128)(2,1)}), bf16[1024,768]{1,0:T(8,128)(2,1)}) %all-gather.3.cloned.1.call-update) | async-done | bytes 1572880 | tf_op jit(solution)/shard_map/all_gather | solution.py:59
  98.4 3.8 %collective-permute-start.5 = (f32[128,256]{0,1:T(8,128)S(1)}, f32[128,256]{0,1:T(8,128)S(1)}, u32[]{:S(2)}, u32[]{:S(2)}) collective-permute-start(f32[128,256]{0,1:T(8,128)S(1)} %get-tuple-element.60), channel_id=1, source_target_pairs={{0,24},{8,16},{16,8},{24,0},{1,25},{9,17},{17,9},{25,1},{2,26},{10... | collective-permute-start | bytes 393224 | tf_op jit(solution)/shard_map/ppermute | solution.py:162
  102.5 4.6 %collective-permute-start.9 = (bf16[64,512]{1,0:T(8,128)(2,1)S(1)}, bf16[64,512]{1,0:T(8,128)(2,1)S(1)}, u32[]{:S(2)}, u32[]{:S(2)}) collective-permute-start(bf16[64,512]{1,0:T(8,128)(2,1)S(1)} %collective-permute-done.8), channel_id=1, source_target_pairs={{0,480},{32,0},{64,32},{96,64},{128,96},{160,128},{192,160},{224,1... | collective-permute-start | bytes 196616 | tf_op jit(solution)/shard_map/ppermute | solution.py:73
  110.8 5.1 %collective-permute-start.10 = (bf16[64,512]{1,0:T(8,128)(2,1)S(1)}, bf16[64,512]{1,0:T(8,128)(2,1)S(1)}, u32[]{:S(2)}, u32[]{:S(2)}) collective-permute-start(bf16[64,512]{1,0:T(8,128)(2,1)S(1)} %collective-permute-done.9), channel_id=1, source_target_pairs={{0,480},{32,0},{64,32},{96,64},{128,96},{160,128},{192,160},{224,1... | collective-permute-start | bytes 196616 | tf_op jit(solution)/shard_map/ppermute | solution.py:73
  118.5 5.1 %collective-permute-start.11 = (bf16[64,512]{1,0:T(8,128)(2,1)S(1)}, bf16[64,512]{1,0:T(8,128)(2,1)S(1)}, u32[]{:S(2)}, u32[]{:S(2)}) collective-permute-start(bf16[64,512]{1,0:T(8,128)(2,1)S(1)} %collective-permute-done.10), channel_id=1, source_target_pairs={{0,480},{32,0},{64,32},{96,64},{128,96},{160,128},{192,160},{224,1... | collective-permute-start | bytes 196616 | tf_op jit(solution)/shard_map/ppermute | solution.py:73
  126.2 5.1 %collective-permute-start.12 = (bf16[64,512]{1,0:T(8,128)(2,1)S(1)}, bf16[64,512]{1,0:T(8,128)(2,1)S(1)}, u32[]{:S(2)}, u32[]{:S(2)}) collective-permute-start(bf16[64,512]{1,0:T(8,128)(2,1)S(1)} %collective-permute-done.11), channel_id=1, source_target_pairs={{0,480},{32,0},{64,32},{96,64},{128,96},{160,128},{192,160},{224,1... | collective-permute-start | bytes 196616 | tf_op jit(solution)/shard_map/ppermute | solution.py:73
  133.9 5.1 %collective-permute-start.13 = (bf16[64,512]{1,0:T(8,128)(2,1)S(1)}, bf16[64,512]{1,0:T(8,128)(2,1)S(1)}, u32[]{:S(2)}, u32[]{:S(2)}) collective-permute-start(bf16[64,512]{1,0:T(8,128)(2,1)S(1)} %collective-permute-done.12), channel_id=1, source_target_pairs={{0,480},{32,0},{64,32},{96,64},{128,96},{160,128},{192,160},{224,1... | collective-permute-start | bytes 196616 | tf_op jit(solution)/shard_map/ppermute | solution.py:73
  141.6 5.2 %collective-permute-start.14 = (bf16[64,512]{1,0:T(8,128)(2,1)S(1)}, bf16[64,512]{1,0:T(8,128)(2,1)S(1)}, u32[]{:S(2)}, u32[]{:S(2)}) collective-permute-start(bf16[64,512]{1,0:T(8,128)(2,1)S(1)} %collective-permute-done.13), channel_id=1, source_target_pairs={{0,480},{32,0},{64,32},{96,64},{128,96},{160,128},{192,160},{224,1... | collective-permute-start | bytes 196616 | tf_op jit(solution)/shard_map/ppermute | solution.py:73
  149.4 5.1 %collective-permute-done.21 = bf16[64,512]{1,0:T(8,128)(2,1)S(1)} collective-permute-done((bf16[64,512]{1,0:T(8,128)(2,1)S(1)}, bf16[64,512]{1,0:T(8,128)(2,1)S(1)}, u32[]{:S(2)}, u32[]{:S(2)}) %collective-permute-start.21) | collective-permute-done | bytes 65568 | tf_op jit(solution)/shard_map/ppermute | solution.py:70
  157.1 4.8 %collective-permute-done.22 = bf16[64,512]{1,0:T(8,128)(2,1)S(1)} collective-permute-done((bf16[64,512]{1,0:T(8,128)(2,1)S(1)}, bf16[64,512]{1,0:T(8,128)(2,1)S(1)}, u32[]{:S(2)}, u32[]{:S(2)}) %collective-permute-start.22) | collective-permute-done | bytes 65568 | tf_op jit(solution)/shard_map/ppermute | solution.py:70
  168.5 9.7 %all-gather.5.cloned.1.call-done = bf16[2176,256]{1,0:T(8,128)(2,1)} async-done(((bf16[136,256]{1,0:T(8,128)(2,1)}), bf16[2176,256]{1,0:T(8,128)(2,1)}) %all-gather.5.cloned.1.call-update) | async-done | bytes 1114128 | tf_op jit(solution)/shard_map/all_gather | solution.py:59
  184.9 9.1 %collective-permute-done.26 = bf16[1024,512]{1,0:T(8,128)(2,1)} collective-permute-done((bf16[1024,512]{1,0:T(8,128)(2,1)S(1)}, bf16[1024,512]{1,0:T(8,128)(2,1)}, u32[]{:S(2)}, u32[]{:S(2)}) %collective-permute-start.26) | collective-permute-done | bytes 1048608 | tf_op jit(solution)/shard_map/ppermute | solution.py:55
  198.8 13.9 %collective-permute-done.6 = bf16[2176,256]{1,0:T(8,128)(2,1)S(1)} collective-permute-done((bf16[2176,256]{1,0:T(8,128)(2,1)}, bf16[2176,256]{1,0:T(8,128)(2,1)S(1)}, u32[]{:S(2)}, u32[]{:S(2)}) %collective-permute-start.6) | collective-permute-done | bytes 1114144 | tf_op jit(solution)/shard_map/ppermute | solution.py:55
  236.2 4.0 %collective-permute-done.24 = f32[128,512]{0,1:T(8,128)} collective-permute-done((f32[128,512]{0,1:T(8,128)}, f32[128,512]{0,1:T(8,128)}, u32[]{:S(2)}, u32[]{:S(2)}) %collective-permute-start.24) | collective-permute-done | bytes 262176 | tf_op jit(solution)/shard_map/ppermute | solution.py:162
  240.2 3.7 %collective-permute-done.25 = f32[128,512]{0,1:T(8,128)} collective-permute-done((f32[128,512]{0,1:T(8,128)}, f32[128,512]{0,1:T(8,128)}, u32[]{:S(2)}, u32[]{:S(2)}) %collective-permute-start.25) | collective-permute-done | bytes 262176 | tf_op jit(solution)/shard_map/ppermute | solution.py:162
  250.6 11.3 %pad_maximum_fusion = bf16[8704,256]{1,0:T(8,128)(2,1)S(1)} fusion(bf16[4352,256]{1,0:T(8,128)(2,1)} %collective-permute-done.7, bf16[2176,256]{1,0:T(8,128)(2,1)S(1)} %copy-done.2, bf16[2176,256]{1,0:T(8,128)(2,1)S(1)} %copy-done), kind=kLoop, calls=%fused_computation.14 | loop fusion | flops 13369344 | bytes 8912896 | tf_op jit(solution)/shard_map/concatenate | solution.py:55
  271.2 4.5 %fusion.65 = (f32[2,4,64]{2,1,0:T(4,128)S(1)}, bf16[2,4,64,2112]{3,2,1,0:T(8,128)(2,1)}) fusion(pred[2,64,2112]{2,1,0:T(8,128)(4,1)S(1)} %compare_and_fusion, bf16[2,2112,256]{2,1,0:T(8,128)(2,1)S(1)} %bitcast.154, bf16[2,64,4,64]{3,1,2,0:T(8,128)(2,1)} %copy.54, bf16[2,64,4,64]{3,1,2,0:T(8,128)(2,1)} %copy.53), kind=kOutput, calls=%fused_computation.175 | convolution fusion | flops 283576384 | bytes 3934208 | tf_op jit(solution)/shard_map/sub | solution.py:212
  293.8 13.8 %collective-permute-done.28 = bf16[128,4,512]{0,2,1:T(8,128)(2,1)} collective-permute-done((bf16[128,4,512]{0,2,1:T(8,128)(2,1)}, bf16[128,4,512]{0,2,1:T(8,128)(2,1)}, u32[]{:S(2)}, u32[]{:S(2)}) %collective-permute-start.28) | collective-permute-done | bytes 524320 | tf_op jit(solution)/shard_map/ppermute | solution.py:112
  313.4 4.8 %collective-permute-start.30 = (bf16[128,512]{0,1:T(8,128)(2,1)S(1)}, bf16[128,512]{0,1:T(8,128)(2,1)S(1)}, u32[]{:S(2)}, u32[]{:S(2)}) collective-permute-start(bf16[128,512]{0,1:T(8,128)(2,1)S(1)} %get-tuple-element.51), channel_id=1, source_target_pairs={{0,4},{2,6},{4,0},{6,2},{1,5},{3,7},{5,1},{7,3},{8,12},{10,14},{12... | collective-permute-start | bytes 393224 | tf_op jit(solution)/shard_map/ppermute | solution.py:116
  328.7 6.4 %psum.22 = f32[2,512]{1,0:T(2,128)S(1)} all-reduce(f32[2,512]{1,0:T(2,128)S(1)} %psum.21), channel_id=1, replica_groups=mesh['z'=16,'xh'=2,'c'=2,'y'=4,'xl'=2] {'xh'}, use_global_device_ids=true, to_apply=%region_12.16 | all-reduce | flops 1024 | bytes 8192 | tf_op jit(solution)/shard_map/psum | solution.py:245
  335.2 27.0 %psum.23 = f32[2,512]{1,0:T(2,128)S(1)} all-reduce(f32[2,512]{1,0:T(2,128)S(1)} %psum.22), channel_id=1, replica_groups=mesh['z'=16,'xh'=2,'c'=2,'y'=4,'xl'=2] {'z'}, use_global_device_ids=true, to_apply=%region_13.17 | all-reduce | flops 1024 | bytes 8192 | tf_op jit(solution)/shard_map/psum | solution.py:245
  (204 shorter events, 136.3 us)
Async XLA Ops:
  7.2 84.2 %all-gather.3.cloned.1.call-start = ((), (), s32[]{:S(2)}) async-start(), calls=%async_computation | async-start | bytes 1671168 | tf_op jit(solution)/shard_map/all_gather | solution.py:59
  7.2 95.3 %collective-permute-start.8 = (bf16[64,512]{1,0:T(8,128)(2,1)}, bf16[64,512]{1,0:T(8,128)(2,1)S(1)}, u32[]{:S(2)}, u32[]{:S(2)}) collective-permute-start(bf16[64,512]{1,0:T(8,128)(2,1)} %param.17), channel_id=1, source_target_pairs={{0,480},{32,0},{64,32},{96,64},{128,96},{160,128},{192,160},{224,1... | collective-permute-start | bytes 196616 | tf_op jit(solution)/shard_map/ppermute | solution.py:73
  18.6 88.5 %collective-permute-start.15 = (bf16[64,512]{1,0:T(8,128)(2,1)}, bf16[64,512]{1,0:T(8,128)(2,1)S(1)}, u32[]{:S(2)}, u32[]{:S(2)}) collective-permute-start(bf16[64,512]{1,0:T(8,128)(2,1)} %param.17), channel_id=1, source_target_pairs={{0,32},{32,64},{64,96},{96,128},{128,160},{160,192},{192,224},{224... | collective-permute-start | bytes 196616 | tf_op jit(solution)/shard_map/ppermute | solution.py:70
  22.1 156.1 %all-gather.5.cloned.1.call-start = ((), (), s32[]{:S(2)}) async-start(), calls=%async_computation.1 | async-start | bytes 1183744 | tf_op jit(solution)/shard_map/all_gather | solution.py:59
  25.4 12.3 %collective-permute-start = (bf16[128,1024]{0,1:T(8,128)(2,1)S(1)}, bf16[128,1024]{0,1:T(8,128)(2,1)S(1)}, u32[]{:S(2)}, u32[]{:S(2)}) collective-permute-start(bf16[128,1024]{0,1:T(8,128)(2,1)S(1)} %get-tuple-element.58), channel_id=1, source_target_pairs={{0,8},{8,0},{16,24},{24,16},{1,9},{9,1},{17,25},{25,17},{2,10},{10... | collective-permute-start | bytes 786440 | tf_op jit(solution)/shard_map/ppermute | solution.py:153
  27.3 12.5 %collective-permute-start.1 = (bf16[128,1024]{0,1:T(8,128)(2,1)S(1)}, bf16[128,1024]{0,1:T(8,128)(2,1)S(1)}, u32[]{:S(2)}, u32[]{:S(2)}) collective-permute-start(bf16[128,1024]{0,1:T(8,128)(2,1)S(1)} %get-tuple-element.57), channel_id=1, source_target_pairs={{0,16},{8,24},{16,0},{24,8},{1,17},{9,25},{17,1},{25,9},{2,18},{10... | collective-permute-start | bytes 786440 | tf_op jit(solution)/shard_map/ppermute | solution.py:153
  30.6 14.0 %collective-permute-start.2 = (bf16[128,1024]{0,1:T(8,128)(2,1)S(1)}, bf16[128,1024]{0,1:T(8,128)(2,1)S(1)}, u32[]{:S(2)}, u32[]{:S(2)}) collective-permute-start(bf16[128,1024]{0,1:T(8,128)(2,1)S(1)} %get-tuple-element.56), channel_id=1, source_target_pairs={{0,24},{8,16},{16,8},{24,0},{1,25},{9,17},{17,9},{25,1},{2,26},{10... | collective-permute-start | bytes 786440 | tf_op jit(solution)/shard_map/ppermute | solution.py:153
  93.1 16.0 %collective-permute-start.3 = (f32[128,256]{0,1:T(8,128)S(1)}, f32[128,256]{0,1:T(8,128)S(1)}, u32[]{:S(2)}, u32[]{:S(2)}) collective-permute-start(f32[128,256]{0,1:T(8,128)S(1)} %get-tuple-element.59), channel_id=1, source_target_pairs={{0,8},{8,0},{16,24},{24,16},{1,9},{9,1},{17,25},{25,17},{2,10},{10... | collective-permute-start | bytes 393224 | tf_op jit(solution)/shard_map/ppermute | solution.py:162
  95.0 14.1 %collective-permute-start.4 = (f32[128,256]{0,1:T(8,128)S(1)}, f32[128,256]{0,1:T(8,128)S(1)}, u32[]{:S(2)}, u32[]{:S(2)}) collective-permute-start(f32[128,256]{0,1:T(8,128)S(1)} %get-tuple-element.61), channel_id=1, source_target_pairs={{0,16},{8,24},{16,0},{24,8},{1,17},{9,25},{17,1},{25,9},{2,18},{10... | collective-permute-start | bytes 393224 | tf_op jit(solution)/shard_map/ppermute | solution.py:162
  98.4 10.7 %collective-permute-start.5 = (f32[128,256]{0,1:T(8,128)S(1)}, f32[128,256]{0,1:T(8,128)S(1)}, u32[]{:S(2)}, u32[]{:S(2)}) collective-permute-start(f32[128,256]{0,1:T(8,128)S(1)} %get-tuple-element.60), channel_id=1, source_target_pairs={{0,24},{8,16},{16,8},{24,0},{1,25},{9,17},{17,9},{25,1},{2,26},{10... | collective-permute-start | bytes 393224 | tf_op jit(solution)/shard_map/ppermute | solution.py:162
  102.5 8.3 %collective-permute-start.9 = (bf16[64,512]{1,0:T(8,128)(2,1)S(1)}, bf16[64,512]{1,0:T(8,128)(2,1)S(1)}, u32[]{:S(2)}, u32[]{:S(2)}) collective-permute-start(bf16[64,512]{1,0:T(8,128)(2,1)S(1)} %collective-permute-done.8), channel_id=1, source_target_pairs={{0,480},{32,0},{64,32},{96,64},{128,96},{160,128},{192,160},{224,1... | collective-permute-start | bytes 196616 | tf_op jit(solution)/shard_map/ppermute | solution.py:73
  107.1 8.8 %collective-permute-start.16 = (bf16[64,512]{1,0:T(8,128)(2,1)S(1)}, bf16[64,512]{1,0:T(8,128)(2,1)S(1)}, u32[]{:S(2)}, u32[]{:S(2)}) collective-permute-start(bf16[64,512]{1,0:T(8,128)(2,1)S(1)} %collective-permute-done.15), channel_id=1, source_target_pairs={{0,32},{32,64},{64,96},{96,128},{128,160},{160,192},{192,224},{224... | collective-permute-start | bytes 196616 | tf_op jit(solution)/shard_map/ppermute | solution.py:70
  139.0 7.8 %collective-permute-start.20 = (bf16[64,512]{1,0:T(8,128)(2,1)S(1)}, bf16[64,512]{1,0:T(8,128)(2,1)S(1)}, u32[]{:S(2)}, u32[]{:S(2)}) collective-permute-start(bf16[64,512]{1,0:T(8,128)(2,1)S(1)} %collective-permute-done.19), channel_id=1, source_target_pairs={{0,32},{32,64},{64,96},{96,128},{128,160},{160,192},{192,224},{224... | collective-permute-start | bytes 196616 | tf_op jit(solution)/shard_map/ppermute | solution.py:70
  141.6 14.8 %collective-permute-start.14 = (bf16[64,512]{1,0:T(8,128)(2,1)S(1)}, bf16[64,512]{1,0:T(8,128)(2,1)S(1)}, u32[]{:S(2)}, u32[]{:S(2)}) collective-permute-start(bf16[64,512]{1,0:T(8,128)(2,1)S(1)} %collective-permute-done.13), channel_id=1, source_target_pairs={{0,480},{32,0},{64,32},{96,64},{128,96},{160,128},{192,160},{224,1... | collective-permute-start | bytes 196616 | tf_op jit(solution)/shard_map/ppermute | solution.py:73
  164.4 29.6 %collective-permute-start.26 = (bf16[1024,512]{1,0:T(8,128)(2,1)S(1)}, bf16[1024,512]{1,0:T(8,128)(2,1)}, u32[]{:S(2)}, u32[]{:S(2)}) collective-permute-start(bf16[1024,512]{1,0:T(8,128)(2,1)S(1)} %slice.166), channel_id=1, source_target_pairs={{0,16},{16,0},{1,17},{17,1},{2,18},{18,2},{3,19},{19,3},{4,20},{20... | collective-permute-start | bytes 3145736 | tf_op jit(solution)/shard_map/ppermute | solution.py:55
  178.2 34.4 %collective-permute-start.6 = (bf16[2176,256]{1,0:T(8,128)(2,1)}, bf16[2176,256]{1,0:T(8,128)(2,1)S(1)}, u32[]{:S(2)}, u32[]{:S(2)}) collective-permute-start(bf16[2176,256]{1,0:T(8,128)(2,1)} %all-gather.5.cloned.1.call-done), channel_id=1, source_target_pairs={{0,16},{16,0},{1,17},{17,1},{2,18},{18,2},{3,19},{19,3},{4,20},{20... | collective-permute-start | bytes 3342344 | tf_op jit(solution)/shard_map/ppermute | solution.py:55
  196.7 50.2 %collective-permute-start.27 = (bf16[2048,512]{1,0:T(8,128)(2,1)}, bf16[2048,512]{1,0:T(8,128)(2,1)}, u32[]{:S(2)}, u32[]{:S(2)}) collective-permute-start(bf16[2048,512]{1,0:T(8,128)(2,1)} %pad_maximum_fusion.3), channel_id=1, source_target_pairs={{0,8},{8,0},{1,9},{9,1},{2,10},{10,2},{3,11},{11,3},{4,12},{12,4},... | collective-permute-start | bytes 6291464 | tf_op jit(solution)/shard_map/ppermute | solution.py:55
  214.4 36.2 %collective-permute-start.7 = (bf16[4352,256]{1,0:T(8,128)(2,1)}, bf16[4352,256]{1,0:T(8,128)(2,1)}, u32[]{:S(2)}, u32[]{:S(2)}) collective-permute-start(bf16[4352,256]{1,0:T(8,128)(2,1)} %pad_maximum_fusion.2), channel_id=1, source_target_pairs={{0,8},{8,0},{1,9},{9,1},{2,10},{10,2},{3,11},{11,3},{4,12},{12,4},... | collective-permute-start | bytes 6684680 | tf_op jit(solution)/shard_map/ppermute | solution.py:55
  224.9 11.3 %collective-permute-start.23 = (f32[128,512]{0,1:T(8,128)}, f32[128,512]{0,1:T(8,128)S(1)}, u32[]{:S(2)}, u32[]{:S(2)}) collective-permute-start(f32[128,512]{0,1:T(8,128)} %get-tuple-element.52), channel_id=1, source_target_pairs={{0,8},{8,0},{16,24},{24,16},{1,9},{9,1},{17,25},{25,17},{2,10},{10... | collective-permute-start | bytes 786440 | tf_op jit(solution)/shard_map/ppermute | solution.py:162
  227.3 12.9 %collective-permute-start.24 = (f32[128,512]{0,1:T(8,128)}, f32[128,512]{0,1:T(8,128)}, u32[]{:S(2)}, u32[]{:S(2)}) collective-permute-start(f32[128,512]{0,1:T(8,128)} %get-tuple-element.54), channel_id=1, source_target_pairs={{0,16},{8,24},{16,0},{24,8},{1,17},{9,25},{17,1},{25,9},{2,18},{10... | collective-permute-start | bytes 786440 | tf_op jit(solution)/shard_map/ppermute | solution.py:162
  230.8 13.1 %collective-permute-start.25 = (f32[128,512]{0,1:T(8,128)}, f32[128,512]{0,1:T(8,128)}, u32[]{:S(2)}, u32[]{:S(2)}) collective-permute-start(f32[128,512]{0,1:T(8,128)} %get-tuple-element.53), channel_id=1, source_target_pairs={{0,24},{8,16},{16,8},{24,0},{1,25},{9,17},{17,9},{25,1},{2,26},{10... | collective-permute-start | bytes 786440 | tf_op jit(solution)/shard_map/ppermute | solution.py:162
  290.9 16.8 %collective-permute-start.28 = (bf16[128,4,512]{0,2,1:T(8,128)(2,1)}, bf16[128,4,512]{0,2,1:T(8,128)(2,1)}, u32[]{:S(2)}, u32[]{:S(2)}) collective-permute-start(bf16[128,4,512]{0,2,1:T(8,128)(2,1)} %bitcast_convert_fusion), channel_id=1, source_target_pairs={{0,1},{1,0},{2,3},{3,2},{4,5},{5,4},{6,7},{7,6},{8,9},{9,8},{10,11... | collective-permute-start | bytes 1572872 | tf_op jit(solution)/shard_map/ppermute | solution.py:112
  309.9 13.0 %collective-permute-start.29 = (bf16[128,512]{0,1:T(8,128)(2,1)S(1)}, bf16[128,512]{0,1:T(8,128)(2,1)S(1)}, u32[]{:S(2)}, u32[]{:S(2)}) collective-permute-start(bf16[128,512]{0,1:T(8,128)(2,1)S(1)} %get-tuple-element.49), channel_id=1, source_target_pairs={{0,2},{2,4},{4,6},{6,0},{1,3},{3,5},{5,7},{7,1},{8,10},{10,12},{12... | collective-permute-start | bytes 393224 | tf_op jit(solution)/shard_map/ppermute | solution.py:116
  313.4 9.5 %collective-permute-start.30 = (bf16[128,512]{0,1:T(8,128)(2,1)S(1)}, bf16[128,512]{0,1:T(8,128)(2,1)S(1)}, u32[]{:S(2)}, u32[]{:S(2)}) collective-permute-start(bf16[128,512]{0,1:T(8,128)(2,1)S(1)} %get-tuple-element.51), channel_id=1, source_target_pairs={{0,4},{2,6},{4,0},{6,2},{1,5},{3,7},{5,1},{7,3},{8,12},{10,14},{12... | collective-permute-start | bytes 393224 | tf_op jit(solution)/shard_map/ppermute | solution.py:116
  (34 other events, 650.2 us)
Sparse Core Ops, SparseCore 0:
  22.2 69.1 all-gather.2
  110.3 67.8 all-gather.4

commit v9 on v7

--- a/solution.py
+++ b/solution.py
@@ -140,9 +140,12 @@
         ]
         stacked = jnp.concatenate([jnp.take(quarters, me, axis=1)] + theirs, axis=0)
         parts = jnp.dot(stacked, w_proj, preferred_element_type=jnp.float32)
-        proj = parts[:tok_rows]
-        for k, perm in enumerate(perms):
-            proj = proj + lax.ppermute(parts[(k + 1) * tok_rows : (k + 2) * tok_rows], pair, perm)
+        rows = tok_rows
+        on_chip = lax.ppermute(
+            jnp.concatenate([parts[rows : 2 * rows], parts[3 * rows : 4 * rows]]), pair, perms[0]
+        )
+        across = lax.ppermute(parts[2 * rows : 3 * rows] + on_chip[rows:], pair, perms[1])
+        proj = parts[:rows] + on_chip[:rows] + across
         queries = proj[:, :q_cols].reshape(tok_rows, group_size, HEAD_DIM)
         key_proj = proj[:, q_cols : q_cols + kv_cols]
         value_proj = proj[:, q_cols + kv_cols :].astype(jnp.bfloat16)

time: 347 us -> 341 us (0.983)
  starting transfers between devices: 42.7 us -> 38.7 us
    ppermute x3 -> x2, starting transfers between devices: 9.08 us -> 5.28 us  [the longest x1 3.36 us: local(): lax.ppermute(parts[2 * rows:3 * rows] + on_chip[rows:], pair, perms[1])]
    ppermute x3 -> x2, waiting for transfers between devices: 15.7 us -> 12.4 us  [the longest x1 11 us: local(): lax.ppermute(parts[2 * rows:3 * rows] + on_chip[rows:], pair, perms[1])]
  transfers between devices with their start and end apart: 16 -> 15, of which waited for: 9 -> 9; matrix products, arithmetic and copies ran while one was open for 6% -> 6% of each run, Pallas kernels for 0% -> 0%
where the time goes in v9:
time: 341 us; the launch traced here: 340 us
  waiting for transfers between devices  173 us (51%)
  starting transfers between devices  38.7 us (11%)
  blocking collectives  38.2 us (11%)
  other arithmetic  38.1 us (11%)
  local copies, waits for them, and re-layouts  23.5 us (7%)
  between operations  15.4 us (5%)
  matrix products  12.8 us (4%)
    all_gather x2, waiting for transfers between devices, gather_z(): return lax.all_gather(x, 'z', axis=0, tiled=True)  122 us
    psum x3, blocking collectives, local(): sums = lax.psum(sums, axis)  38.2 us
    concatenate x4, other arithmetic, swap_cat(): return jnp.concatenate([x, lax.ppermute(x, axis_name, [(0, 1), (1, 0)])], 0)  19.3 us
    ppermute x1, waiting for transfers between devices, reduce_scatter_head(): lax.ppermute(sent, 'xl', [(0, 1), (1, 0)]).astype(jnp.float32)  14.3 us
    ppermute x4, waiting for transfers between devices, swap_cat(): return jnp.concatenate([x, lax.ppermute(x, axis_name, [(0, 1), (1, 0)])], 0)  12.7 us
    ppermute x3, starting transfers between devices, reduce_scatter_head(): lax.ppermute(piece, 'y', [(i, (i + shift) % ny) for i in range(ny)])  11.3 us
    ppermute x1, waiting for transfers between devices, local(): lax.ppermute(parts[2 * rows:3 * rows] + on_chip[rows:], pair, perms[1])  11 us
    ppermute x4, starting transfers between devices, swap_cat(): return jnp.concatenate([x, lax.ppermute(x, axis_name, [(0, 1), (1, 0)])], 0)  10.7 us
  transfers between devices with their start and end apart: 15, of which 9 were waited for; matrix products, arithmetic and copies ran while one was open for 6% of the time, Pallas kernels for 0%

profile of v9, /device:TPU:6, one launch (start us, length us, event | category | flops | bytes accessed | tf_op | source)
XLA Modules:
  0.0 340.1 jit_solution(14610306532192259415)
XLA Ops:
  14.0 3.3 collective-permute-start.1
  17.3 3.9 %collective-permute-start.2 = (bf16[128,1024]{0,1:T(8,128)(2,1)S(1)}, bf16[128,1024]{0,1:T(8,128)(2,1)}, u32[]{:S(2)}, u32[]{:S(2)}) collective-permute-start(bf16[128,1024]{0,1:T(8,128)(2,1)S(1)} %get-tuple-element.59), channel_id=1, source_target_pairs={{0,24},{8,16},{16,8},{24,0},{1,25},{9,17},{17,9},{25,1},{2,26},{10... | collective-permute-start | bytes 786440 | tf_op jit(solution)/shard_map/ppermute | solution.py:138
  21.2 5.3 %collective-permute-done.1 = bf16[128,1024]{0,1:T(8,128)(2,1)S(1)} collective-permute-done((bf16[128,1024]{0,1:T(8,128)(2,1)S(1)}, bf16[128,1024]{0,1:T(8,128)(2,1)S(1)}, u32[]{:S(2)}, u32[]{:S(2)}) %collective-permute-start.1) | collective-permute-done | bytes 262176 | tf_op jit(solution)/shard_map/ppermute | solution.py:138
  26.5 4.9 %collective-permute-done.2 = bf16[128,1024]{0,1:T(8,128)(2,1)} collective-permute-done((bf16[128,1024]{0,1:T(8,128)(2,1)S(1)}, bf16[128,1024]{0,1:T(8,128)(2,1)}, u32[]{:S(2)}, u32[]{:S(2)}) %collective-permute-start.2) | collective-permute-done | bytes 262176 | tf_op jit(solution)/shard_map/ppermute | solution.py:138
  31.4 58.1 %all-gather.3.cloned.1.call-done = bf16[1024,1280]{1,0:T(8,128)(2,1)} async-done(((bf16[64,1280]{1,0:T(8,128)(2,1)}), bf16[1024,1280]{1,0:T(8,128)(2,1)}) %all-gather.3.cloned.1.call-update) | async-done | bytes 2621456 | tf_op jit(solution)/shard_map/all_gather | solution.py:59
  97.5 3.4 collective-permute-start.4
  101.1 11.0 %collective-permute-done.4 = f32[128,768]{0,1:T(8,128)S(1)} collective-permute-done((f32[128,768]{0,1:T(8,128)S(1)}, f32[128,768]{0,1:T(8,128)S(1)}, u32[]{:S(2)}, u32[]{:S(2)}) %collective-permute-start.4) | collective-permute-done | bytes 393248 | tf_op jit(solution)/shard_map/ppermute | solution.py:147
  116.8 3.4 collective-permute-start.7
  120.2 63.7 %all-gather.5.cloned.1.call-done = bf16[2176,256]{1,0:T(8,128)(2,1)} async-done(((bf16[136,256]{1,0:T(8,128)(2,1)}), bf16[2176,256]{1,0:T(8,128)(2,1)}) %all-gather.5.cloned.1.call-update) | async-done | bytes 1114128 | tf_op jit(solution)/shard_map/all_gather | solution.py:59
  183.9 3.4 collective-permute-start.5
  187.3 2.7 pad_maximum_fusion.3
  192.0 12.7 %collective-permute-done.5 = bf16[2176,256]{1,0:T(8,128)(2,1)S(1)} collective-permute-done((bf16[2176,256]{1,0:T(8,128)(2,1)}, bf16[2176,256]{1,0:T(8,128)(2,1)S(1)}, u32[]{:S(2)}, u32[]{:S(2)}) %collective-permute-start.5) | collective-permute-done | bytes 1114144 | tf_op jit(solution)/shard_map/ppermute | solution.py:55
  214.3 3.6 %pad_maximum_fusion.1 = bf16[4096,512]{1,0:T(8,128)(2,1)} fusion(bf16[2048,512]{1,0:T(8,128)(2,1)} %collective-permute-done.8, bf16[1024,512]{1,0:T(8,128)(2,1)} %collective-permute-done.7, bf16[1024,512]{1,0:T(8,128)(2,1)S(1)} %slice.159), kind=kLoop, calls=%fused_computation.14 | loop fusion | flops 12582912 | bytes 8388608 | tf_op jit(solution)/shard_map/concatenate | solution.py:55
  217.9 11.3 %pad_maximum_fusion = bf16[8704,256]{1,0:T(8,128)(2,1)S(1)} fusion(bf16[4352,256]{1,0:T(8,128)(2,1)} %collective-permute-done.6, bf16[2176,256]{1,0:T(8,128)(2,1)S(1)} %copy-done.2, bf16[2176,256]{1,0:T(8,128)(2,1)S(1)} %copy-done), kind=kLoop, calls=%fused_computation.13 | loop fusion | flops 13369344 | bytes 8912896 | tf_op jit(solution)/shard_map/concatenate | solution.py:55
  235.2 2.9 gather_fusion.2
  238.5 4.5 %fusion.63 = (f32[2,4,64]{2,1,0:T(4,128)S(1)}, bf16[2,4,64,2112]{3,2,1,0:T(8,128)(2,1)}) fusion(pred[2,64,2112]{2,1,0:T(8,128)(4,1)S(1)} %compare_and_fusion, bf16[2,2112,256]{2,1,0:T(8,128)(2,1)S(1)} %bitcast.117, bf16[2,64,4,64]{3,1,2,0:T(8,128)(2,1)} %copy.98, bf16[2,64,4,64]{3,1,2,0:T(8,128)(2,1)} %copy.97), kind=kOutput, calls=%fused_computation.145 | convolution fusion | flops 283576384 | bytes 3934208 | tf_op jit(solution)/shard_map/sub | solution.py:192
  245.6 3.4 %fusion.40 = f32[128,2,2,16,64]{0,4,3,2,1:T(8,128)S(1)} fusion(bf16[2,2,16,64,512]{4,3,2,1,0:T(8,128)(2,1)} %bitcast.111, bf16[128,512,1,1,1]{1,0,2,3,4:T(8,128)(2,1)S(1)} %reshape.594), kind=kOutput, calls=%fused_computation.71 | convolution fusion | flops 536870912 | bytes 6422528 | tf_op jit(solution)/shard_map/tk,jdk->tjd/dot_general | solution.py:203
  251.1 3.3 select_bitcast_fusion.1
  260.4 14.3 %collective-permute-done.9 = bf16[128,4,512]{0,2,1:T(8,128)(2,1)} collective-permute-done((bf16[128,4,512]{0,2,1:T(8,128)(2,1)}, bf16[128,4,512]{0,2,1:T(8,128)(2,1)}, u32[]{:S(2)}, u32[]{:S(2)}) %collective-permute-start.9) | collective-permute-done | bytes 524320 | tf_op jit(solution)/shard_map/ppermute | solution.py:97
  276.9 3.4 collective-permute-start.10
  280.3 4.6 %collective-permute-start.11 = (bf16[128,512]{0,1:T(8,128)(2,1)S(1)}, bf16[128,512]{0,1:T(8,128)(2,1)S(1)}, u32[]{:S(2)}, u32[]{:S(2)}) collective-permute-start(bf16[128,512]{0,1:T(8,128)(2,1)S(1)} %get-tuple-element.57), channel_id=1, source_target_pairs={{0,4},{2,6},{4,0},{6,2},{1,5},{3,7},{5,1},{7,3},{8,12},{10,14},{12... | collective-permute-start | bytes 393224 | tf_op jit(solution)/shard_map/ppermute | solution.py:101
  284.9 3.3 collective-permute-start.12
  295.5 6.4 %psum.22 = f32[2,512]{1,0:T(2,128)S(1)} all-reduce(f32[2,512]{1,0:T(2,128)S(1)} %psum.21), channel_id=1, replica_groups=mesh['z'=16,'xh'=2,'c'=2,'y'=4,'xl'=2] {'xh'}, use_global_device_ids=true, to_apply=%region_12.16 | all-reduce | flops 1024 | bytes 8192 | tf_op jit(solution)/shard_map/psum | solution.py:225
  301.9 29.3 %psum.23 = f32[2,512]{1,0:T(2,128)S(1)} all-reduce(f32[2,512]{1,0:T(2,128)S(1)} %psum.22), channel_id=1, replica_groups=mesh['z'=16,'xh'=2,'c'=2,'y'=4,'xl'=2] {'z'}, use_global_device_ids=true, to_apply=%region_13.17 | all-reduce | flops 1024 | bytes 8192 | tf_op jit(solution)/shard_map/psum | solution.py:225
  (124 shorter events, 58.6 us)
Async XLA Ops:
  7.2 4.0 %copy-start.5 = (f32[4096]{0:T(1024)S(1)}, f32[4096]{0:T(1024)}, u32[]{:S(2)}) copy-start(f32[4096]{0:T(1024)} %param.16) | copy-start | bytes 49156
  7.2 82.3 %all-gather.3.cloned.1.call-start = ((), (), s32[]{:S(2)}) async-start(), calls=%async_computation | async-start | bytes 2785280 | tf_op jit(solution)/shard_map/all_gather | solution.py:59
  8.8 175.0 %all-gather.5.cloned.1.call-start = ((), (), s32[]{:S(2)}) async-start(), calls=%async_computation.1 | async-start | bytes 1183744 | tf_op jit(solution)/shard_map/all_gather | solution.py:59
  12.1 9.1 %collective-permute-start = (bf16[128,1024]{0,1:T(8,128)(2,1)S(1)}, bf16[128,1024]{0,1:T(8,128)(2,1)S(1)}, u32[]{:S(2)}, u32[]{:S(2)}) collective-permute-start(bf16[128,1024]{0,1:T(8,128)(2,1)S(1)} %get-tuple-element.61), channel_id=1, source_target_pairs={{0,8},{8,0},{16,24},{24,16},{1,9},{9,1},{17,25},{25,17},{2,10},{10... | collective-permute-start | bytes 786440 | tf_op jit(solution)/shard_map/ppermute | solution.py:138
  14.0 12.5 %collective-permute-start.1 = (bf16[128,1024]{0,1:T(8,128)(2,1)S(1)}, bf16[128,1024]{0,1:T(8,128)(2,1)S(1)}, u32[]{:S(2)}, u32[]{:S(2)}) collective-permute-start(bf16[128,1024]{0,1:T(8,128)(2,1)S(1)} %get-tuple-element.60), channel_id=1, source_target_pairs={{0,16},{8,24},{16,0},{24,8},{1,17},{9,25},{17,1},{25,9},{2,18},{10... | collective-permute-start | bytes 786440 | tf_op jit(solution)/shard_map/ppermute | solution.py:138
  17.3 14.1 %collective-permute-start.2 = (bf16[128,1024]{0,1:T(8,128)(2,1)S(1)}, bf16[128,1024]{0,1:T(8,128)(2,1)}, u32[]{:S(2)}, u32[]{:S(2)}) collective-permute-start(bf16[128,1024]{0,1:T(8,128)(2,1)S(1)} %get-tuple-element.59), channel_id=1, source_target_pairs={{0,24},{8,16},{16,8},{24,0},{1,25},{9,17},{17,9},{25,1},{2,26},{10... | collective-permute-start | bytes 786440 | tf_op jit(solution)/shard_map/ppermute | solution.py:138
  92.0 2.3 copy-start.9
  92.2 4.3 %collective-permute-start.3 = (f32[256,768]{0,1:T(8,128)S(1)}, f32[256,768]{0,1:T(8,128)}, u32[]{:S(2)}, u32[]{:S(2)}) collective-permute-start(f32[256,768]{0,1:T(8,128)S(1)} %pad_maximum_fusion.4), channel_id=1, source_target_pairs={{0,8},{8,0},{16,24},{24,16},{1,9},{9,1},{17,25},{25,17},{2,10},{10... | collective-permute-start | bytes 2359304 | tf_op jit(solution)/shard_map/ppermute | solution.py:144
  97.5 14.6 %collective-permute-start.4 = (f32[128,768]{0,1:T(8,128)S(1)}, f32[128,768]{0,1:T(8,128)S(1)}, u32[]{:S(2)}, u32[]{:S(2)}) collective-permute-start(f32[128,768]{0,1:T(8,128)S(1)} %slice_add_fusion), channel_id=1, source_target_pairs={{0,16},{8,24},{16,0},{24,8},{1,17},{9,25},{17,1},{25,9},{2,18},{10... | collective-permute-start | bytes 1179656 | tf_op jit(solution)/shard_map/ppermute | solution.py:147
  116.8 70.4 %collective-permute-start.7 = (bf16[1024,512]{1,0:T(8,128)(2,1)S(1)}, bf16[1024,512]{1,0:T(8,128)(2,1)}, u32[]{:S(2)}, u32[]{:S(2)}) collective-permute-start(bf16[1024,512]{1,0:T(8,128)(2,1)S(1)} %slice.159), channel_id=1, source_target_pairs={{0,16},{16,0},{1,17},{17,1},{2,18},{18,2},{3,19},{19,3},{4,20},{20... | collective-permute-start | bytes 3145736 | tf_op jit(solution)/shard_map/ppermute | solution.py:55
  183.9 20.9 %copy-start = (bf16[2176,256]{1,0:T(8,128)(2,1)S(1)}, bf16[2176,256]{1,0:T(8,128)(2,1)}, u32[]{:S(2)}) copy-start(bf16[2176,256]{1,0:T(8,128)(2,1)} %all-gather.5.cloned.1.call-done) | copy-start | bytes 3342340
  183.9 20.9 %collective-permute-start.5 = (bf16[2176,256]{1,0:T(8,128)(2,1)}, bf16[2176,256]{1,0:T(8,128)(2,1)S(1)}, u32[]{:S(2)}, u32[]{:S(2)}) collective-permute-start(bf16[2176,256]{1,0:T(8,128)(2,1)} %all-gather.5.cloned.1.call-done), channel_id=1, source_target_pairs={{0,16},{16,0},{1,17},{17,1},{2,18},{18,2},{3,19},{19,3},{4,20},{20... | collective-permute-start | bytes 3342344 | tf_op jit(solution)/shard_map/ppermute | solution.py:55
  190.0 20.2 %slice-start = ((f32[128,768]{0,1:T(8,128)}), f32[128,512]{0,1:T(8,128)S(1)}, s32[]{:S(2)}) async-start(f32[128,768]{0,1:T(8,128)} %copy-done.4), calls=%async_computation.2 | async-start | bytes 524288 | tf_op jit(solution)/shard_map/slice | solution.py:149
  190.0 24.3 %collective-permute-start.8 = (bf16[2048,512]{1,0:T(8,128)(2,1)}, bf16[2048,512]{1,0:T(8,128)(2,1)}, u32[]{:S(2)}, u32[]{:S(2)}) collective-permute-start(bf16[2048,512]{1,0:T(8,128)(2,1)} %pad_maximum_fusion.3), channel_id=1, source_target_pairs={{0,8},{8,0},{1,9},{9,1},{2,10},{10,2},{3,11},{11,3},{4,12},{12,4},... | collective-permute-start | bytes 6291464 | tf_op jit(solution)/shard_map/ppermute | solution.py:55
  206.5 11.4 %collective-permute-start.6 = (bf16[4352,256]{1,0:T(8,128)(2,1)}, bf16[4352,256]{1,0:T(8,128)(2,1)}, u32[]{:S(2)}, u32[]{:S(2)}) collective-permute-start(bf16[4352,256]{1,0:T(8,128)(2,1)} %pad_maximum_fusion.2), channel_id=1, source_target_pairs={{0,8},{8,0},{1,9},{9,1},{2,10},{10,2},{3,11},{11,3},{4,12},{12,4},... | collective-permute-start | bytes 6684680 | tf_op jit(solution)/shard_map/ppermute | solution.py:55
  214.3 3.6 %copy-start.2 = (bf16[2176,256]{1,0:T(8,128)(2,1)S(1)}, bf16[2176,256]{1,0:T(8,128)(2,1)}, u32[]{:S(2)}) copy-start(bf16[2176,256]{1,0:T(8,128)(2,1)} %copy-done.1) | copy-start | bytes 3342340
  235.2 3.0 copy-start.12
  257.3 31.0 %copy-start.13 = (s32[32]{0:T(128)S(1)}, s32[32]{0:T(128)}, u32[]{:S(2)}) copy-start(s32[32]{0:T(128)} %param.23) | copy-start | bytes 388
  257.3 32.4 %copy-start.10 = (s32[128]{0:T(128)S(1)}, s32[128]{0:T(128)}, u32[]{:S(2)}) copy-start(s32[128]{0:T(128)} %param.21) | copy-start | bytes 1540
  257.3 32.4 %copy-start.11 = (s32[32]{0:T(128)S(1)}, s32[32]{0:T(128)}, u32[]{:S(2)}) copy-start(s32[32]{0:T(128)} %get-tuple-element.76) | copy-start | bytes 388
  258.2 16.5 %collective-permute-start.9 = (bf16[128,4,512]{0,2,1:T(8,128)(2,1)}, bf16[128,4,512]{0,2,1:T(8,128)(2,1)}, u32[]{:S(2)}, u32[]{:S(2)}) collective-permute-start(bf16[128,4,512]{0,2,1:T(8,128)(2,1)} %bitcast_convert_fusion), channel_id=1, source_target_pairs={{0,1},{1,0},{2,3},{3,2},{4,5},{5,4},{6,7},{7,6},{8,9},{9,8},{10,11... | collective-permute-start | bytes 1572872 | tf_op jit(solution)/shard_map/ppermute | solution.py:97
  276.9 12.9 %collective-permute-start.10 = (bf16[128,512]{0,1:T(8,128)(2,1)S(1)}, bf16[128,512]{0,1:T(8,128)(2,1)S(1)}, u32[]{:S(2)}, u32[]{:S(2)}) collective-permute-start(bf16[128,512]{0,1:T(8,128)(2,1)S(1)} %get-tuple-element.55), channel_id=1, source_target_pairs={{0,2},{2,4},{4,6},{6,0},{1,3},{3,5},{5,7},{7,1},{8,10},{10,12},{12... | collective-permute-start | bytes 393224 | tf_op jit(solution)/shard_map/ppermute | solution.py:101
  280.3 9.5 %collective-permute-start.11 = (bf16[128,512]{0,1:T(8,128)(2,1)S(1)}, bf16[128,512]{0,1:T(8,128)(2,1)S(1)}, u32[]{:S(2)}, u32[]{:S(2)}) collective-permute-start(bf16[128,512]{0,1:T(8,128)(2,1)S(1)} %get-tuple-element.57), channel_id=1, source_target_pairs={{0,4},{2,6},{4,0},{6,2},{1,5},{3,7},{5,1},{7,3},{8,12},{10,14},{12... | collective-permute-start | bytes 393224 | tf_op jit(solution)/shard_map/ppermute | solution.py:101
  284.9 6.9 %collective-permute-start.12 = (bf16[128,512]{0,1:T(8,128)(2,1)S(1)}, bf16[128,512]{0,1:T(8,128)(2,1)S(1)}, u32[]{:S(2)}, u32[]{:S(2)}) collective-permute-start(bf16[128,512]{0,1:T(8,128)(2,1)S(1)} %get-tuple-element.56), channel_id=1, source_target_pairs={{0,6},{2,0},{4,2},{6,4},{1,7},{3,1},{5,3},{7,5},{8,14},{10,8},{12,... | collective-permute-start | bytes 393224 | tf_op jit(solution)/shard_map/ppermute | solution.py:101
  (6 other events, 9.9 us)
Sparse Core Ops, SparseCore 0:
  10.1 79.3 all-gather.2
  115.7 68.1 all-gather.4

commit v10 on v9

--- a/solution.py
+++ b/solution.py
@@ -161,7 +161,7 @@
         kv = gather_pair(gather_z(kv_buf)).reshape(nctx, tok_rows + 8, 2 * kv_cols)
         pos_code = kv[:, tok_rows, :].astype(jnp.int32)
         key_pos_all = pos_code[:, :tok_rows] * RUN + pos_code[:, tok_rows:]
-        kv_halves = kv[:, :tok_rows].reshape(total_runs, RUN, 2 * kv_cols)
+        kv_rows = kv.reshape(nctx * (tok_rows + 8), 2 * kv_cols)
         pos_halves = key_pos_all.reshape(total_runs, RUN)
         run_of_half = pos_halves[:, 0] // RUN
         half_of_run = jnp.zeros((total_runs,), jnp.int32).at[run_of_half].set(
@@ -174,7 +174,9 @@
         first_run = jnp.maximum(q_run - (win_runs - 1), 0)
         win = first_run[:, None] + jnp.arange(win_runs, dtype=jnp.int32)[None, :]
         win_halves = half_of_run[win]
-        kv_win = kv_halves[win_halves].reshape(runs_here, win_runs * RUN, 2 * kv_cols)
+        win_first = (win_halves // 2) * (tok_rows + 8) + (win_halves % 2) * RUN
+        win_rows = win_first[..., None] + jnp.arange(RUN, dtype=jnp.int32)
+        kv_win = kv_rows[win_rows].reshape(runs_here, win_runs * RUN, 2 * kv_cols)
         k_pos = pos_halves[win_halves].reshape(runs_here, win_runs * RUN)
         k_win = kv_win[..., :kv_cols]
         v_win = kv_win[..., kv_cols:]

time: 341 us -> 344 us (level)
  local copies, waits for them, and re-layouts: 23.5 us -> 35.5 us
  other arithmetic: 38.1 us -> 28.4 us
    concatenate x4 -> x3, other arithmetic: 19.3 us -> 8.06 us  [swap_cat(): return jnp.concatenate([x, lax.ppermute(x, axis_name, [(0, 1), (1, 0)])], 0)]
    gather x1, local copies, waits for them, and re-layouts: 2.89 us -> 13.6 us  [local(): kv_win = kv_rows[win_rows].reshape(runs_here, win_runs * RUN, 2 * kv_cols)]
    unnamed x31 -> x33, local copies, waits for them, and re-layouts: 4.27 us -> 7.57 us
where the time goes in v10:
time: 344 us; the launch traced here: 343 us
  waiting for transfers between devices  174 us (51%)
  starting transfers between devices  38.5 us (11%)
  blocking collectives  37.8 us (11%)
  local copies, waits for them, and re-layouts  35.5 us (10%)
  other arithmetic  28.4 us (8%)
  between operations  15.4 us (4%)
  matrix products  13.5 us (4%)
    all_gather x2, waiting for transfers between devices, gather_z(): return lax.all_gather(x, 'z', axis=0, tiled=True)  122 us
    psum x3, blocking collectives, local(): sums = lax.psum(sums, axis)  37.8 us
    ppermute x1, waiting for transfers between devices, reduce_scatter_head(): lax.ppermute(sent, 'xl', [(0, 1), (1, 0)]).astype(jnp.float32)  14.2 us
    ppermute x4, waiting for transfers between devices, swap_cat(): return jnp.concatenate([x, lax.ppermute(x, axis_name, [(0, 1), (1, 0)])], 0)  14 us
    gather x1, local copies, waits for them, and re-layouts, local(): kv_win = kv_rows[win_rows].reshape(runs_here, win_runs * RUN, 2 * kv_cols)  13.6 us
    ppermute x3, starting transfers between devices, reduce_scatter_head(): lax.ppermute(piece, 'y', [(i, (i + shift) % ny) for i in range(ny)])  11.4 us
    ppermute x1, waiting for transfers between devices, local(): lax.ppermute(parts[2 * rows:3 * rows] + on_chip[rows:], pair, perms[1])  11 us
    ppermute x4, starting transfers between devices, swap_cat(): return jnp.concatenate([x, lax.ppermute(x, axis_name, [(0, 1), (1, 0)])], 0)  10.4 us
  transfers between devices with their start and end apart: 15, of which 9 were waited for; matrix products, arithmetic and copies ran while one was open for 6% of the time, Pallas kernels for 0%

profile of v10, /device:TPU:6, one launch (start us, length us, event | category | flops | bytes accessed | tf_op | source)
XLA Modules:
  0.0 343.2 jit_solution(10009434483830612406)
XLA Ops:
  14.0 3.3 collective-permute-start.1
  17.3 3.9 %collective-permute-start.2 = (bf16[128,1024]{0,1:T(8,128)(2,1)S(1)}, bf16[128,1024]{0,1:T(8,128)(2,1)}, u32[]{:S(2)}, u32[]{:S(2)}) collective-permute-start(bf16[128,1024]{0,1:T(8,128)(2,1)S(1)} %get-tuple-element.59), channel_id=1, source_target_pairs={{0,24},{8,16},{16,8},{24,0},{1,25},{9,17},{17,9},{25,1},{2,26},{10... | collective-permute-start | bytes 786440 | tf_op jit(solution)/shard_map/ppermute | solution.py:138
  21.2 5.3 %collective-permute-done.1 = bf16[128,1024]{0,1:T(8,128)(2,1)S(1)} collective-permute-done((bf16[128,1024]{0,1:T(8,128)(2,1)S(1)}, bf16[128,1024]{0,1:T(8,128)(2,1)S(1)}, u32[]{:S(2)}, u32[]{:S(2)}) %collective-permute-start.1) | collective-permute-done | bytes 262176 | tf_op jit(solution)/shard_map/ppermute | solution.py:138
  27.2 4.2 %collective-permute-done.2 = bf16[128,1024]{0,1:T(8,128)(2,1)} collective-permute-done((bf16[128,1024]{0,1:T(8,128)(2,1)S(1)}, bf16[128,1024]{0,1:T(8,128)(2,1)}, u32[]{:S(2)}, u32[]{:S(2)}) %collective-permute-start.2) | collective-permute-done | bytes 262176 | tf_op jit(solution)/shard_map/ppermute | solution.py:138
  31.4 58.1 %all-gather.3.cloned.1.call-done = bf16[1024,1280]{1,0:T(8,128)(2,1)} async-done(((bf16[64,1280]{1,0:T(8,128)(2,1)}), bf16[1024,1280]{1,0:T(8,128)(2,1)}) %all-gather.3.cloned.1.call-update) | async-done | bytes 2621456 | tf_op jit(solution)/shard_map/all_gather | solution.py:59
  98.8 3.4 collective-permute-start.4
  102.3 11.0 %collective-permute-done.4 = f32[128,768]{0,1:T(8,128)S(1)} collective-permute-done((f32[128,768]{0,1:T(8,128)S(1)}, f32[128,768]{0,1:T(8,128)S(1)}, u32[]{:S(2)}, u32[]{:S(2)}) %collective-permute-start.4) | collective-permute-done | bytes 393248 | tf_op jit(solution)/shard_map/ppermute | solution.py:147
  117.3 3.4 collective-permute-start.7
  120.7 63.7 %all-gather.5.cloned.1.call-done = bf16[2176,256]{1,0:T(8,128)(2,1)} async-done(((bf16[136,256]{1,0:T(8,128)(2,1)}), bf16[2176,256]{1,0:T(8,128)(2,1)}) %all-gather.5.cloned.1.call-update) | async-done | bytes 1114128 | tf_op jit(solution)/shard_map/all_gather | solution.py:59
  184.4 3.2 collective-permute-start.5
  191.1 14.0 %collective-permute-done.5 = bf16[2176,256]{1,0:T(8,128)(2,1)} collective-permute-done((bf16[2176,256]{1,0:T(8,128)(2,1)}, bf16[2176,256]{1,0:T(8,128)(2,1)}, u32[]{:S(2)}, u32[]{:S(2)}) %collective-permute-start.5) | collective-permute-done | bytes 1114144 | tf_op jit(solution)/shard_map/ppermute | solution.py:55
  205.1 3.1 pad_maximum_fusion.1
  214.9 3.5 %pad_maximum_fusion = bf16[4096,512]{1,0:T(8,128)(2,1)} fusion(bf16[2048,512]{1,0:T(8,128)(2,1)} %collective-permute-done.8, bf16[1024,512]{1,0:T(8,128)(2,1)S(1)} %collective-permute-done.7, bf16[1024,512]{1,0:T(8,128)(2,1)S(1)} %slice.154), kind=kLoop, calls=%fused_computation.13 | loop fusion | flops 12582912 | bytes 8388608 | tf_op jit(solution)/shard_map/concatenate | solution.py:55
  226.6 13.6 %gather_fusion.2 = bf16[4224,256]{1,0:T(8,128)(2,1)} fusion(bf16[8704,256]{1,0:T(8,128)(2,1)} %copy-done, s32[5120]{0:T(1024)S(1)} %pad_clamp_fusion), kind=kCustom, calls=%fused_computation.2 | custom fusion | bytes 4342272 | tf_op jit(solution)/shard_map/gather | solution.py:179
  241.4 4.8 %fusion.65 = (f32[2,4,64]{2,1,0:T(4,128)S(1)}, bf16[2,4,64,2112]{3,2,1,0:T(8,128)(2,1)}) fusion(pred[2,64,2112]{2,1,0:T(8,128)(4,1)S(1)} %compare_and_fusion, bf16[2,2112,256]{2,1,0:T(8,128)(2,1)} %bitcast.116, bf16[2,64,4,64]{3,1,2,0:T(8,128)(2,1)S(1)} %copy.100, bf16[2,64,4,64]{3,1,2,0:T(8,128)(2,1)S(1)} %copy-done.3), kind=kOutput, calls=%fused_computation.156 | convolution fusion | flops 283576384 | bytes 4065280 | tf_op jit(solution)/shard_map/sub | solution.py:194
  246.2 2.6 fusion.19
  249.0 3.4 %fusion.40 = f32[128,2,2,16,64]{0,4,3,2,1:T(8,128)S(1)} fusion(bf16[2,2,16,64,512]{4,3,2,1,0:T(8,128)(2,1)} %bitcast.111, bf16[128,512,1,1,1]{1,0,2,3,4:T(8,128)(2,1)S(1)} %reshape.635), kind=kOutput, calls=%fused_computation.70 | convolution fusion | flops 536870912 | bytes 6422528 | tf_op jit(solution)/shard_map/tk,jdk->tjd/dot_general | solution.py:205
  254.5 3.3 select_bitcast_fusion.1
  264.0 14.2 %collective-permute-done.9 = bf16[128,4,512]{0,2,1:T(8,128)(2,1)} collective-permute-done((bf16[128,4,512]{0,2,1:T(8,128)(2,1)}, bf16[128,4,512]{0,2,1:T(8,128)(2,1)}, u32[]{:S(2)}, u32[]{:S(2)}) %collective-permute-start.9) | collective-permute-done | bytes 524320 | tf_op jit(solution)/shard_map/ppermute | solution.py:97
  280.3 3.4 collective-permute-start.10
  283.8 4.6 %collective-permute-start.11 = (bf16[128,512]{0,1:T(8,128)(2,1)S(1)}, bf16[128,512]{0,1:T(8,128)(2,1)S(1)}, u32[]{:S(2)}, u32[]{:S(2)}) collective-permute-start(bf16[128,512]{0,1:T(8,128)(2,1)S(1)} %get-tuple-element.57), channel_id=1, source_target_pairs={{0,4},{2,6},{4,0},{6,2},{1,5},{3,7},{5,1},{7,3},{8,12},{10,14},{12... | collective-permute-start | bytes 393224 | tf_op jit(solution)/shard_map/ppermute | solution.py:101
  288.4 3.3 collective-permute-start.12
  298.9 6.4 %psum.22 = f32[2,512]{1,0:T(2,128)S(1)} all-reduce(f32[2,512]{1,0:T(2,128)S(1)} %psum.21), channel_id=1, replica_groups=mesh['z'=16,'xh'=2,'c'=2,'y'=4,'xl'=2] {'xh'}, use_global_device_ids=true, to_apply=%region_12.16 | all-reduce | flops 1024 | bytes 8192 | tf_op jit(solution)/shard_map/psum | solution.py:227
  305.4 28.9 %psum.23 = f32[2,512]{1,0:T(2,128)S(1)} all-reduce(f32[2,512]{1,0:T(2,128)S(1)} %psum.22), channel_id=1, replica_groups=mesh['z'=16,'xh'=2,'c'=2,'y'=4,'xl'=2] {'z'}, use_global_device_ids=true, to_apply=%region_13.17 | all-reduce | flops 1024 | bytes 8192 | tf_op jit(solution)/shard_map/psum | solution.py:227
  (129 shorter events, 59.1 us)
Async XLA Ops:
  7.2 4.0 %copy-start.4 = (f32[4096]{0:T(1024)S(1)}, f32[4096]{0:T(1024)}, u32[]{:S(2)}) copy-start(f32[4096]{0:T(1024)} %param.16) | copy-start | bytes 49156
  7.2 82.3 %all-gather.3.cloned.1.call-start = ((), (), s32[]{:S(2)}) async-start(), calls=%async_computation | async-start | bytes 2785280 | tf_op jit(solution)/shard_map/all_gather | solution.py:59
  8.8 175.5 %all-gather.5.cloned.1.call-start = ((), (), s32[]{:S(2)}) async-start(), calls=%async_computation.1 | async-start | bytes 1183744 | tf_op jit(solution)/shard_map/all_gather | solution.py:59
  12.1 9.1 %collective-permute-start = (bf16[128,1024]{0,1:T(8,128)(2,1)S(1)}, bf16[128,1024]{0,1:T(8,128)(2,1)S(1)}, u32[]{:S(2)}, u32[]{:S(2)}) collective-permute-start(bf16[128,1024]{0,1:T(8,128)(2,1)S(1)} %get-tuple-element.61), channel_id=1, source_target_pairs={{0,8},{8,0},{16,24},{24,16},{1,9},{9,1},{17,25},{25,17},{2,10},{10... | collective-permute-start | bytes 786440 | tf_op jit(solution)/shard_map/ppermute | solution.py:138
  14.0 12.5 %collective-permute-start.1 = (bf16[128,1024]{0,1:T(8,128)(2,1)S(1)}, bf16[128,1024]{0,1:T(8,128)(2,1)S(1)}, u32[]{:S(2)}, u32[]{:S(2)}) collective-permute-start(bf16[128,1024]{0,1:T(8,128)(2,1)S(1)} %get-tuple-element.60), channel_id=1, source_target_pairs={{0,16},{8,24},{16,0},{24,8},{1,17},{9,25},{17,1},{25,9},{2,18},{10... | collective-permute-start | bytes 786440 | tf_op jit(solution)/shard_map/ppermute | solution.py:138
  17.3 14.1 %collective-permute-start.2 = (bf16[128,1024]{0,1:T(8,128)(2,1)S(1)}, bf16[128,1024]{0,1:T(8,128)(2,1)}, u32[]{:S(2)}, u32[]{:S(2)}) collective-permute-start(bf16[128,1024]{0,1:T(8,128)(2,1)S(1)} %get-tuple-element.59), channel_id=1, source_target_pairs={{0,24},{8,16},{16,8},{24,0},{1,25},{9,17},{17,9},{25,1},{2,26},{10... | collective-permute-start | bytes 786440 | tf_op jit(solution)/shard_map/ppermute | solution.py:138
  92.1 3.0 copy-start.7
  92.1 3.3 copy-start.8
  93.2 4.5 %collective-permute-start.3 = (f32[256,768]{0,1:T(8,128)}, f32[256,768]{0,1:T(8,128)}, u32[]{:S(2)}, u32[]{:S(2)}) collective-permute-start(f32[256,768]{0,1:T(8,128)} %pad_maximum_fusion.3), channel_id=1, source_target_pairs={{0,8},{8,0},{16,24},{24,16},{1,9},{9,1},{17,25},{25,17},{2,10},{10... | collective-permute-start | bytes 2359304 | tf_op jit(solution)/shard_map/ppermute | solution.py:144
  98.8 14.6 %collective-permute-start.4 = (f32[128,768]{0,1:T(8,128)S(1)}, f32[128,768]{0,1:T(8,128)S(1)}, u32[]{:S(2)}, u32[]{:S(2)}) collective-permute-start(f32[128,768]{0,1:T(8,128)S(1)} %slice_add_fusion), channel_id=1, source_target_pairs={{0,16},{8,24},{16,0},{24,8},{1,17},{9,25},{17,1},{25,9},{2,18},{10... | collective-permute-start | bytes 1179656 | tf_op jit(solution)/shard_map/ppermute | solution.py:147
  117.3 70.3 %collective-permute-start.7 = (bf16[1024,512]{1,0:T(8,128)(2,1)S(1)}, bf16[1024,512]{1,0:T(8,128)(2,1)S(1)}, u32[]{:S(2)}, u32[]{:S(2)}) collective-permute-start(bf16[1024,512]{1,0:T(8,128)(2,1)S(1)} %slice.154), channel_id=1, source_target_pairs={{0,16},{16,0},{1,17},{17,1},{2,18},{18,2},{3,19},{19,3},{4,20},{20... | collective-permute-start | bytes 3145736 | tf_op jit(solution)/shard_map/ppermute | solution.py:55
  184.4 20.7 %collective-permute-start.5 = (bf16[2176,256]{1,0:T(8,128)(2,1)}, bf16[2176,256]{1,0:T(8,128)(2,1)}, u32[]{:S(2)}, u32[]{:S(2)}) collective-permute-start(bf16[2176,256]{1,0:T(8,128)(2,1)} %all-gather.5.cloned.1.call-done), channel_id=1, source_target_pairs={{0,16},{16,0},{1,17},{17,1},{2,18},{18,2},{3,19},{19,3},{4,20},{20... | collective-permute-start | bytes 3342344 | tf_op jit(solution)/shard_map/ppermute | solution.py:55
  189.1 25.8 %collective-permute-start.8 = (bf16[2048,512]{1,0:T(8,128)(2,1)}, bf16[2048,512]{1,0:T(8,128)(2,1)}, u32[]{:S(2)}, u32[]{:S(2)}) collective-permute-start(bf16[2048,512]{1,0:T(8,128)(2,1)} %pad_maximum_fusion.2), channel_id=1, source_target_pairs={{0,8},{8,0},{1,9},{9,1},{2,10},{10,2},{3,11},{11,3},{4,12},{12,4},... | collective-permute-start | bytes 6291464 | tf_op jit(solution)/shard_map/ppermute | solution.py:55
  208.2 11.6 %collective-permute-start.6 = (bf16[4352,256]{1,0:T(8,128)(2,1)}, bf16[4352,256]{1,0:T(8,128)(2,1)}, u32[]{:S(2)}, u32[]{:S(2)}) collective-permute-start(bf16[4352,256]{1,0:T(8,128)(2,1)} %pad_maximum_fusion.1), channel_id=1, source_target_pairs={{0,8},{8,0},{1,9},{9,1},{2,10},{10,2},{3,11},{11,3},{4,12},{12,4},... | collective-permute-start | bytes 6684680 | tf_op jit(solution)/shard_map/ppermute | solution.py:55
  214.9 3.5 %copy-start.1 = (bf16[2176,256]{1,0:T(8,128)(2,1)S(1)}, bf16[2176,256]{1,0:T(8,128)(2,1)}, u32[]{:S(2)}) copy-start(bf16[2176,256]{1,0:T(8,128)(2,1)} %all-gather.5.cloned.1.call-done) | copy-start | bytes 3342340
  226.6 14.5 %copy-start.11 = (s32[2,64]{1,0:T(2,128)S(1)}, s32[2,64]{1,0:T(2,128)}, u32[]{:S(2)}) copy-start(s32[2,64]{1,0:T(2,128)} %ge.64) | copy-start | bytes 1540
  226.6 14.8 %copy-start.3 = (bf16[2,64,4,64]{3,1,2,0:T(8,128)(2,1)S(1)}, bf16[2,64,4,64]{3,1,2,0:T(8,128)(2,1)}, u32[]{:S(2)}) copy-start(bf16[2,64,4,64]{3,1,2,0:T(8,128)(2,1)} %copy.99) | copy-start | bytes 196612
  260.7 31.1 %copy-start.13 = (s32[32]{0:T(128)S(1)}, s32[32]{0:T(128)}, u32[]{:S(2)}) copy-start(s32[32]{0:T(128)} %param.23) | copy-start | bytes 388
  260.7 32.4 %copy-start.9 = (s32[128]{0:T(128)S(1)}, s32[128]{0:T(128)}, u32[]{:S(2)}) copy-start(s32[128]{0:T(128)} %param.21) | copy-start | bytes 1540
  260.7 32.4 %copy-start.10 = (s32[32]{0:T(128)S(1)}, s32[32]{0:T(128)}, u32[]{:S(2)}) copy-start(s32[32]{0:T(128)} %get-tuple-element.76) | copy-start | bytes 388
  261.6 16.5 %collective-permute-start.9 = (bf16[128,4,512]{0,2,1:T(8,128)(2,1)}, bf16[128,4,512]{0,2,1:T(8,128)(2,1)}, u32[]{:S(2)}, u32[]{:S(2)}) collective-permute-start(bf16[128,4,512]{0,2,1:T(8,128)(2,1)} %bitcast_convert_fusion), channel_id=1, source_target_pairs={{0,1},{1,0},{2,3},{3,2},{4,5},{5,4},{6,7},{7,6},{8,9},{9,8},{10,11... | collective-permute-start | bytes 1572872 | tf_op jit(solution)/shard_map/ppermute | solution.py:97
  280.3 12.9 %collective-permute-start.10 = (bf16[128,512]{0,1:T(8,128)(2,1)S(1)}, bf16[128,512]{0,1:T(8,128)(2,1)S(1)}, u32[]{:S(2)}, u32[]{:S(2)}) collective-permute-start(bf16[128,512]{0,1:T(8,128)(2,1)S(1)} %get-tuple-element.55), channel_id=1, source_target_pairs={{0,2},{2,4},{4,6},{6,0},{1,3},{3,5},{5,7},{7,1},{8,10},{10,12},{12... | collective-permute-start | bytes 393224 | tf_op jit(solution)/shard_map/ppermute | solution.py:101
  283.8 9.5 %collective-permute-start.11 = (bf16[128,512]{0,1:T(8,128)(2,1)S(1)}, bf16[128,512]{0,1:T(8,128)(2,1)S(1)}, u32[]{:S(2)}, u32[]{:S(2)}) collective-permute-start(bf16[128,512]{0,1:T(8,128)(2,1)S(1)} %get-tuple-element.57), channel_id=1, source_target_pairs={{0,4},{2,6},{4,0},{6,2},{1,5},{3,7},{5,1},{7,3},{8,12},{10,14},{12... | collective-permute-start | bytes 393224 | tf_op jit(solution)/shard_map/ppermute | solution.py:101
  288.4 6.9 %collective-permute-start.12 = (bf16[128,512]{0,1:T(8,128)(2,1)S(1)}, bf16[128,512]{0,1:T(8,128)(2,1)S(1)}, u32[]{:S(2)}, u32[]{:S(2)}) collective-permute-start(bf16[128,512]{0,1:T(8,128)(2,1)S(1)} %get-tuple-element.56), channel_id=1, source_target_pairs={{0,6},{2,0},{4,2},{6,4},{1,7},{3,1},{5,3},{7,5},{8,14},{10,8},{12,... | collective-permute-start | bytes 393224 | tf_op jit(solution)/shard_map/ppermute | solution.py:101
  (5 other events, 8.1 us)
Sparse Core Ops, SparseCore 0:
  10.1 79.3 all-gather.2
  116.1 68.1 all-gather.4

commit v11 on v9

--- a/solution.py
+++ b/solution.py
@@ -221,7 +221,7 @@
         sums = jnp.stack(
             [jnp.sum(harm_rows[:, None] * stream, 0), jnp.sum(safe_rows[:, None] * stream, 0)]
         )
-        for axis in ("c", "xh", "z"):
+        for axis in (("xh", "c"), "z"):
             sums = lax.psum(sums, axis)
         refusal_direction = sums[0] / harmful - sums[1] / harmless
         return (residual_out, refusal_direction)

time: 341 us -> 341 us (level)
    psum x3 -> x2, blocking collectives: 38.2 us -> 36.5 us  [local(): sums = lax.psum(sums, axis)]
where the time goes in v11:
time: 341 us; the launch traced here: 338 us
  waiting for transfers between devices  173 us (51%)
  starting transfers between devices  38.7 us (11%)
  other arithmetic  38.1 us (11%)
  blocking collectives  36.5 us (11%)
  local copies, waits for them, and re-layouts  23.5 us (7%)
  between operations  15.4 us (5%)
  matrix products  12.8 us (4%)
    all_gather x2, waiting for transfers between devices, gather_z(): return lax.all_gather(x, 'z', axis=0, tiled=True)  122 us
    psum x2, blocking collectives, local(): sums = lax.psum(sums, axis)  36.5 us
    concatenate x4, other arithmetic, swap_cat(): return jnp.concatenate([x, lax.ppermute(x, axis_name, [(0, 1), (1, 0)])], 0)  19.3 us
    ppermute x1, waiting for transfers between devices, reduce_scatter_head(): lax.ppermute(sent, 'xl', [(0, 1), (1, 0)]).astype(jnp.float32)  14.3 us
    ppermute x4, waiting for transfers between devices, swap_cat(): return jnp.concatenate([x, lax.ppermute(x, axis_name, [(0, 1), (1, 0)])], 0)  12.7 us
    ppermute x3, starting transfers between devices, reduce_scatter_head(): lax.ppermute(piece, 'y', [(i, (i + shift) % ny) for i in range(ny)])  11.4 us
    ppermute x1, waiting for transfers between devices, local(): lax.ppermute(parts[2 * rows:3 * rows] + on_chip[rows:], pair, perms[1])  11 us
    ppermute x4, starting transfers between devices, swap_cat(): return jnp.concatenate([x, lax.ppermute(x, axis_name, [(0, 1), (1, 0)])], 0)  10.7 us
  transfers between devices with their start and end apart: 15, of which 9 were waited for; matrix products, arithmetic and copies ran while one was open for 6% of the time, Pallas kernels for 0%

profile of v11, /device:TPU:6, one launch (start us, length us, event | category | flops | bytes accessed | tf_op | source)
XLA Modules:
  0.0 338.4 jit_solution(16196009366355087545)
XLA Ops:
  14.0 3.3 collective-permute-start.1
  17.3 3.9 %collective-permute-start.2 = (bf16[128,1024]{0,1:T(8,128)(2,1)S(1)}, bf16[128,1024]{0,1:T(8,128)(2,1)}, u32[]{:S(2)}, u32[]{:S(2)}) collective-permute-start(bf16[128,1024]{0,1:T(8,128)(2,1)S(1)} %get-tuple-element.59), channel_id=1, source_target_pairs={{0,24},{8,16},{16,8},{24,0},{1,25},{9,17},{17,9},{25,1},{2,26},{10... | collective-permute-start | bytes 786440 | tf_op jit(solution)/shard_map/ppermute | solution.py:138
  21.2 5.3 %collective-permute-done.1 = bf16[128,1024]{0,1:T(8,128)(2,1)S(1)} collective-permute-done((bf16[128,1024]{0,1:T(8,128)(2,1)S(1)}, bf16[128,1024]{0,1:T(8,128)(2,1)S(1)}, u32[]{:S(2)}, u32[]{:S(2)}) %collective-permute-start.1) | collective-permute-done | bytes 262176 | tf_op jit(solution)/shard_map/ppermute | solution.py:138
  26.5 4.9 %collective-permute-done.2 = bf16[128,1024]{0,1:T(8,128)(2,1)} collective-permute-done((bf16[128,1024]{0,1:T(8,128)(2,1)S(1)}, bf16[128,1024]{0,1:T(8,128)(2,1)}, u32[]{:S(2)}, u32[]{:S(2)}) %collective-permute-start.2) | collective-permute-done | bytes 262176 | tf_op jit(solution)/shard_map/ppermute | solution.py:138
  31.4 58.1 %all-gather.3.cloned.1.call-done = bf16[1024,1280]{1,0:T(8,128)(2,1)} async-done(((bf16[64,1280]{1,0:T(8,128)(2,1)}), bf16[1024,1280]{1,0:T(8,128)(2,1)}) %all-gather.3.cloned.1.call-update) | async-done | bytes 2621456 | tf_op jit(solution)/shard_map/all_gather | solution.py:59
  97.5 3.4 collective-permute-start.4
  101.1 11.0 %collective-permute-done.4 = f32[128,768]{0,1:T(8,128)S(1)} collective-permute-done((f32[128,768]{0,1:T(8,128)S(1)}, f32[128,768]{0,1:T(8,128)S(1)}, u32[]{:S(2)}, u32[]{:S(2)}) %collective-permute-start.4) | collective-permute-done | bytes 393248 | tf_op jit(solution)/shard_map/ppermute | solution.py:147
  116.8 3.4 collective-permute-start.7
  120.2 63.7 %all-gather.5.cloned.1.call-done = bf16[2176,256]{1,0:T(8,128)(2,1)} async-done(((bf16[136,256]{1,0:T(8,128)(2,1)}), bf16[2176,256]{1,0:T(8,128)(2,1)}) %all-gather.5.cloned.1.call-update) | async-done | bytes 1114128 | tf_op jit(solution)/shard_map/all_gather | solution.py:59
  183.9 3.4 %collective-permute-start.5 = (bf16[2176,256]{1,0:T(8,128)(2,1)}, bf16[2176,256]{1,0:T(8,128)(2,1)S(1)}, u32[]{:S(2)}, u32[]{:S(2)}) collective-permute-start(bf16[2176,256]{1,0:T(8,128)(2,1)} %all-gather.5.cloned.1.call-done), channel_id=1, source_target_pairs={{0,16},{16,0},{1,17},{17,1},{2,18},{18,2},{3,19},{19,3},{4,20},{20... | collective-permute-start | bytes 3342344 | tf_op jit(solution)/shard_map/ppermute | solution.py:55
  187.3 2.7 pad_maximum_fusion.3
  192.0 12.7 %collective-permute-done.5 = bf16[2176,256]{1,0:T(8,128)(2,1)S(1)} collective-permute-done((bf16[2176,256]{1,0:T(8,128)(2,1)}, bf16[2176,256]{1,0:T(8,128)(2,1)S(1)}, u32[]{:S(2)}, u32[]{:S(2)}) %collective-permute-start.5) | collective-permute-done | bytes 1114144 | tf_op jit(solution)/shard_map/ppermute | solution.py:55
  214.3 3.6 %pad_maximum_fusion.1 = bf16[4096,512]{1,0:T(8,128)(2,1)} fusion(bf16[2048,512]{1,0:T(8,128)(2,1)} %collective-permute-done.8, bf16[1024,512]{1,0:T(8,128)(2,1)} %collective-permute-done.7, bf16[1024,512]{1,0:T(8,128)(2,1)S(1)} %slice.159), kind=kLoop, calls=%fused_computation.14 | loop fusion | flops 12582912 | bytes 8388608 | tf_op jit(solution)/shard_map/concatenate | solution.py:55
  217.9 11.3 %pad_maximum_fusion = bf16[8704,256]{1,0:T(8,128)(2,1)S(1)} fusion(bf16[4352,256]{1,0:T(8,128)(2,1)} %collective-permute-done.6, bf16[2176,256]{1,0:T(8,128)(2,1)S(1)} %copy-done.2, bf16[2176,256]{1,0:T(8,128)(2,1)S(1)} %copy-done), kind=kLoop, calls=%fused_computation.13 | loop fusion | flops 13369344 | bytes 8912896 | tf_op jit(solution)/shard_map/concatenate | solution.py:55
  235.2 2.9 gather_fusion.2
  238.5 4.5 %fusion.63 = (f32[2,4,64]{2,1,0:T(4,128)S(1)}, bf16[2,4,64,2112]{3,2,1,0:T(8,128)(2,1)}) fusion(pred[2,64,2112]{2,1,0:T(8,128)(4,1)S(1)} %compare_and_fusion, bf16[2,2112,256]{2,1,0:T(8,128)(2,1)S(1)} %bitcast.117, bf16[2,64,4,64]{3,1,2,0:T(8,128)(2,1)} %copy.98, bf16[2,64,4,64]{3,1,2,0:T(8,128)(2,1)} %copy.97), kind=kOutput, calls=%fused_computation.145 | convolution fusion | flops 283576384 | bytes 3934208 | tf_op jit(solution)/shard_map/sub | solution.py:192
  245.6 3.4 %fusion.40 = f32[128,2,2,16,64]{0,4,3,2,1:T(8,128)S(1)} fusion(bf16[2,2,16,64,512]{4,3,2,1,0:T(8,128)(2,1)} %bitcast.111, bf16[128,512,1,1,1]{1,0,2,3,4:T(8,128)(2,1)S(1)} %reshape.594), kind=kOutput, calls=%fused_computation.71 | convolution fusion | flops 536870912 | bytes 6422528 | tf_op jit(solution)/shard_map/tk,jdk->tjd/dot_general | solution.py:203
  251.1 3.3 select_bitcast_fusion.1
  260.4 14.3 %collective-permute-done.9 = bf16[128,4,512]{0,2,1:T(8,128)(2,1)} collective-permute-done((bf16[128,4,512]{0,2,1:T(8,128)(2,1)}, bf16[128,4,512]{0,2,1:T(8,128)(2,1)}, u32[]{:S(2)}, u32[]{:S(2)}) %collective-permute-start.9) | collective-permute-done | bytes 524320 | tf_op jit(solution)/shard_map/ppermute | solution.py:97
  276.9 3.4 %collective-permute-start.10 = (bf16[128,512]{0,1:T(8,128)(2,1)S(1)}, bf16[128,512]{0,1:T(8,128)(2,1)S(1)}, u32[]{:S(2)}, u32[]{:S(2)}) collective-permute-start(bf16[128,512]{0,1:T(8,128)(2,1)S(1)} %get-tuple-element.55), channel_id=1, source_target_pairs={{0,2},{2,4},{4,6},{6,0},{1,3},{3,5},{5,7},{7,1},{8,10},{10,12},{12... | collective-permute-start | bytes 393224 | tf_op jit(solution)/shard_map/ppermute | solution.py:101
  280.3 4.6 %collective-permute-start.11 = (bf16[128,512]{0,1:T(8,128)(2,1)S(1)}, bf16[128,512]{0,1:T(8,128)(2,1)S(1)}, u32[]{:S(2)}, u32[]{:S(2)}) collective-permute-start(bf16[128,512]{0,1:T(8,128)(2,1)S(1)} %get-tuple-element.57), channel_id=1, source_target_pairs={{0,4},{2,6},{4,0},{6,2},{1,5},{3,7},{5,1},{7,3},{8,12},{10,14},{12... | collective-permute-start | bytes 393224 | tf_op jit(solution)/shard_map/ppermute | solution.py:101
  284.9 3.3 collective-permute-start.12
  293.0 7.2 %psum.14 = f32[2,512]{1,0:T(2,128)S(1)} all-reduce(f32[2,512]{1,0:T(2,128)S(1)} %pad_maximum_fusion.12), channel_id=1, replica_groups=mesh['z'=16,'xh'=2,'c'=2,'y'=4,'xl'=2] {'xh','c'}, use_global_device_ids=true, to_apply=%region_11.15 | all-reduce | flops 1024 | bytes 8192 | tf_op jit(solution)/shard_map/psum | solution.py:225
  300.2 29.3 %psum.15 = f32[2,512]{1,0:T(2,128)S(1)} all-reduce(f32[2,512]{1,0:T(2,128)S(1)} %psum.14), channel_id=1, replica_groups=mesh['z'=16,'xh'=2,'c'=2,'y'=4,'xl'=2] {'z'}, use_global_device_ids=true, to_apply=%region_12.16 | all-reduce | flops 1024 | bytes 8192 | tf_op jit(solution)/shard_map/psum | solution.py:225
  (123 shorter events, 56.1 us)
Async XLA Ops:
  7.2 4.0 %copy-start.5 = (f32[4096]{0:T(1024)S(1)}, f32[4096]{0:T(1024)}, u32[]{:S(2)}) copy-start(f32[4096]{0:T(1024)} %param.16) | copy-start | bytes 49156
  7.2 82.3 %all-gather.3.cloned.1.call-start = ((), (), s32[]{:S(2)}) async-start(), calls=%async_computation | async-start | bytes 2785280 | tf_op jit(solution)/shard_map/all_gather | solution.py:59
  8.8 175.0 %all-gather.5.cloned.1.call-start = ((), (), s32[]{:S(2)}) async-start(), calls=%async_computation.1 | async-start | bytes 1183744 | tf_op jit(solution)/shard_map/all_gather | solution.py:59
  12.1 9.1 %collective-permute-start = (bf16[128,1024]{0,1:T(8,128)(2,1)S(1)}, bf16[128,1024]{0,1:T(8,128)(2,1)S(1)}, u32[]{:S(2)}, u32[]{:S(2)}) collective-permute-start(bf16[128,1024]{0,1:T(8,128)(2,1)S(1)} %get-tuple-element.61), channel_id=1, source_target_pairs={{0,8},{8,0},{16,24},{24,16},{1,9},{9,1},{17,25},{25,17},{2,10},{10... | collective-permute-start | bytes 786440 | tf_op jit(solution)/shard_map/ppermute | solution.py:138
  14.0 12.5 %collective-permute-start.1 = (bf16[128,1024]{0,1:T(8,128)(2,1)S(1)}, bf16[128,1024]{0,1:T(8,128)(2,1)S(1)}, u32[]{:S(2)}, u32[]{:S(2)}) collective-permute-start(bf16[128,1024]{0,1:T(8,128)(2,1)S(1)} %get-tuple-element.60), channel_id=1, source_target_pairs={{0,16},{8,24},{16,0},{24,8},{1,17},{9,25},{17,1},{25,9},{2,18},{10... | collective-permute-start | bytes 786440 | tf_op jit(solution)/shard_map/ppermute | solution.py:138
  17.3 14.1 %collective-permute-start.2 = (bf16[128,1024]{0,1:T(8,128)(2,1)S(1)}, bf16[128,1024]{0,1:T(8,128)(2,1)}, u32[]{:S(2)}, u32[]{:S(2)}) collective-permute-start(bf16[128,1024]{0,1:T(8,128)(2,1)S(1)} %get-tuple-element.59), channel_id=1, source_target_pairs={{0,24},{8,16},{16,8},{24,0},{1,25},{9,17},{17,9},{25,1},{2,26},{10... | collective-permute-start | bytes 786440 | tf_op jit(solution)/shard_map/ppermute | solution.py:138
  92.0 2.3 copy-start.9
  92.2 4.3 %collective-permute-start.3 = (f32[256,768]{0,1:T(8,128)S(1)}, f32[256,768]{0,1:T(8,128)}, u32[]{:S(2)}, u32[]{:S(2)}) collective-permute-start(f32[256,768]{0,1:T(8,128)S(1)} %pad_maximum_fusion.4), channel_id=1, source_target_pairs={{0,8},{8,0},{16,24},{24,16},{1,9},{9,1},{17,25},{25,17},{2,10},{10... | collective-permute-start | bytes 2359304 | tf_op jit(solution)/shard_map/ppermute | solution.py:144
  97.5 14.6 %collective-permute-start.4 = (f32[128,768]{0,1:T(8,128)S(1)}, f32[128,768]{0,1:T(8,128)S(1)}, u32[]{:S(2)}, u32[]{:S(2)}) collective-permute-start(f32[128,768]{0,1:T(8,128)S(1)} %slice_add_fusion), channel_id=1, source_target_pairs={{0,16},{8,24},{16,0},{24,8},{1,17},{9,25},{17,1},{25,9},{2,18},{10... | collective-permute-start | bytes 1179656 | tf_op jit(solution)/shard_map/ppermute | solution.py:147
  116.8 70.4 %collective-permute-start.7 = (bf16[1024,512]{1,0:T(8,128)(2,1)S(1)}, bf16[1024,512]{1,0:T(8,128)(2,1)}, u32[]{:S(2)}, u32[]{:S(2)}) collective-permute-start(bf16[1024,512]{1,0:T(8,128)(2,1)S(1)} %slice.159), channel_id=1, source_target_pairs={{0,16},{16,0},{1,17},{17,1},{2,18},{18,2},{3,19},{19,3},{4,20},{20... | collective-permute-start | bytes 3145736 | tf_op jit(solution)/shard_map/ppermute | solution.py:55
  183.9 20.9 %copy-start = (bf16[2176,256]{1,0:T(8,128)(2,1)S(1)}, bf16[2176,256]{1,0:T(8,128)(2,1)}, u32[]{:S(2)}) copy-start(bf16[2176,256]{1,0:T(8,128)(2,1)} %all-gather.5.cloned.1.call-done) | copy-start | bytes 3342340
  183.9 20.9 %collective-permute-start.5 = (bf16[2176,256]{1,0:T(8,128)(2,1)}, bf16[2176,256]{1,0:T(8,128)(2,1)S(1)}, u32[]{:S(2)}, u32[]{:S(2)}) collective-permute-start(bf16[2176,256]{1,0:T(8,128)(2,1)} %all-gather.5.cloned.1.call-done), channel_id=1, source_target_pairs={{0,16},{16,0},{1,17},{17,1},{2,18},{18,2},{3,19},{19,3},{4,20},{20... | collective-permute-start | bytes 3342344 | tf_op jit(solution)/shard_map/ppermute | solution.py:55
  190.0 20.2 %slice-start = ((f32[128,768]{0,1:T(8,128)}), f32[128,512]{0,1:T(8,128)S(1)}, s32[]{:S(2)}) async-start(f32[128,768]{0,1:T(8,128)} %copy-done.4), calls=%async_computation.2 | async-start | bytes 524288 | tf_op jit(solution)/shard_map/slice | solution.py:149
  190.0 24.3 %collective-permute-start.8 = (bf16[2048,512]{1,0:T(8,128)(2,1)}, bf16[2048,512]{1,0:T(8,128)(2,1)}, u32[]{:S(2)}, u32[]{:S(2)}) collective-permute-start(bf16[2048,512]{1,0:T(8,128)(2,1)} %pad_maximum_fusion.3), channel_id=1, source_target_pairs={{0,8},{8,0},{1,9},{9,1},{2,10},{10,2},{3,11},{11,3},{4,12},{12,4},... | collective-permute-start | bytes 6291464 | tf_op jit(solution)/shard_map/ppermute | solution.py:55
  206.5 11.4 %collective-permute-start.6 = (bf16[4352,256]{1,0:T(8,128)(2,1)}, bf16[4352,256]{1,0:T(8,128)(2,1)}, u32[]{:S(2)}, u32[]{:S(2)}) collective-permute-start(bf16[4352,256]{1,0:T(8,128)(2,1)} %pad_maximum_fusion.2), channel_id=1, source_target_pairs={{0,8},{8,0},{1,9},{9,1},{2,10},{10,2},{3,11},{11,3},{4,12},{12,4},... | collective-permute-start | bytes 6684680 | tf_op jit(solution)/shard_map/ppermute | solution.py:55
  214.3 3.6 %copy-start.2 = (bf16[2176,256]{1,0:T(8,128)(2,1)S(1)}, bf16[2176,256]{1,0:T(8,128)(2,1)}, u32[]{:S(2)}) copy-start(bf16[2176,256]{1,0:T(8,128)(2,1)} %copy-done.1) | copy-start | bytes 3342340
  235.2 3.0 copy-start.12
  257.3 31.0 %copy-start.13 = (s32[32]{0:T(128)S(1)}, s32[32]{0:T(128)}, u32[]{:S(2)}) copy-start(s32[32]{0:T(128)} %param.23) | copy-start | bytes 388
  257.3 32.4 %copy-start.10 = (s32[128]{0:T(128)S(1)}, s32[128]{0:T(128)}, u32[]{:S(2)}) copy-start(s32[128]{0:T(128)} %param.21) | copy-start | bytes 1540
  257.3 32.4 %copy-start.11 = (s32[32]{0:T(128)S(1)}, s32[32]{0:T(128)}, u32[]{:S(2)}) copy-start(s32[32]{0:T(128)} %get-tuple-element.76) | copy-start | bytes 388
  258.2 16.5 %collective-permute-start.9 = (bf16[128,4,512]{0,2,1:T(8,128)(2,1)}, bf16[128,4,512]{0,2,1:T(8,128)(2,1)}, u32[]{:S(2)}, u32[]{:S(2)}) collective-permute-start(bf16[128,4,512]{0,2,1:T(8,128)(2,1)} %bitcast_convert_fusion), channel_id=1, source_target_pairs={{0,1},{1,0},{2,3},{3,2},{4,5},{5,4},{6,7},{7,6},{8,9},{9,8},{10,11... | collective-permute-start | bytes 1572872 | tf_op jit(solution)/shard_map/ppermute | solution.py:97
  276.9 12.9 %collective-permute-start.10 = (bf16[128,512]{0,1:T(8,128)(2,1)S(1)}, bf16[128,512]{0,1:T(8,128)(2,1)S(1)}, u32[]{:S(2)}, u32[]{:S(2)}) collective-permute-start(bf16[128,512]{0,1:T(8,128)(2,1)S(1)} %get-tuple-element.55), channel_id=1, source_target_pairs={{0,2},{2,4},{4,6},{6,0},{1,3},{3,5},{5,7},{7,1},{8,10},{10,12},{12... | collective-permute-start | bytes 393224 | tf_op jit(solution)/shard_map/ppermute | solution.py:101
  280.3 9.5 %collective-permute-start.11 = (bf16[128,512]{0,1:T(8,128)(2,1)S(1)}, bf16[128,512]{0,1:T(8,128)(2,1)S(1)}, u32[]{:S(2)}, u32[]{:S(2)}) collective-permute-start(bf16[128,512]{0,1:T(8,128)(2,1)S(1)} %get-tuple-element.57), channel_id=1, source_target_pairs={{0,4},{2,6},{4,0},{6,2},{1,5},{3,7},{5,1},{7,3},{8,12},{10,14},{12... | collective-permute-start | bytes 393224 | tf_op jit(solution)/shard_map/ppermute | solution.py:101
  284.9 6.9 %collective-permute-start.12 = (bf16[128,512]{0,1:T(8,128)(2,1)S(1)}, bf16[128,512]{0,1:T(8,128)(2,1)S(1)}, u32[]{:S(2)}, u32[]{:S(2)}) collective-permute-start(bf16[128,512]{0,1:T(8,128)(2,1)S(1)} %get-tuple-element.56), channel_id=1, source_target_pairs={{0,6},{2,0},{4,2},{6,4},{1,7},{3,1},{5,3},{7,5},{8,14},{10,8},{12,... | collective-permute-start | bytes 393224 | tf_op jit(solution)/shard_map/ppermute | solution.py:101
  (6 other events, 9.9 us)
Sparse Core Ops, SparseCore 0:
  10.1 79.3 all-gather.2
  115.7 68.1 all-gather.4

commit v12 on v7

--- a/solution.py
+++ b/solution.py
@@ -140,9 +140,11 @@
         ]
         stacked = jnp.concatenate([jnp.take(quarters, me, axis=1)] + theirs, axis=0)
         parts = jnp.dot(stacked, w_proj, preferred_element_type=jnp.float32)
-        proj = parts[:tok_rows]
-        for k, perm in enumerate(perms):
-            proj = proj + lax.ppermute(parts[(k + 1) * tok_rows : (k + 2) * tok_rows], pair, perm)
+        rows = tok_rows
+        for_relay = lax.ppermute(parts[3 * rows : 4 * rows], pair, perms[0])
+        across = lax.ppermute(parts[2 * rows : 3 * rows] + for_relay, pair, perms[1])
+        on_chip = lax.ppermute(parts[rows : 2 * rows], pair, perms[0])
+        proj = parts[:rows] + on_chip + across
         queries = proj[:, :q_cols].reshape(tok_rows, group_size, HEAD_DIM)
         key_proj = proj[:, q_cols : q_cols + kv_cols]
         value_proj = proj[:, q_cols + kv_cols :].astype(jnp.bfloat16)

time: 347 us -> 342 us (0.986)
  no operation moved by 1% of the time
where the time goes in v12:
time: 342 us; the launch traced here: 341 us
  waiting for transfers between devices  173 us (51%)
  starting transfers between devices  41.1 us (12%)
  blocking collectives  38.2 us (11%)
  other arithmetic  36.9 us (11%)
  local copies, waits for them, and re-layouts  23.6 us (7%)
  between operations  15.4 us (5%)
  matrix products  12.9 us (4%)
    all_gather x2, waiting for transfers between devices, gather_z(): return lax.all_gather(x, 'z', axis=0, tiled=True)  121 us
    psum x3, blocking collectives, local(): sums = lax.psum(sums, axis)  38.2 us
    concatenate x4, other arithmetic, swap_cat(): return jnp.concatenate([x, lax.ppermute(x, axis_name, [(0, 1), (1, 0)])], 0)  19.3 us
    ppermute x1, waiting for transfers between devices, reduce_scatter_head(): lax.ppermute(sent, 'xl', [(0, 1), (1, 0)]).astype(jnp.float32)  14.2 us
    ppermute x4, waiting for transfers between devices, swap_cat(): return jnp.concatenate([x, lax.ppermute(x, axis_name, [(0, 1), (1, 0)])], 0)  12.7 us
    ppermute x1, waiting for transfers between devices, local(): across = lax.ppermute(parts[2 * rows:3 * rows] + for_relay, pair, perms[1])  11.4 us
    ppermute x3, starting transfers between devices, reduce_scatter_head(): lax.ppermute(piece, 'y', [(i, (i + shift) % ny) for i in range(ny)])  11.4 us
    ppermute x4, starting transfers between devices, swap_cat(): return jnp.concatenate([x, lax.ppermute(x, axis_name, [(0, 1), (1, 0)])], 0)  11 us
  transfers between devices with their start and end apart: 16, of which 9 were waited for; matrix products, arithmetic and copies ran while one was open for 6% of the time, Pallas kernels for 0%

profile of v12, /device:TPU:6, one launch (start us, length us, event | category | flops | bytes accessed | tf_op | source)
XLA Modules:
  0.0 340.7 jit_solution(16723467296093903645)
XLA Ops:
  14.0 3.3 collective-permute-start.1
  17.3 3.9 %collective-permute-start.2 = (bf16[128,1024]{0,1:T(8,128)(2,1)S(1)}, bf16[128,1024]{0,1:T(8,128)(2,1)S(1)}, u32[]{:S(2)}, u32[]{:S(2)}) collective-permute-start(bf16[128,1024]{0,1:T(8,128)(2,1)S(1)} %get-tuple-element.59), channel_id=1, source_target_pairs={{0,24},{8,16},{16,8},{24,0},{1,25},{9,17},{17,9},{25,1},{2,26},{10... | collective-permute-start | bytes 786440 | tf_op jit(solution)/shard_map/ppermute | solution.py:138
  21.5 5.0 %collective-permute-done.1 = bf16[128,1024]{0,1:T(8,128)(2,1)S(1)} collective-permute-done((bf16[128,1024]{0,1:T(8,128)(2,1)S(1)}, bf16[128,1024]{0,1:T(8,128)(2,1)S(1)}, u32[]{:S(2)}, u32[]{:S(2)}) %collective-permute-start.1) | collective-permute-done | bytes 262176 | tf_op jit(solution)/shard_map/ppermute | solution.py:138
  26.5 4.8 %collective-permute-done.2 = bf16[128,1024]{0,1:T(8,128)(2,1)S(1)} collective-permute-done((bf16[128,1024]{0,1:T(8,128)(2,1)S(1)}, bf16[128,1024]{0,1:T(8,128)(2,1)S(1)}, u32[]{:S(2)}, u32[]{:S(2)}) %collective-permute-start.2) | collective-permute-done | bytes 262176 | tf_op jit(solution)/shard_map/ppermute | solution.py:138
  31.3 58.2 %all-gather.3.cloned.1.call-done = bf16[1024,1280]{1,0:T(8,128)(2,1)} async-done(((bf16[64,1280]{1,0:T(8,128)(2,1)}), bf16[1024,1280]{1,0:T(8,128)(2,1)}) %all-gather.3.cloned.1.call-update) | async-done | bytes 2621456 | tf_op jit(solution)/shard_map/all_gather | solution.py:59
  98.8 3.4 collective-permute-start.5
  102.4 11.4 %collective-permute-done.5 = f32[128,768]{0,1:T(8,128)S(1)} collective-permute-done((f32[128,768]{0,1:T(8,128)}, f32[128,768]{0,1:T(8,128)S(1)}, u32[]{:S(2)}, u32[]{:S(2)}) %collective-permute-start.5) | collective-permute-done | bytes 393248 | tf_op jit(solution)/shard_map/ppermute | solution.py:145
  117.5 3.4 collective-permute-start.8
  120.9 63.3 %all-gather.5.cloned.1.call-done = bf16[2176,256]{1,0:T(8,128)(2,1)} async-done(((bf16[136,256]{1,0:T(8,128)(2,1)}), bf16[2176,256]{1,0:T(8,128)(2,1)}) %all-gather.5.cloned.1.call-update) | async-done | bytes 1114128 | tf_op jit(solution)/shard_map/all_gather | solution.py:59
  184.2 3.5 %collective-permute-start.6 = (bf16[2176,256]{1,0:T(8,128)(2,1)}, bf16[2176,256]{1,0:T(8,128)(2,1)S(1)}, u32[]{:S(2)}, u32[]{:S(2)}) collective-permute-start(bf16[2176,256]{1,0:T(8,128)(2,1)} %all-gather.5.cloned.1.call-done), channel_id=1, source_target_pairs={{0,16},{16,0},{1,17},{17,1},{2,18},{18,2},{3,19},{19,3},{4,20},{20... | collective-permute-start | bytes 3342344 | tf_op jit(solution)/shard_map/ppermute | solution.py:55
  187.7 2.7 pad_maximum_fusion.3
  192.5 12.7 %collective-permute-done.6 = bf16[2176,256]{1,0:T(8,128)(2,1)S(1)} collective-permute-done((bf16[2176,256]{1,0:T(8,128)(2,1)}, bf16[2176,256]{1,0:T(8,128)(2,1)S(1)}, u32[]{:S(2)}, u32[]{:S(2)}) %collective-permute-start.6) | collective-permute-done | bytes 1114144 | tf_op jit(solution)/shard_map/ppermute | solution.py:55
  214.9 3.6 %pad_maximum_fusion.1 = bf16[4096,512]{1,0:T(8,128)(2,1)} fusion(bf16[2048,512]{1,0:T(8,128)(2,1)} %collective-permute-done.9, bf16[1024,512]{1,0:T(8,128)(2,1)} %collective-permute-done.8, bf16[1024,512]{1,0:T(8,128)(2,1)S(1)} %slice.149), kind=kLoop, calls=%fused_computation.14 | loop fusion | flops 12582912 | bytes 8388608 | tf_op jit(solution)/shard_map/concatenate | solution.py:55
  218.5 11.3 %pad_maximum_fusion = bf16[8704,256]{1,0:T(8,128)(2,1)S(1)} fusion(bf16[4352,256]{1,0:T(8,128)(2,1)} %collective-permute-done.7, bf16[2176,256]{1,0:T(8,128)(2,1)S(1)} %copy-done.2, bf16[2176,256]{1,0:T(8,128)(2,1)S(1)} %copy-done), kind=kLoop, calls=%fused_computation.13 | loop fusion | flops 13369344 | bytes 8912896 | tf_op jit(solution)/shard_map/concatenate | solution.py:55
  235.8 2.9 gather_fusion.2
  239.1 4.5 %fusion.63 = (f32[2,4,64]{2,1,0:T(4,128)S(1)}, bf16[2,4,64,2112]{3,2,1,0:T(8,128)(2,1)}) fusion(pred[2,64,2112]{2,1,0:T(8,128)(4,1)S(1)} %compare_and_fusion, bf16[2,2112,256]{2,1,0:T(8,128)(2,1)S(1)} %bitcast.117, bf16[2,64,4,64]{3,1,2,0:T(8,128)(2,1)} %copy.98, bf16[2,64,4,64]{3,1,2,0:T(8,128)(2,1)} %copy.97), kind=kOutput, calls=%fused_computation.144 | convolution fusion | flops 283576384 | bytes 3934208 | tf_op jit(solution)/shard_map/sub | solution.py:191
  246.2 3.4 %fusion.40 = f32[128,2,2,16,64]{0,4,3,2,1:T(8,128)S(1)} fusion(bf16[2,2,16,64,512]{4,3,2,1,0:T(8,128)(2,1)} %bitcast.111, bf16[128,512,1,1,1]{1,0,2,3,4:T(8,128)(2,1)S(1)} %reshape.594), kind=kOutput, calls=%fused_computation.70 | convolution fusion | flops 536870912 | bytes 6422528 | tf_op jit(solution)/shard_map/tk,jdk->tjd/dot_general | solution.py:202
  251.7 3.3 select_bitcast_fusion.1
  261.1 14.2 %collective-permute-done.10 = bf16[128,4,512]{0,2,1:T(8,128)(2,1)} collective-permute-done((bf16[128,4,512]{0,2,1:T(8,128)(2,1)}, bf16[128,4,512]{0,2,1:T(8,128)(2,1)}, u32[]{:S(2)}, u32[]{:S(2)}) %collective-permute-start.10) | collective-permute-done | bytes 524320 | tf_op jit(solution)/shard_map/ppermute | solution.py:97
  277.5 3.4 collective-permute-start.11
  280.9 4.6 %collective-permute-start.12 = (bf16[128,512]{0,1:T(8,128)(2,1)S(1)}, bf16[128,512]{0,1:T(8,128)(2,1)S(1)}, u32[]{:S(2)}, u32[]{:S(2)}) collective-permute-start(bf16[128,512]{0,1:T(8,128)(2,1)S(1)} %get-tuple-element.57), channel_id=1, source_target_pairs={{0,4},{2,6},{4,0},{6,2},{1,5},{3,7},{5,1},{7,3},{8,12},{10,14},{12... | collective-permute-start | bytes 393224 | tf_op jit(solution)/shard_map/ppermute | solution.py:101
  285.6 3.3 collective-permute-start.13
  296.1 6.4 %psum.22 = f32[2,512]{1,0:T(2,128)S(1)} all-reduce(f32[2,512]{1,0:T(2,128)S(1)} %psum.21), channel_id=1, replica_groups=mesh['z'=16,'xh'=2,'c'=2,'y'=4,'xl'=2] {'xh'}, use_global_device_ids=true, to_apply=%region_12.16 | all-reduce | flops 1024 | bytes 8192 | tf_op jit(solution)/shard_map/psum | solution.py:224
  302.5 29.3 %psum.23 = f32[2,512]{1,0:T(2,128)S(1)} all-reduce(f32[2,512]{1,0:T(2,128)S(1)} %psum.22), channel_id=1, replica_groups=mesh['z'=16,'xh'=2,'c'=2,'y'=4,'xl'=2] {'z'}, use_global_device_ids=true, to_apply=%region_13.17 | all-reduce | flops 1024 | bytes 8192 | tf_op jit(solution)/shard_map/psum | solution.py:224
  (129 shorter events, 59.4 us)
Async XLA Ops:
  7.2 82.3 %all-gather.3.cloned.1.call-start = ((), (), s32[]{:S(2)}) async-start(), calls=%async_computation | async-start | bytes 2785280 | tf_op jit(solution)/shard_map/all_gather | solution.py:59
  8.8 175.4 %all-gather.5.cloned.1.call-start = ((), (), s32[]{:S(2)}) async-start(), calls=%async_computation.1 | async-start | bytes 1183744 | tf_op jit(solution)/shard_map/all_gather | solution.py:59
  11.8 9.3 %copy-start.8 = (s32[32]{0:T(128)S(1)}, s32[32]{0:T(128)}, u32[]{:S(2)}) copy-start(s32[32]{0:T(128)} %param.22) | copy-start | bytes 388
  12.1 9.4 %collective-permute-start = (bf16[128,1024]{0,1:T(8,128)(2,1)S(1)}, bf16[128,1024]{0,1:T(8,128)(2,1)S(1)}, u32[]{:S(2)}, u32[]{:S(2)}) collective-permute-start(bf16[128,1024]{0,1:T(8,128)(2,1)S(1)} %get-tuple-element.61), channel_id=1, source_target_pairs={{0,8},{8,0},{16,24},{24,16},{1,9},{9,1},{17,25},{25,17},{2,10},{10... | collective-permute-start | bytes 786440 | tf_op jit(solution)/shard_map/ppermute | solution.py:138
  14.0 12.5 %collective-permute-start.1 = (bf16[128,1024]{0,1:T(8,128)(2,1)S(1)}, bf16[128,1024]{0,1:T(8,128)(2,1)S(1)}, u32[]{:S(2)}, u32[]{:S(2)}) collective-permute-start(bf16[128,1024]{0,1:T(8,128)(2,1)S(1)} %get-tuple-element.60), channel_id=1, source_target_pairs={{0,16},{8,24},{16,0},{24,8},{1,17},{9,25},{17,1},{25,9},{2,18},{10... | collective-permute-start | bytes 786440 | tf_op jit(solution)/shard_map/ppermute | solution.py:138
  17.3 14.0 %collective-permute-start.2 = (bf16[128,1024]{0,1:T(8,128)(2,1)S(1)}, bf16[128,1024]{0,1:T(8,128)(2,1)S(1)}, u32[]{:S(2)}, u32[]{:S(2)}) collective-permute-start(bf16[128,1024]{0,1:T(8,128)(2,1)S(1)} %get-tuple-element.59), channel_id=1, source_target_pairs={{0,24},{8,16},{16,8},{24,0},{1,25},{9,17},{17,9},{25,1},{2,26},{10... | collective-permute-start | bytes 786440 | tf_op jit(solution)/shard_map/ppermute | solution.py:138
  26.5 63.0 %copy-start.13 = (bf16[128,1024]{0,1:T(8,128)(2,1)}, bf16[128,1024]{0,1:T(8,128)(2,1)S(1)}, u32[]{:S(2)}) copy-start(bf16[128,1024]{0,1:T(8,128)(2,1)S(1)} %collective-permute-done.1) | copy-start | bytes 786436
  31.3 58.2 %copy-start.14 = (bf16[128,1024]{0,1:T(8,128)(2,1)}, bf16[128,1024]{0,1:T(8,128)(2,1)S(1)}, u32[]{:S(2)}) copy-start(bf16[128,1024]{0,1:T(8,128)(2,1)S(1)} %collective-permute-done.2) | copy-start | bytes 786436
  92.2 3.6 %collective-permute-start.4 = (f32[128,768]{0,1:T(8,128)S(1)}, f32[128,768]{0,1:T(8,128)S(1)}, u32[]{:S(2)}, u32[]{:S(2)}) collective-permute-start(f32[128,768]{0,1:T(8,128)S(1)} %slice.135), channel_id=1, source_target_pairs={{0,8},{8,0},{16,24},{24,16},{1,9},{9,1},{17,25},{25,17},{2,10},{10... | collective-permute-start | bytes 1179656 | tf_op jit(solution)/shard_map/ppermute | solution.py:144
  96.8 5.6 %collective-permute-start.3 = (f32[128,768]{0,1:T(8,128)}, f32[128,768]{0,1:T(8,128)S(1)}, u32[]{:S(2)}, u32[]{:S(2)}) collective-permute-start(f32[128,768]{0,1:T(8,128)} %get-tuple-element.53), channel_id=1, source_target_pairs={{0,8},{8,0},{16,24},{24,16},{1,9},{9,1},{17,25},{25,17},{2,10},{10... | collective-permute-start | bytes 1179656 | tf_op jit(solution)/shard_map/ppermute | solution.py:146
  98.8 15.0 %collective-permute-start.5 = (f32[128,768]{0,1:T(8,128)}, f32[128,768]{0,1:T(8,128)S(1)}, u32[]{:S(2)}, u32[]{:S(2)}) collective-permute-start(f32[128,768]{0,1:T(8,128)} %get-tuple-element.54), channel_id=1, source_target_pairs={{0,16},{8,24},{16,0},{24,8},{1,17},{9,25},{17,1},{25,9},{2,18},{10... | collective-permute-start | bytes 1179656 | tf_op jit(solution)/shard_map/ppermute | solution.py:145
  117.5 70.2 %collective-permute-start.8 = (bf16[1024,512]{1,0:T(8,128)(2,1)S(1)}, bf16[1024,512]{1,0:T(8,128)(2,1)}, u32[]{:S(2)}, u32[]{:S(2)}) collective-permute-start(bf16[1024,512]{1,0:T(8,128)(2,1)S(1)} %slice.149), channel_id=1, source_target_pairs={{0,16},{16,0},{1,17},{17,1},{2,18},{18,2},{3,19},{19,3},{4,20},{20... | collective-permute-start | bytes 3145736 | tf_op jit(solution)/shard_map/ppermute | solution.py:55
  184.2 20.9 %copy-start = (bf16[2176,256]{1,0:T(8,128)(2,1)S(1)}, bf16[2176,256]{1,0:T(8,128)(2,1)}, u32[]{:S(2)}) copy-start(bf16[2176,256]{1,0:T(8,128)(2,1)} %all-gather.5.cloned.1.call-done) | copy-start | bytes 3342340
  184.2 20.9 %collective-permute-start.6 = (bf16[2176,256]{1,0:T(8,128)(2,1)}, bf16[2176,256]{1,0:T(8,128)(2,1)S(1)}, u32[]{:S(2)}, u32[]{:S(2)}) collective-permute-start(bf16[2176,256]{1,0:T(8,128)(2,1)} %all-gather.5.cloned.1.call-done), channel_id=1, source_target_pairs={{0,16},{16,0},{1,17},{17,1},{2,18},{18,2},{3,19},{19,3},{4,20},{20... | collective-permute-start | bytes 3342344 | tf_op jit(solution)/shard_map/ppermute | solution.py:55
  190.4 20.4 %slice-start = ((f32[128,768]{0,1:T(8,128)}), f32[128,512]{0,1:T(8,128)S(1)}, s32[]{:S(2)}) async-start(f32[128,768]{0,1:T(8,128)} %copy-done.4), calls=%async_computation.2 | async-start | bytes 524288 | tf_op jit(solution)/shard_map/slice | solution.py:148
  190.4 24.5 %collective-permute-start.9 = (bf16[2048,512]{1,0:T(8,128)(2,1)}, bf16[2048,512]{1,0:T(8,128)(2,1)}, u32[]{:S(2)}, u32[]{:S(2)}) collective-permute-start(bf16[2048,512]{1,0:T(8,128)(2,1)} %pad_maximum_fusion.3), channel_id=1, source_target_pairs={{0,8},{8,0},{1,9},{9,1},{2,10},{10,2},{3,11},{11,3},{4,12},{12,4},... | collective-permute-start | bytes 6291464 | tf_op jit(solution)/shard_map/ppermute | solution.py:55
  206.9 11.6 %collective-permute-start.7 = (bf16[4352,256]{1,0:T(8,128)(2,1)}, bf16[4352,256]{1,0:T(8,128)(2,1)}, u32[]{:S(2)}, u32[]{:S(2)}) collective-permute-start(bf16[4352,256]{1,0:T(8,128)(2,1)} %pad_maximum_fusion.2), channel_id=1, source_target_pairs={{0,8},{8,0},{1,9},{9,1},{2,10},{10,2},{3,11},{11,3},{4,12},{12,4},... | collective-permute-start | bytes 6684680 | tf_op jit(solution)/shard_map/ppermute | solution.py:55
  257.9 31.1 %copy-start.15 = (s32[32]{0:T(128)S(1)}, s32[32]{0:T(128)}, u32[]{:S(2)}) copy-start(s32[32]{0:T(128)} %param.23) | copy-start | bytes 388
  257.9 32.4 %copy-start.10 = (s32[128]{0:T(128)S(1)}, s32[128]{0:T(128)}, u32[]{:S(2)}) copy-start(s32[128]{0:T(128)} %param.21) | copy-start | bytes 1540
  257.9 32.4 %copy-start.11 = (s32[32]{0:T(128)S(1)}, s32[32]{0:T(128)}, u32[]{:S(2)}) copy-start(s32[32]{0:T(128)} %get-tuple-element.76) | copy-start | bytes 388
  258.8 16.5 %collective-permute-start.10 = (bf16[128,4,512]{0,2,1:T(8,128)(2,1)}, bf16[128,4,512]{0,2,1:T(8,128)(2,1)}, u32[]{:S(2)}, u32[]{:S(2)}) collective-permute-start(bf16[128,4,512]{0,2,1:T(8,128)(2,1)} %bitcast_convert_fusion), channel_id=1, source_target_pairs={{0,1},{1,0},{2,3},{3,2},{4,5},{5,4},{6,7},{7,6},{8,9},{9,8},{10,11... | collective-permute-start | bytes 1572872 | tf_op jit(solution)/shard_map/ppermute | solution.py:97
  277.5 12.9 %collective-permute-start.11 = (bf16[128,512]{0,1:T(8,128)(2,1)S(1)}, bf16[128,512]{0,1:T(8,128)(2,1)S(1)}, u32[]{:S(2)}, u32[]{:S(2)}) collective-permute-start(bf16[128,512]{0,1:T(8,128)(2,1)S(1)} %get-tuple-element.55), channel_id=1, source_target_pairs={{0,2},{2,4},{4,6},{6,0},{1,3},{3,5},{5,7},{7,1},{8,10},{10,12},{12... | collective-permute-start | bytes 393224 | tf_op jit(solution)/shard_map/ppermute | solution.py:101
  280.9 9.5 %collective-permute-start.12 = (bf16[128,512]{0,1:T(8,128)(2,1)S(1)}, bf16[128,512]{0,1:T(8,128)(2,1)S(1)}, u32[]{:S(2)}, u32[]{:S(2)}) collective-permute-start(bf16[128,512]{0,1:T(8,128)(2,1)S(1)} %get-tuple-element.57), channel_id=1, source_target_pairs={{0,4},{2,6},{4,0},{6,2},{1,5},{3,7},{5,1},{7,3},{8,12},{10,14},{12... | collective-permute-start | bytes 393224 | tf_op jit(solution)/shard_map/ppermute | solution.py:101
  285.6 6.9 %collective-permute-start.13 = (bf16[128,512]{0,1:T(8,128)(2,1)S(1)}, bf16[128,512]{0,1:T(8,128)(2,1)S(1)}, u32[]{:S(2)}, u32[]{:S(2)}) collective-permute-start(bf16[128,512]{0,1:T(8,128)(2,1)S(1)} %get-tuple-element.56), channel_id=1, source_target_pairs={{0,6},{2,0},{4,2},{6,4},{1,7},{3,1},{5,3},{7,5},{8,14},{10,8},{12,... | collective-permute-start | bytes 393224 | tf_op jit(solution)/shard_map/ppermute | solution.py:101
  (9 other events, 23.0 us)
Sparse Core Ops, SparseCore 0:
  10.1 79.3 all-gather.2
  116.4 67.7 all-gather.4
